TPU v7x, 1024 devices: a whole 4x8x16 slice. The times are simulated.
1024 devices in a mesh: dp: 16 (over z), fsdp: 32 (over y, x), llm: 2 (over core).
Axes of the slice: x: 4, y: 8, z: 16, core: 2. Of those that a mesh axis runs over, the one named last changes fastest.
Arguments:
- tile_rows: bfloat16 [131072, 768], P(('dp', 'fsdp')), may hold values from -6 to 6
- grad_seq: bfloat16 [262144, 768], P(('dp', 'fsdp')), may hold values from -6 to 6
- visual_pos: int32 [512, 256], P(('dp', 'fsdp')), may hold values from 0 to 511, as said below
- assign: int32 [512, 16], P(('dp', 'fsdp')), may hold values from 0 to 15, each once within a row
- tile_count: int32 [512], P(('dp', 'fsdp')), may hold values from 1 to 4
- kernel: float32 [7, 7, 768], replicated, may hold values from -0.875 to 0.875
- norm_gain: float32 [768], replicated, may hold values from 0.5 to 2
- layer_scale: float32 [768], replicated, may hold values from 0.2 to 2
- weight_in: bfloat16 [768, 1536], P('fsdp', 'llm'), may hold values from -0.21875 to 0.21875
- weight_out: bfloat16 [768, 1536], P('fsdp', 'llm'), may hold values from -0.15625 to 0.15625
Outputs:
- grad_tiles: bfloat16 [131072, 768], P(('dp', 'fsdp'), 'llm')
- grad_weight_in: float32 [12288, 1536], P(('dp', 'fsdp'), 'llm')
- grad_weight_out: float32 [12288, 1536], P(('dp', 'fsdp'), 'llm')
Inputs may be any that keep to these rules, and one draw needn't show every extreme that they name: `visual_pos`: each row is strictly increasing. `assign`: each row names every group once.
All inputs are finite; a program needn't handle non-finite values.
Results may differ from a plain program's by a relative error of at most 0.015.
Values may be sent and summed in bfloat16 or wider, within the bound.
No kernel may reach another device: no remote copies, remote signals or barrier semaphores. Data moves between devices by JAX's collectives and lax.ppermute only.
A program may use at most 32 MiB of HBM per device.

v0:
```python
import jax
import jax.numpy as jnp
from jax import lax
from jax.sharding import PartitionSpec as P

SIDE = 8
ACCUM = 64


def depthwise(images, kernel):
    return lax.conv_general_dilated(
        images,
        kernel[:, :, None, :],
        (1, 1),
        "SAME",
        dimension_numbers=("NHWC", "HWIO", "NHWC"),
        feature_group_count=images.shape[3],
        precision=lax.Precision.HIGHEST,
    )


def gelu_parts(hidden_in):
    cumulative = 0.5 * (1.0 + lax.erf(hidden_in * 0.7071067811865476))
    density = jnp.exp(-0.5 * hidden_in * hidden_in) * 0.3989422804014327
    return (hidden_in * cumulative, cumulative + hidden_in * density)


def body(
    tile_rows,
    grad_seq,
    visual_pos,
    assign,
    tile_count,
    kernel,
    norm_gain,
    layer_scale,
    weight_in,
    weight_out,
):
    groups = lax.axis_size("dp")
    shards = lax.axis_size("fsdp")
    row_count = tile_rows.shape[0]
    channels = tile_rows.shape[1]
    block_rows = row_count // groups
    visual = jnp.take(grad_seq, visual_pos[0], axis=0)
    outgoing = jnp.take(visual.reshape(groups, block_rows, channels), assign[0], axis=0).reshape(
        row_count, channels
    )
    arrived = lax.all_to_all(outgoing, "dp", split_axis=0, concat_axis=0, tiled=True)
    present = jnp.arange(row_count) // (SIDE * SIDE) < tile_count[0]
    grad_out = jnp.where(present[:, None], arrived, jnp.zeros_like(arrived))
    w_in_full = lax.all_gather(weight_in, "fsdp", axis=0, tiled=True)
    mixed = depthwise(
        tile_rows.astype(jnp.float32).reshape(-1, SIDE, SIDE, channels), kernel
    ).reshape(row_count, channels)
    row_mean = jnp.mean(mixed, axis=1, keepdims=True)
    centred = mixed - row_mean
    inv_std = lax.rsqrt(jnp.mean(centred * centred, axis=1, keepdims=True) + 1e-06)
    unit = centred * inv_std
    normed = (unit * norm_gain).astype(jnp.bfloat16)
    hidden_in = jnp.dot(normed, w_in_full, preferred_element_type=jnp.float32)
    activated, slope = gelu_parts(hidden_in)
    hidden = activated.astype(jnp.bfloat16)
    w_out_full, w_in_full = (
        lax.all_gather(weight_out, "fsdp", axis=0, tiled=True),
        lax.all_gather(weight_in, "fsdp", axis=0, tiled=True),
    )
    scaled = (grad_out.astype(jnp.float32) * layer_scale).astype(jnp.bfloat16)
    grad_hidden = jnp.dot(scaled, w_out_full, preferred_element_type=jnp.float32)
    grad_pre = (grad_hidden * slope).astype(jnp.bfloat16)
    normed_part = lax.slice_in_dim(normed, 0, channels // shards * lax.axis_size("fsdp"), axis=1)
    term_in = lax.dot_general(
        normed_part, grad_pre, (((0,), (0,)), ((), ())), preferred_element_type=jnp.float32
    )
    term_out = lax.dot_general(
        scaled, hidden, (((0,), (0,)), ((), ())), preferred_element_type=jnp.float32
    )
    totals = lax.psum_scatter(
        jnp.concatenate([term_in, term_out], axis=1).astype(jnp.bfloat16),
        "fsdp",
        scatter_dimension=0,
        tiled=True,
    ).astype(jnp.float32)
    hidden_half = hidden.shape[1]
    grad_in = totals[:, :hidden_half] / ACCUM
    grad_outw = totals[:, hidden_half:] / ACCUM
    grad_part = lax.dot_general(
        grad_pre, w_in_full, (((1,), (1,)), ((), ())), preferred_element_type=jnp.float32
    )
    core_index = lax.axis_index("llm")
    half_width = channels // lax.axis_size("llm")
    dy_half = lax.dynamic_slice_in_dim(grad_out, core_index * half_width, half_width, 1).astype(
        jnp.float32
    )
    grad_normed = lax.psum(grad_part.astype(jnp.bfloat16), "llm").astype(jnp.float32)
    grad_unit = grad_normed * norm_gain
    mean_grad = jnp.mean(grad_unit, axis=1, keepdims=True)
    mean_cross = jnp.mean(grad_unit * unit, axis=1, keepdims=True)
    grad_mixed = inv_std * (grad_unit - mean_grad - unit * mean_cross)
    backward = depthwise(grad_mixed.reshape(-1, SIDE, SIDE, channels), kernel[::-1, ::-1]).reshape(
        row_count, channels
    )
    backward_half = lax.dynamic_slice_in_dim(backward, core_index * half_width, half_width, 1)
    grad_tiles = (dy_half + backward_half).astype(jnp.bfloat16)
    return (grad_tiles, grad_in, grad_outw)


def solution(mesh):
    in_specs = (
        P(("dp", "fsdp"), None),
        P(("dp", "fsdp"), None),
        P(("dp", "fsdp"), None),
        P(("dp", "fsdp"), None),
        P(("dp", "fsdp")),
        P(),
        P(),
        P(),
        P("fsdp", "llm"),
        P("fsdp", "llm"),
    )
    out_specs = (P(("dp", "fsdp"), "llm"), P(("dp", "fsdp"), "llm"), P(("dp", "fsdp"), "llm"))
    return jax.shard_map(body, mesh=mesh, in_specs=in_specs, out_specs=out_specs, check_vma=False)
```

profile of v0, /device:TPU:64, one launch (start us, length us, event | category | flops | bytes accessed | tf_op | source)
XLA Modules:
  0.0 505.7 jit_solution(5386720362195007479)
XLA Ops:
  7.2 0.7 all-gather.5.cloned.1.call-update
  7.9 0.5 broadcast.177
  8.4 1.3 reduce.5
  9.8 0.7 compare_select_fusion.1
  10.6 1.2 gather_fusion
  11.9 0.6 gather_fusion.1
  12.5 0.9 broadcast_select_fusion
  13.4 18.4 %all-to-all-start = ((bf16[16,16,768]{2,1,0:T(8,128)(2,1)}), bf16[16,16,768]{2,1,0:T(8,128)(2,1)S(1)}, u32[]{:S(2)}, u32[]{:S(2)}) async-start(bf16[16,16,768]{2,1,0:T(8,128)(2,1)} %broadcast_select_fusion), calls=%async_computation | async-start | bytes 786432 | tf_op jit(solution)/shard_map/all_to_all | solution.py:49
  31.9 0.7 all-gather.3.cloned.1.call-update
  32.6 4.8 fusion.15
  37.9 0.3 multiply_reduce_fusion.1
  39.4 14.3 %all-to-all-done = bf16[16,16,768]{2,1,0:T(8,128)(2,1)S(1)} async-done(((bf16[16,16,768]{2,1,0:T(8,128)(2,1)}), bf16[16,16,768]{2,1,0:T(8,128)(2,1)S(1)}, u32[]{:S(2)}, u32[]{:S(2)}) %all-to-all-start) | async-done | bytes 393248 | tf_op jit(solution)/shard_map/all_to_all | solution.py:49
  53.8 58.3 %all-gather.5.cloned.1.call-done = bf16[768,768]{1,0:T(8,128)(2,1)} async-done(((bf16[24,768]{1,0:T(8,128)(2,1)}), bf16[768,768]{1,0:T(8,128)(2,1)}) %all-gather.5.cloned.1.call-update) | async-done | bytes 1179664 | tf_op jit(solution)/shard_map/all_gather | solution.py:52
  112.2 1.7 fusion.16
  113.9 0.9 copy-done.3
  114.8 1.6 convolution_convert_fusion
  116.4 90.9 %all-gather.3.cloned.1.call-done = bf16[768,768]{1,0:T(8,128)(2,1)} async-done(((bf16[24,768]{1,0:T(8,128)(2,1)}), bf16[768,768]{1,0:T(8,128)(2,1)}) %all-gather.3.cloned.1.call-update) | async-done | bytes 1179664 | tf_op jit(solution)/shard_map/all_gather | solution.py:65
  207.3 2.0 fusion
  209.4 0.7 copy-done.5
  210.1 1.3 convolution_convert_fusion.2
  211.5 1.6 convolution_convert_fusion.1
  213.1 1.6 pad_maximum_fusion
  214.7 4.3 copy.49
  219.0 0.9 copy-done.7
  220.0 35.4 %all-reduce.2.cloned.1.call-done = bf16[256,768]{1,0:T(8,128)(2,1)} async-done(((bf16[256,768]{1,0:T(8,128)(2,1)}), bf16[256,768]{1,0:T(8,128)(2,1)}) %all-reduce.2.cloned.1.call-update) | async-done | bytes 393232 | tf_op jit(solution)/shard_map/psum | solution.py:95
  255.4 1.3 fusion.8
  257.0 3.3 fusion.6
  260.5 0.7 add_convert_fusion
  261.2 235.2 %reduce-scatter.4.cloned.1.call-done = bf16[24,1536]{1,0:T(8,128)(2,1)} async-done(((bf16[768,1536]{1,0:T(8,128)(2,1)}), bf16[24,1536]{1,0:T(8,128)(2,1)}) %reduce-scatter.4.cloned.1.call-update) | async-done | bytes 73744
  496.4 1.1 copy.50
  497.6 0.8 copy.47
  498.4 0.8 copy.48
  (51 shorter events, 2.2 us)
Async XLA Ops:
  7.2 3.4 copy-start
  7.2 105.0 %all-gather.5.cloned.1.call-start = ((), (), s32[]{:S(2)}) async-start(), calls=%async_computation.3 | async-start | bytes 1216512 | tf_op jit(solution)/shard_map/all_gather | solution.py:52
  10.5 1.2 copy-start.11
  11.9 20.7 %copy-start.6 = (f32[7,7,768]{2,1,0:T(8,128)S(1)}, f32[7,7,768]{2,1,0:T(8,128)}, u32[]{:S(2)}) copy-start(f32[7,7,768]{2,1,0:T(8,128)} %param.15) | copy-start | bytes 451588
  11.9 20.7 %copy-start.10 = (bf16[256,768]{1,0:T(8,128)(2,1)S(1)}, bf16[256,768]{1,0:T(8,128)(2,1)}, u32[]{:S(2)}) copy-start(bf16[256,768]{1,0:T(8,128)(2,1)} %param.10) | copy-start | bytes 1179652
  13.4 40.3 %all-to-all-start = ((bf16[16,16,768]{2,1,0:T(8,128)(2,1)}), bf16[16,16,768]{2,1,0:T(8,128)(2,1)S(1)}, u32[]{:S(2)}, u32[]{:S(2)}) async-start(bf16[16,16,768]{2,1,0:T(8,128)(2,1)} %broadcast_select_fusion), calls=%async_computation | async-start | bytes 786432 | tf_op jit(solution)/shard_map/all_to_all | solution.py:49
  31.8 175.5 %all-gather.3.cloned.1.call-start = ((), (), s32[]{:S(2)}) async-start(), calls=%async_computation.2 | async-start | bytes 1216512 | tf_op jit(solution)/shard_map/all_gather | solution.py:65
  32.6 222.8 %all-reduce.2.cloned.1.call-start = ((), (), s32[]{:S(2)}) async-start(), calls=%async_computation.4 | async-start | bytes 786432 | tf_op jit(solution)/shard_map/psum | solution.py:95
  37.8 1.4 copy-start.8
  53.8 61.0 %copy-start.9 = (f32[768]{0:T(1024)S(1)}, f32[768]{0:T(1024)}, u32[]{:S(2)}) copy-start(f32[768]{0:T(1024)} %param.17) | copy-start | bytes 9220
  113.9 0.9 copy-start.3
  116.4 93.7 %copy-start.1 = (bf16[768,768]{1,0:T(8,128)(2,1)S(1)}, bf16[768,768]{1,0:T(8,128)(2,1)}, u32[]{:S(2)}) copy-start(bf16[768,768]{1,0:T(8,128)(2,1)} %all-gather.5.cloned.1.call-done) | copy-start | bytes 3538948
  209.4 0.8 copy-start.5
  211.4 1.7 copy-start.2
  211.4 284.9 %reduce-scatter.4.cloned.1.call-start = ((), (), s32[]{:S(2)}) async-start(), calls=%async_computation.5 | async-start | bytes 2433024
  218.9 0.9 copy-start.7
  255.4 1.4 copy-start.4
Sparse Core Ops, SparseCore 0:
  12.4 99.7 all-gather.4
  116.5 90.7 all-gather.2
  211.6 43.7 all-reduce.1
  261.8 234.5 reduce-scatter.3
where the time goes:
time: 507 us; the launch traced here: 506 us
  waiting for transfers between devices  435 us (86%)
  starting transfers between devices  18.6 us (4%)
  matrix products  16.3 us (3%)
  between operations  14.7 us (3%)
  local copies, waits for them, and re-layouts  12.9 us (3%)
  other arithmetic  7.71 us (2%)
    unnamed x5, waiting for transfers between devices  237 us
    all_gather x1, waiting for transfers between devices, body(): lax.all_gather(weight_out, 'fsdp', axis=0, tiled=True)  90.9 us
    all_gather x1, waiting for transfers between devices, body(): w_in_full = lax.all_gather(weight_in, 'fsdp', axis=0, tiled=True)  58.3 us
    psum x1, waiting for transfers between devices, body(): lax.psum(grad_part.astype(jnp.bfloat16), 'llm').astype(jnp.float32)  35.4 us
    all_to_all x1, starting transfers between devices, body(): lax.all_to_all(outgoing, 'dp', split_axis=0, concat_axis=0, tiled=True)  18.4 us
    all_to_all x1, waiting for transfers between devices, body(): lax.all_to_all(outgoing, 'dp', split_axis=0, concat_axis=0, tiled=True)  14.3 us
  transfers between devices with their start and end apart: 5, of which 5 were waited for; matrix products, arithmetic and copies ran while one was open for 6% of the time, Pallas kernels for 0%

commit v1 on v0

v1 whole, which is shorter than its diff:
```python
import jax
import jax.numpy as jnp
from jax import lax
from jax.sharding import PartitionSpec as P

SIDE = 8
ACCUM = 64


def depthwise(images, kernel):
    return lax.conv_general_dilated(
        images,
        kernel[:, :, None, :],
        (1, 1),
        "SAME",
        dimension_numbers=("NHWC", "HWIO", "NHWC"),
        feature_group_count=images.shape[3],
        precision=lax.Precision.HIGHEST,
    )


def gelu_parts(hidden_in):
    cumulative = 0.5 * (1.0 + lax.erf(hidden_in * 0.7071067811865476))
    density = jnp.exp(-0.5 * hidden_in * hidden_in) * 0.3989422804014327
    return (hidden_in * cumulative, cumulative + hidden_in * density)


SWAP = [(0, 1), (1, 0)]


def body(
    tile_rows,
    grad_seq,
    visual_pos,
    assign,
    tile_count,
    kernel,
    norm_gain,
    layer_scale,
    weight_in,
    weight_out,
):
    groups = lax.axis_size("dp")
    shards = lax.axis_size("fsdp")
    row_count = tile_rows.shape[0]
    channels = tile_rows.shape[1]
    block_rows = row_count // groups
    half_width = channels // lax.axis_size("llm")
    core_index = lax.axis_index("llm")

    visual = jnp.take(grad_seq, visual_pos[0], axis=0)
    outgoing = jnp.take(visual.reshape(groups, block_rows, channels), assign[0], axis=0).reshape(
        row_count, channels
    )
    out_half = lax.dynamic_slice_in_dim(outgoing, core_index * half_width, half_width, 1)
    arrived_half = lax.all_to_all(out_half, "dp", split_axis=0, concat_axis=0, tiled=True)
    present = jnp.arange(row_count) // (SIDE * SIDE) < tile_count[0]
    mine_half = jnp.where(present[:, None], arrived_half, jnp.zeros_like(arrived_half))
    other_half = lax.ppermute(mine_half, "llm", SWAP)
    first = jnp.where(core_index == 0, mine_half, other_half)
    second = jnp.where(core_index == 0, other_half, mine_half)
    grad_out = jnp.concatenate([first, second], axis=1)

    hid = weight_in.shape[1]
    both = jnp.concatenate([weight_in, weight_out], axis=1)
    both_tiled = jnp.broadcast_to(both[None], (shards,) + both.shape)
    both_full = lax.all_to_all(both_tiled, "fsdp", split_axis=0, concat_axis=0).reshape(
        shards * both.shape[0], both.shape[1]
    )
    w_in_full = both_full[:, :hid]
    w_out_full = both_full[:, hid:]

    mixed = depthwise(
        tile_rows.astype(jnp.float32).reshape(-1, SIDE, SIDE, channels), kernel
    ).reshape(row_count, channels)
    row_mean = jnp.mean(mixed, axis=1, keepdims=True)
    centred = mixed - row_mean
    inv_std = lax.rsqrt(jnp.mean(centred * centred, axis=1, keepdims=True) + 1e-06)
    unit = centred * inv_std
    normed = (unit * norm_gain).astype(jnp.bfloat16)
    hidden_in = jnp.dot(normed, w_in_full, preferred_element_type=jnp.float32)
    activated, slope = gelu_parts(hidden_in)
    hidden = activated.astype(jnp.bfloat16)
    scaled = (grad_out.astype(jnp.float32) * layer_scale).astype(jnp.bfloat16)
    grad_hidden = jnp.dot(scaled, w_out_full, preferred_element_type=jnp.float32)
    grad_pre = (grad_hidden * slope).astype(jnp.bfloat16)

    term_in = lax.dot_general(
        normed, grad_pre, (((0,), (0,)), ((), ())), preferred_element_type=jnp.float32
    )
    term_out = lax.dot_general(
        scaled, hidden, (((0,), (0,)), ((), ())), preferred_element_type=jnp.float32
    )
    terms = jnp.concatenate([term_in, term_out], axis=1).astype(jnp.bfloat16)
    terms = terms.reshape(shards, channels // shards, 2 * hid)
    gathered = lax.all_to_all(terms, "fsdp", split_axis=0, concat_axis=0)
    totals = jnp.sum(gathered.astype(jnp.float32), axis=0)
    grad_in = totals[:, :hid] / ACCUM
    grad_outw = totals[:, hid:] / ACCUM

    grad_part = lax.dot_general(
        grad_pre, w_in_full, (((1,), (1,)), ((), ())), preferred_element_type=jnp.float32
    )
    part_lo = grad_part[:, :half_width]
    part_hi = grad_part[:, half_width:]
    keep = jnp.where(core_index == 0, part_lo, part_hi)
    send = jnp.where(core_index == 0, part_hi, part_lo).astype(jnp.bfloat16)
    received = lax.ppermute(send, "llm", SWAP)
    grad_normed = keep + received.astype(jnp.float32)
    gain_half = lax.dynamic_slice_in_dim(norm_gain, core_index * half_width, half_width, 0)
    unit_half = lax.dynamic_slice_in_dim(unit, core_index * half_width, half_width, 1)
    grad_unit = grad_normed * gain_half
    sums = jnp.stack(
        [jnp.sum(grad_unit, axis=1), jnp.sum(grad_unit * unit_half, axis=1)], axis=1
    )
    sums = sums + lax.ppermute(sums, "llm", SWAP)
    mean_grad = sums[:, 0:1] / channels
    mean_cross = sums[:, 1:2] / channels
    grad_mixed = inv_std * (grad_unit - mean_grad - unit_half * mean_cross)
    kernel_half = lax.dynamic_slice_in_dim(kernel, core_index * half_width, half_width, 2)
    backward_half = depthwise(
        grad_mixed.reshape(-1, SIDE, SIDE, half_width), kernel_half[::-1, ::-1]
    ).reshape(row_count, half_width)
    grad_tiles = (mine_half.astype(jnp.float32) + backward_half).astype(jnp.bfloat16)
    return (grad_tiles, grad_in, grad_outw)


def solution(mesh):
    in_specs = (
        P(("dp", "fsdp"), None),
        P(("dp", "fsdp"), None),
        P(("dp", "fsdp"), None),
        P(("dp", "fsdp"), None),
        P(("dp", "fsdp")),
        P(),
        P(),
        P(),
        P("fsdp", "llm"),
        P("fsdp", "llm"),
    )
    out_specs = (P(("dp", "fsdp"), "llm"), P(("dp", "fsdp"), "llm"), P(("dp", "fsdp"), "llm"))
    return jax.shard_map(body, mesh=mesh, in_specs=in_specs, out_specs=out_specs, check_vma=False)
```

time: 507 us -> 178 us (0.35)
  the two profiles are of different devices: /device:TPU:64 before, /device:TPU:80 now
where the time goes in v1:
time: 178 us; the launch traced here: 177 us
  waiting for transfers between devices  98.1 us (55%)
  starting transfers between devices  40.5 us (23%)
  other arithmetic  15.5 us (9%)
  matrix products  12 us (7%)
  local copies, waits for them, and re-layouts  9.57 us (5%)
    all_to_all x1, waiting for transfers between devices, body(): gathered = lax.all_to_all(terms, 'fsdp', split_axis=0, concat_axis=0)  43.4 us
    all_to_all x1, waiting for transfers between devices, body(): lax.all_to_all(both_tiled, 'fsdp', split_axis=0, concat_axis=0)  36.7 us
    all_to_all x1, starting transfers between devices, body(): lax.all_to_all(out_half, 'dp', split_axis=0, concat_axis=0, tiled=True)  18.4 us
    all_to_all x1, waiting for transfers between devices, body(): lax.all_to_all(out_half, 'dp', split_axis=0, concat_axis=0, tiled=True)  15.8 us
    all_to_all x1, starting transfers between devices, body(): lax.all_to_all(both_tiled, 'fsdp', split_axis=0, concat_axis=0)  10.2 us
    conv_general_dilated x2, matrix products, depthwise(): lax.conv_general_dilated(images, kernel[:, :, None, :], (1, 1), 'SAME', d...  7.21 us
    all_to_all x1, starting transfers between devices, body(): gathered = lax.all_to_all(terms, 'fsdp', split_axis=0, concat_axis=0)  5.9 us
  transfers between devices with their start and end apart: 6, of which 5 were waited for; matrix products, arithmetic and copies ran while one was open for 12% of the time, Pallas kernels for 0%

profile of v1, /device:TPU:80, one launch (start us, length us, event | category | flops | bytes accessed | tf_op | source)
XLA Modules:
  0.0 177.4 jit_solution(3968865010566593369)
XLA Ops:
  0.6 0.7 fusion.21
  1.4 0.7 compare_and_fusion.1
  2.0 0.7 compare_select_fusion.1
  3.2 1.3 reduce.5
  4.9 1.2 gather_fusion
  6.8 0.8 dynamic-slice_select_fusion
  7.6 18.4 %all-to-all-start = ((bf16[16,16,384]{2,1,0:T(8,128)(2,1)}), bf16[16,16,384]{2,1,0:T(8,128)(2,1)S(1)}, u32[]{:S(2)}, u32[]{:S(2)}) async-start(bf16[16,16,384]{2,1,0:T(8,128)(2,1)} %bitcast.8), calls=%async_computation | async-start | bytes 393216 | tf_op jit(solution)/shard_map/all_to_all | solution.py:56
  26.0 15.8 %all-to-all-done = bf16[16,16,384]{2,1,0:T(8,128)(2,1)S(1)} async-done(((bf16[16,16,384]{2,1,0:T(8,128)(2,1)}), bf16[16,16,384]{2,1,0:T(8,128)(2,1)S(1)}, u32[]{:S(2)}, u32[]{:S(2)}) %all-to-all-start) | async-done | bytes 196640 | tf_op jit(solution)/shard_map/all_to_all | solution.py:56
  41.8 1.6 broadcast_in_dim.62
  43.4 10.2 %all-to-all-start.1 = ((bf16[32,24,1536]{2,1,0:T(8,128)(2,1)}), bf16[32,24,1536]{2,1,0:T(8,128)(2,1)S(1)}, u32[]{:S(2)}, u32[]{:S(2)}) async-start(bf16[32,24,1536]{2,1,0:T(8,128)(2,1)} %broadcast_in_dim.62), calls=%async_computation.1 | async-start | bytes 4718592 | tf_op jit(solution)/shard_map/all_to_all | solution.py:67
  53.6 5.6 %fusion.27 = (f32[4,8,8]{0,2,1:T(8,128)S(1)}, f32[4,8,8,768]{3,0,2,1:T(4,128)}) fusion(f32[7,7,1,768]{3,1,0,2:T(8,128)S(1)} %bitcast.56, bf16[4,8,8,768]{3,2,1,0:T(8,128)(2,1)} %bitcast.64), kind=kOutput, calls=%fused_computation.71 | convolution fusion | flops 71565056 | bytes 1331200 | tf_op jit(solution)/shard_map/conv_general_dilated | solution.py:11
  59.5 2.2 %copy.41 = f32[4,8,8,768]{3,2,1,0:T(8,128)} copy(f32[4,8,8,768]{3,0,2,1:T(4,128)} %get-tuple-element.15) | data formatting | bytes 1572864 | tf_op jit(solution)/shard_map/conv_general_dilated | solution.py:11
  61.7 1.5 multiply_reduce_fusion
  64.2 1.9 %collective-permute-start = (bf16[256,384]{1,0:T(8,128)(2,1)S(1)}, bf16[256,384]{1,0:T(8,128)(2,1)}, u32[]{:S(2)}, u32[]{:S(2)}) collective-permute-start(bf16[256,384]{1,0:T(8,128)(2,1)S(1)} %bitcast_select_fusion), channel_id=1, source_target_pairs={{0,1},{1,0},{2,3},{3,2},{4,5},{5,4},{6,7},{7,6},{8,9},{9,8},{10,11... | collective-permute-start | bytes 589832 | tf_op jit(solution)/shard_map/ppermute | solution.py:59
  66.1 2.4 %fusion.18 = (bf16[768,256]{0,1:T(8,128)(2,1)}, f32[256,768]{1,0:T(8,128)}) fusion(f32[768]{0:T(1024)S(1)} %copy-done.10, f32[256]{0:T(256)S(1)} %rsqrt.12, f32[256]{0:T(256)S(1)} %div.32, f32[4,8,8,768]{3,2,1,0:T(8,128)} %copy.41), kind=kLoop, calls=%fused_computation.42 | loop fusion | flops 786432 | bytes 1971200 | tf_op jit(solution)/shard_map/dot_general | solution.py:88
  68.5 1.9 %copy.45 = bf16[768,256]{1,0:T(8,128)(2,1)} copy(bf16[768,256]{0,1:T(8,128)(2,1)} %get-tuple-element.5) | data formatting | bytes 786432 | tf_op jit(solution)/shard_map/dot_general | solution.py:88
  70.4 1.7 broadcast_select_fusion.2
  72.2 36.7 %all-to-all-done.1 = bf16[32,24,1536]{2,1,0:T(8,128)(2,1)S(1)} async-done(((bf16[32,24,1536]{2,1,0:T(8,128)(2,1)}), bf16[32,24,1536]{2,1,0:T(8,128)(2,1)S(1)}, u32[]{:S(2)}, u32[]{:S(2)}) %all-to-all-start.1) | async-done | bytes 2359328 | tf_op jit(solution)/shard_map/all_to_all | solution.py:67
  108.9 1.6 fusion.4
  111.2 0.6 convolution_convert_fusion
  112.8 1.6 pad_maximum_fusion
  114.4 5.9 %all-to-all-start.2 = ((bf16[32,24,1536]{2,1,0:T(8,128)(2,1)}), bf16[32,24,1536]{2,1,0:T(8,128)(2,1)}, u32[]{:S(2)}, u32[]{:S(2)}) async-start(bf16[32,24,1536]{2,1,0:T(8,128)(2,1)} %pad_maximum_fusion), calls=%async_computation.2 | async-start | bytes 4718592 | tf_op jit(solution)/shard_map/all_to_all | solution.py:96
  120.3 1.6 fusion.2
  122.0 2.1 %collective-permute-start.1 = (bf16[256,384]{1,0:T(8,128)(2,1)S(1)}, bf16[256,384]{1,0:T(8,128)(2,1)S(1)}, u32[]{:S(2)}, u32[]{:S(2)}) collective-permute-start(bf16[256,384]{1,0:T(8,128)(2,1)S(1)} %select_convert_fusion), channel_id=1, source_target_pairs={{0,1},{1,0},{2,3},{3,2},{4,5},{5,4},{6,7},{7,6},{8,9},{9,8},{10,11... | collective-permute-start | bytes 589832 | tf_op jit(solution)/shard_map/ppermute | solution.py:108
  124.1 1.3 collective-permute-done.1
  125.6 2.1 %collective-permute-start.2 = (f32[256,2]{0,1:T(2,128)S(1)}, f32[256,2]{0,1:T(2,128)S(1)}, u32[]{:S(2)}, u32[]{:S(2)}) collective-permute-start(f32[256,2]{0,1:T(2,128)S(1)} %pad_maximum_fusion.2), channel_id=1, source_target_pairs={{0,1},{1,0},{2,3},{3,2},{4,5},{5,4},{6,7},{7,6},{8,9},{9,8},{10,11... | collective-permute-start | bytes 6152 | tf_op jit(solution)/shard_map/ppermute | solution.py:116
  127.8 0.8 collective-permute-done.2
  128.9 1.6 fusion.13
  130.6 0.8 fusion.12
  131.4 43.4 %all-to-all-done.2 = bf16[32,24,1536]{2,1,0:T(8,128)(2,1)} async-done(((bf16[32,24,1536]{2,1,0:T(8,128)(2,1)}), bf16[32,24,1536]{2,1,0:T(8,128)(2,1)}, u32[]{:S(2)}, u32[]{:S(2)}) %all-to-all-start.2) | async-done | bytes 2359328 | tf_op jit(solution)/shard_map/all_to_all | solution.py:96
  174.7 2.0 %convert_reduce_fusion = f32[24,1536]{1,0:T(8,128)S(1)} fusion(bf16[32,24,1536]{2,1,0:T(8,128)(2,1)} %all-to-all-done.2), kind=kLoop, calls=%fused_computation.2 | loop fusion | flops 2322432 | bytes 2506752 | tf_op jit(solution)/shard_map/reduce_sum | solution.py:97
  176.7 0.7 slice_multiply_fusion
  (56 shorter events, 4.4 us)
Async XLA Ops:
  0.6 4.2 %copy-start = (bf16[512,768]{1,0:T(8,128)(2,1)S(1)}, bf16[512,768]{1,0:T(8,128)(2,1)}, u32[]{:S(2)}) copy-start(bf16[512,768]{1,0:T(8,128)(2,1)} %param.11) | copy-start | bytes 2359300
  4.9 21.1 %copy-start.8 = (bf16[24,768]{1,0:T(8,128)(2,1)S(1)}, bf16[24,768]{1,0:T(8,128)(2,1)}, u32[]{:S(2)}) copy-start(bf16[24,768]{1,0:T(8,128)(2,1)} %param.19) | copy-start | bytes 110596
  4.9 21.1 %copy-start.9 = (bf16[24,768]{1,0:T(8,128)(2,1)S(1)}, bf16[24,768]{1,0:T(8,128)(2,1)}, u32[]{:S(2)}) copy-start(bf16[24,768]{1,0:T(8,128)(2,1)} %param.18) | copy-start | bytes 110596
  7.6 34.2 %all-to-all-start = ((bf16[16,16,384]{2,1,0:T(8,128)(2,1)}), bf16[16,16,384]{2,1,0:T(8,128)(2,1)S(1)}, u32[]{:S(2)}, u32[]{:S(2)}) async-start(bf16[16,16,384]{2,1,0:T(8,128)(2,1)} %bitcast.8), calls=%async_computation | async-start | bytes 393216 | tf_op jit(solution)/shard_map/all_to_all | solution.py:56
  43.4 10.2 %copy-start.6 = (f32[7,7,768]{2,1,0:T(8,128)S(1)}, f32[7,7,768]{2,1,0:T(8,128)}, u32[]{:S(2)}) copy-start(f32[7,7,768]{2,1,0:T(8,128)} %param.15) | copy-start | bytes 451588
  43.4 65.6 %all-to-all-start.1 = ((bf16[32,24,1536]{2,1,0:T(8,128)(2,1)}), bf16[32,24,1536]{2,1,0:T(8,128)(2,1)S(1)}, u32[]{:S(2)}, u32[]{:S(2)}) async-start(bf16[32,24,1536]{2,1,0:T(8,128)(2,1)} %broadcast_in_dim.62), calls=%async_computation.1 | async-start | bytes 4718592 | tf_op jit(solution)/shard_map/all_to_all | solution.py:67
  53.6 12.5 %copy-start.10 = (f32[768]{0:T(1024)S(1)}, f32[768]{0:T(1024)}, u32[]{:S(2)}) copy-start(f32[768]{0:T(1024)} %param.16) | copy-start | bytes 9220
  64.2 6.3 %collective-permute-start = (bf16[256,384]{1,0:T(8,128)(2,1)S(1)}, bf16[256,384]{1,0:T(8,128)(2,1)}, u32[]{:S(2)}, u32[]{:S(2)}) collective-permute-start(bf16[256,384]{1,0:T(8,128)(2,1)S(1)} %bitcast_select_fusion), channel_id=1, source_target_pairs={{0,1},{1,0},{2,3},{3,2},{4,5},{5,4},{6,7},{7,6},{8,9},{9,8},{10,11... | collective-permute-start | bytes 589832 | tf_op jit(solution)/shard_map/ppermute | solution.py:59
  68.5 42.1 %copy-start.11 = (f32[768]{0:T(1024)S(1)}, f32[768]{0:T(1024)}, u32[]{:S(2)}) copy-start(f32[768]{0:T(1024)} %param.17) | copy-start | bytes 9220
  108.9 1.7 copy-start.5
  111.2 0.8 copy-start.3
  111.2 1.1 copy-start.4
  114.4 60.3 %all-to-all-start.2 = ((bf16[32,24,1536]{2,1,0:T(8,128)(2,1)}), bf16[32,24,1536]{2,1,0:T(8,128)(2,1)}, u32[]{:S(2)}, u32[]{:S(2)}) async-start(bf16[32,24,1536]{2,1,0:T(8,128)(2,1)} %pad_maximum_fusion), calls=%async_computation.2 | async-start | bytes 4718592 | tf_op jit(solution)/shard_map/all_to_all | solution.py:96
  120.3 5.1 %copy-start.1 = (f32[256,768]{1,0:T(8,128)S(1)}, f32[256,768]{1,0:T(8,128)}, u32[]{:S(2)}) copy-start(f32[256,768]{1,0:T(8,128)} %get-tuple-element.6) | copy-start | bytes 2359300
  120.3 7.4 %copy-start.7 = (f32[7,7,768]{2,1,0:T(8,128)S(1)}, f32[7,7,768]{2,1,0:T(8,128)}, u32[]{:S(2)}) copy-start(f32[7,7,768]{2,1,0:T(8,128)} %param.15) | copy-start | bytes 451588
  121.9 6.8 %copy-start.2 = (f32[256,768]{1,0:T(8,128)S(1)}, f32[256,768]{1,0:T(8,128)}, u32[]{:S(2)}) copy-start(f32[256,768]{1,0:T(8,128)} %get-tuple-element.6) | copy-start | bytes 2359300
  122.0 3.5 %collective-permute-start.1 = (bf16[256,384]{1,0:T(8,128)(2,1)S(1)}, bf16[256,384]{1,0:T(8,128)(2,1)S(1)}, u32[]{:S(2)}, u32[]{:S(2)}) collective-permute-start(bf16[256,384]{1,0:T(8,128)(2,1)S(1)} %select_convert_fusion), channel_id=1, source_target_pairs={{0,1},{1,0},{2,3},{3,2},{4,5},{5,4},{6,7},{7,6},{8,9},{9,8},{10,11... | collective-permute-start | bytes 589832 | tf_op jit(solution)/shard_map/ppermute | solution.py:108
  125.6 3.1 %collective-permute-start.2 = (f32[256,2]{0,1:T(2,128)S(1)}, f32[256,2]{0,1:T(2,128)S(1)}, u32[]{:S(2)}, u32[]{:S(2)}) collective-permute-start(f32[256,2]{0,1:T(2,128)S(1)} %pad_maximum_fusion.2), channel_id=1, source_target_pairs={{0,1},{1,0},{2,3},{3,2},{4,5},{5,4},{6,7},{7,6},{8,9},{9,8},{10,11... | collective-permute-start | bytes 6152 | tf_op jit(solution)/shard_map/ppermute | solution.py:116

commit v2 on v1

--- a/solution.py
+++ b/solution.py
@@ -1,3 +1,5 @@
+import functools
+
 import jax
 import jax.numpy as jnp
 from jax import lax
@@ -25,10 +27,64 @@
     return (hidden_in * cumulative, cumulative + hidden_in * density)
 
 
+def ring_perm(size, width, step_y, step_x):
+    height = size // width
+    return [
+        (y * width + x, ((y + step_y) % height) * width + (x + step_x) % width)
+        for y in range(height)
+        for x in range(width)
+    ]
+
+
+def ring_gather(block, width):
+    size = lax.axis_size("fsdp")
+    height = size // width
+    f = lax.axis_index("fsdp")
+    y, x = f // width, f % width
+    rows = block.shape[0]
+
+    def send(value, step_y, step_x):
+        return lax.ppermute(value, "fsdp", ring_perm(size, width, step_y, step_x))
+
+    rel = [None] * width
+    rel[0] = block
+    right, left = block, block
+    for k in range(1, width // 2 + 1):
+        if 2 * k == width:
+            half = rows // 2
+            low = send(right[:half], 0, 1)
+            high = send(left[half:], 0, -1)
+            rel[k] = jnp.concatenate([low, high], axis=0)
+        else:
+            right = send(right, 0, 1)
+            left = send(left, 0, -1)
+            rel[width - k] = right
+            rel[k] = left
+    xblock = jnp.stack(rel)
+    rely = [None] * height
+    rely[0] = xblock
+    up, down = xblock, xblock
+    for m in range(1, height // 2 + 1):
+        if 2 * m == height:
+            half = rows // 2
+            low = send(up[:, :half], -1, 0)
+            high = send(down[:, half:], 1, 0)
+            rely[m] = jnp.concatenate([low, high], axis=1)
+        else:
+            up = send(up, -1, 0)
+            down = send(down, 1, 0)
+            rely[m] = up
+            rely[height - m] = down
+    full = jnp.stack(rely)
+    full = jnp.roll(full, (y, x), axis=(0, 1))
+    return full.reshape(size * rows, block.shape[1])
+
+
 SWAP = [(0, 1), (1, 0)]
 
 
 def body(
+    fsdp_x,
     tile_rows,
     grad_seq,
     visual_pos,
@@ -63,10 +119,7 @@
 
     hid = weight_in.shape[1]
     both = jnp.concatenate([weight_in, weight_out], axis=1)
-    both_tiled = jnp.broadcast_to(both[None], (shards,) + both.shape)
-    both_full = lax.all_to_all(both_tiled, "fsdp", split_axis=0, concat_axis=0).reshape(
-        shards * both.shape[0], both.shape[1]
-    )
+    both_full = ring_gather(both, fsdp_x)
     w_in_full = both_full[:, :hid]
     w_out_full = both_full[:, hid:]
 
@@ -125,6 +178,14 @@
     return (grad_tiles, grad_in, grad_outw)
 
 
+def x_width(mesh):
+    group = mesh.devices[0, :, 0]
+    try:
+        return len({d.coords[0] for d in group})
+    except (AttributeError, TypeError, IndexError):
+        return 4
+
+
 def solution(mesh):
     in_specs = (
         P(("dp", "fsdp"), None),
@@ -139,4 +200,4 @@
         P("fsdp", "llm"),
     )
     out_specs = (P(("dp", "fsdp"), "llm"), P(("dp", "fsdp"), "llm"), P(("dp", "fsdp"), "llm"))
-    return jax.shard_map(body, mesh=mesh, in_specs=in_specs, out_specs=out_specs, check_vma=False)
+    return jax.shard_map(functools.partial(body, x_width(mesh)), mesh=mesh, in_specs=in_specs, out_specs=out_specs, check_vma=False)

time: 178 us -> 178 us (level)
  the two profiles are of different devices: /device:TPU:80 before, /device:TPU:2 now
where the time goes in v2:
time: 178 us; the launch traced here: 176 us
  starting transfers between devices  75.3 us (42%)
  waiting for transfers between devices  51.4 us (29%)
  local copies, waits for them, and re-layouts  20.1 us (11%)
  other arithmetic  17.2 us (10%)
  matrix products  10.4 us (6%)
  between operations  1.96 us (1%)
    ppermute x12, starting transfers between devices, send(): return lax.ppermute(value, 'fsdp', ring_perm(size, width, step_y, step_x))  52.3 us
    all_to_all x1, waiting for transfers between devices, body(): gathered = lax.all_to_all(terms, 'fsdp', split_axis=0, concat_axis=0)  37.7 us
    unnamed x43, local copies, waits for them, and re-layouts  13.6 us
    ppermute x12, waiting for transfers between devices, send(): return lax.ppermute(value, 'fsdp', ring_perm(size, width, step_y, step_x))  11.6 us
    all_to_all x1, starting transfers between devices, body(): gathered = lax.all_to_all(terms, 'fsdp', split_axis=0, concat_axis=0)  9.39 us
    all_to_all x1, starting transfers between devices, body(): lax.all_to_all(out_half, 'dp', split_axis=0, concat_axis=0, tiled=True)  7.69 us
    conv_general_dilated x2, matrix products, depthwise(): lax.conv_general_dilated(images, kernel[:, :, None, :], (1, 1), 'SAME', d...  6.4 us
    unnamed x5, other arithmetic  5.32 us
  transfers between devices with their start and end apart: 17, of which 9 were waited for; matrix products, arithmetic and copies ran while one was open for 15% of the time, Pallas kernels for 0%

profile of v2, /device:TPU:2, one launch (start us, length us, event | category | flops | bytes accessed | tf_op | source)
XLA Modules:
  0.0 176.5 jit_solution(15474362840952568380)
XLA Ops:
  2.3 3.4 %collective-permute-start.2 = (bf16[24,1536]{1,0:T(8,128)(2,1)S(1)}, bf16[24,1536]{1,0:T(8,128)(2,1)S(1)}, u32[]{:S(2)}, u32[]{:S(2)}) collective-permute-start(bf16[24,1536]{1,0:T(8,128)(2,1)S(1)} %constant_dynamic-update-slice_fusion), channel_id=1, source_target_pairs={{0,2},{2,4},{4,6},{6,0},{8,10},{10,12},{12,14},{14,8},{16,18},{18,... | collective-permute-start | bytes 221192 | tf_op jit(solution)/shard_map/ppermute | solution.py:47
  5.7 13.6 %collective-permute-start.1 = (bf16[24,1536]{1,0:T(8,128)(2,1)S(1)}, bf16[24,1536]{1,0:T(8,128)(2,1)S(1)}, u32[]{:S(2)}, u32[]{:S(2)}) collective-permute-start(bf16[24,1536]{1,0:T(8,128)(2,1)S(1)} %constant_dynamic-update-slice_fusion), channel_id=1, source_target_pairs={{0,6},{2,0},{4,2},{6,4},{8,14},{10,8},{12,10},{14,12},{16,22},{18,... | collective-permute-start | bytes 221192 | tf_op jit(solution)/shard_map/ppermute | solution.py:47
  26.1 7.7 %all-to-all-start = ((bf16[16,16,384]{2,1,0:T(8,128)(2,1)}), bf16[16,16,384]{2,1,0:T(8,128)(2,1)S(1)}, u32[]{:S(2)}, u32[]{:S(2)}) async-start(bf16[16,16,384]{2,1,0:T(8,128)(2,1)} %bitcast.8), calls=%async_computation | async-start | bytes 393216 | tf_op jit(solution)/shard_map/all_to_all | solution.py:112
  33.9 4.8 %fusion.30 = (f32[4,8,8]{0,2,1:T(8,128)S(1)}, f32[4,8,8,768]{3,0,2,1:T(4,128)S(1)}) fusion(f32[7,7,1,768]{3,1,0,2:T(8,128)S(1)} %bitcast.97, bf16[4,8,8,768]{3,2,1,0:T(8,128)(2,1)S(1)} %bitcast.105), kind=kOutput, calls=%fused_computation.95 | convolution fusion | flops 71565056 | bytes 1331200 | tf_op jit(solution)/shard_map/conv_general_dilated | solution.py:13
  39.8 3.4 %collective-permute-start.3 = (bf16[12,1536]{1,0:T(8,128)(2,1)S(1)}, bf16[12,1536]{1,0:T(8,128)(2,1)S(1)}, u32[]{:S(2)}, u32[]{:S(2)}) collective-permute-start(bf16[12,1536]{1,0:T(8,128)(2,1)S(1)} %slice.52), channel_id=1, source_target_pairs={{0,2},{2,4},{4,6},{6,0},{8,10},{10,12},{12,14},{14,8},{16,18},{18,... | collective-permute-start | bytes 110600 | tf_op jit(solution)/shard_map/ppermute | solution.py:47
  43.2 2.4 %collective-permute-start.4 = (bf16[12,1536]{1,0:T(8,128)(2,1)S(1)}, bf16[12,1536]{1,0:T(8,128)(2,1)S(1)}, u32[]{:S(2)}, u32[]{:S(2)}) collective-permute-start(bf16[12,1536]{1,0:T(8,128)(2,1)S(1)} %slice.53), channel_id=1, source_target_pairs={{0,6},{2,0},{4,2},{6,4},{8,14},{10,8},{12,10},{14,12},{16,22},{18,... | collective-permute-start | bytes 110600 | tf_op jit(solution)/shard_map/ppermute | solution.py:47
  46.5 2.7 %collective-permute-done.4 = bf16[12,1536]{1,0:T(8,128)(2,1)S(1)} collective-permute-done((bf16[12,1536]{1,0:T(8,128)(2,1)S(1)}, bf16[12,1536]{1,0:T(8,128)(2,1)S(1)}, u32[]{:S(2)}, u32[]{:S(2)}) %collective-permute-start.4) | collective-permute-done | bytes 36896 | tf_op jit(solution)/shard_map/ppermute | solution.py:47
  50.0 5.4 %collective-permute-start.5 = (bf16[4,24,1536]{2,1,0:T(8,128)(2,1)}, bf16[4,24,1536]{2,1,0:T(8,128)(2,1)S(1)}, u32[]{:S(2)}, u32[]{:S(2)}) collective-permute-start(bf16[4,24,1536]{2,1,0:T(8,128)(2,1)} %pad_maximum_fusion.1), channel_id=1, source_target_pairs={{0,56},{2,58},{4,60},{6,62},{8,0},{10,2},{12,4},{14,6},{16,8},{18,... | collective-permute-start | bytes 884744 | tf_op jit(solution)/shard_map/ppermute | solution.py:47
  55.3 1.9 %collective-permute-start.9 = (bf16[4,24,1536]{2,1,0:T(8,128)(2,1)}, bf16[4,24,1536]{2,1,0:T(8,128)(2,1)S(1)}, u32[]{:S(2)}, u32[]{:S(2)}) collective-permute-start(bf16[4,24,1536]{2,1,0:T(8,128)(2,1)} %pad_maximum_fusion.1), channel_id=1, source_target_pairs={{0,8},{2,10},{4,12},{6,14},{8,16},{10,18},{12,20},{14,22},{16,24},... | collective-permute-start | bytes 884744 | tf_op jit(solution)/shard_map/ppermute | solution.py:47
  57.5 1.7 bitcast_dynamic-update-slice_fusion.12
  59.9 5.5 %collective-permute-start.6 = (bf16[4,24,1536]{2,1,0:T(8,128)(2,1)S(1)}, bf16[4,24,1536]{2,1,0:T(8,128)(2,1)}, u32[]{:S(2)}, u32[]{:S(2)}) collective-permute-start(bf16[4,24,1536]{2,1,0:T(8,128)(2,1)S(1)} %collective-permute-done.5), channel_id=1, source_target_pairs={{0,56},{2,58},{4,60},{6,62},{8,0},{10,2},{12,4},{14,6},{16,8},{18,... | collective-permute-start | bytes 884744 | tf_op jit(solution)/shard_map/ppermute | solution.py:47
  65.4 1.9 %collective-permute-start.10 = (bf16[4,24,1536]{2,1,0:T(8,128)(2,1)S(1)}, bf16[4,24,1536]{2,1,0:T(8,128)(2,1)}, u32[]{:S(2)}, u32[]{:S(2)}) collective-permute-start(bf16[4,24,1536]{2,1,0:T(8,128)(2,1)S(1)} %collective-permute-done.9), channel_id=1, source_target_pairs={{0,8},{2,10},{4,12},{6,14},{8,16},{10,18},{12,20},{14,22},{16,24},... | collective-permute-start | bytes 884744 | tf_op jit(solution)/shard_map/ppermute | solution.py:47
  68.1 1.5 collective-permute-done.6
  69.6 5.7 %collective-permute-start.7 = (bf16[4,24,1536]{2,1,0:T(8,128)(2,1)}, bf16[4,24,1536]{2,1,0:T(8,128)(2,1)S(1)}, u32[]{:S(2)}, u32[]{:S(2)}) collective-permute-start(bf16[4,24,1536]{2,1,0:T(8,128)(2,1)} %collective-permute-done.6), channel_id=1, source_target_pairs={{0,56},{2,58},{4,60},{6,62},{8,0},{10,2},{12,4},{14,6},{16,8},{18,... | collective-permute-start | bytes 884744 | tf_op jit(solution)/shard_map/ppermute | solution.py:47
  75.4 2.0 %collective-permute-start.11 = (bf16[4,24,1536]{2,1,0:T(8,128)(2,1)}, bf16[4,24,1536]{2,1,0:T(8,128)(2,1)S(1)}, u32[]{:S(2)}, u32[]{:S(2)}) collective-permute-start(bf16[4,24,1536]{2,1,0:T(8,128)(2,1)} %collective-permute-done.10), channel_id=1, source_target_pairs={{0,8},{2,10},{4,12},{6,14},{8,16},{10,18},{12,20},{14,22},{16,24},... | collective-permute-start | bytes 884744 | tf_op jit(solution)/shard_map/ppermute | solution.py:47
  77.6 1.9 %collective-permute-start = (bf16[256,384]{1,0:T(8,128)(2,1)S(1)}, bf16[256,384]{1,0:T(8,128)(2,1)S(1)}, u32[]{:S(2)}, u32[]{:S(2)}) collective-permute-start(bf16[256,384]{1,0:T(8,128)(2,1)S(1)} %bitcast_select_fusion), channel_id=1, source_target_pairs={{0,1},{1,0},{2,3},{3,2},{4,5},{5,4},{6,7},{7,6},{8,9},{9,8},{10,11... | collective-permute-start | bytes 589832 | tf_op jit(solution)/shard_map/ppermute | solution.py:115
  79.5 1.7 bitcast_dynamic-update-slice_fusion.8
  81.3 4.2 %collective-permute-done.11 = bf16[4,24,1536]{2,1,0:T(8,128)(2,1)S(1)} collective-permute-done((bf16[4,24,1536]{2,1,0:T(8,128)(2,1)}, bf16[4,24,1536]{2,1,0:T(8,128)(2,1)S(1)}, u32[]{:S(2)}, u32[]{:S(2)}) %collective-permute-start.11) | collective-permute-done | bytes 294944 | tf_op jit(solution)/shard_map/ppermute | solution.py:47
  85.6 1.9 %collective-permute-start.12 = (bf16[4,12,1536]{2,1,0:T(8,128)(2,1)S(1)}, bf16[4,12,1536]{2,1,0:T(8,128)(2,1)S(1)}, u32[]{:S(2)}, u32[]{:S(2)}) collective-permute-start(bf16[4,12,1536]{2,1,0:T(8,128)(2,1)S(1)} %slice.55), channel_id=1, source_target_pairs={{0,8},{2,10},{4,12},{6,14},{8,16},{10,18},{12,20},{14,22},{16,24},... | collective-permute-start | bytes 442376 | tf_op jit(solution)/shard_map/ppermute | solution.py:47
  87.6 5.1 %collective-permute-start.8 = (bf16[4,12,1536]{2,1,0:T(8,128)(2,1)S(1)}, bf16[4,12,1536]{2,1,0:T(8,128)(2,1)S(1)}, u32[]{:S(2)}, u32[]{:S(2)}) collective-permute-start(bf16[4,12,1536]{2,1,0:T(8,128)(2,1)S(1)} %slice.54), channel_id=1, source_target_pairs={{0,56},{2,58},{4,60},{6,62},{8,0},{10,2},{12,4},{14,6},{16,8},{18,... | collective-permute-start | bytes 442376 | tf_op jit(solution)/shard_map/ppermute | solution.py:47
  97.4 1.7 bitcast_dynamic-update-slice_fusion.2
  101.3 1.7 bitcast_dynamic-update-slice_fusion.9
  105.2 1.7 bitcast_dynamic-update-slice_fusion.3
  107.7 1.8 %constant_dynamic-slice_fusion.1 = bf16[8,4,24,1536]{3,2,1,0:T(8,128)(2,1)S(1)} fusion(bf16[16,4,24,1536]{3,2,1,0:T(8,128)(2,1)} %bitcast_dynamic-update-slice_fusion.1, s32[]{:T(128)S(6)} %select_n.130), kind=kLoop, calls=%fused_computation.86 | loop fusion | bytes 4718596 | tf_op jit(solution)/shard_map/jit(_roll_dynamic)/dynamic_slice | solution.py:79
  112.8 1.6 pad_maximum_fusion
  114.4 9.4 %all-to-all-start.1 = ((bf16[32,24,1536]{2,1,0:T(8,128)(2,1)}), bf16[32,24,1536]{2,1,0:T(8,128)(2,1)S(1)}, u32[]{:S(2)}, u32[]{:S(2)}) async-start(bf16[32,24,1536]{2,1,0:T(8,128)(2,1)} %pad_maximum_fusion), calls=%async_computation.1 | async-start | bytes 4718592 | tf_op jit(solution)/shard_map/all_to_all | solution.py:149
  123.8 1.9 %fusion.3 = f32[256,768]{1,0:T(8,128)S(1)} fusion(bf16[256,768]{1,0:T(8,128)(2,1)} %copy-done.3, bf16[768,1536]{1,0:T(8,128)(2,1)} %bitcast.81), kind=kOutput, calls=%fused_computation.13 | convolution fusion | flops 301989888 | bytes 2359296 | tf_op jit(solution)/shard_map/dot_general | solution.py:154
  125.8 1.9 %collective-permute-start.13 = (bf16[256,384]{1,0:T(8,128)(2,1)S(1)}, bf16[256,384]{1,0:T(8,128)(2,1)S(1)}, u32[]{:S(2)}, u32[]{:S(2)}) collective-permute-start(bf16[256,384]{1,0:T(8,128)(2,1)S(1)} %select_convert_fusion), channel_id=1, source_target_pairs={{0,1},{1,0},{2,3},{3,2},{4,5},{5,4},{6,7},{7,6},{8,9},{9,8},{10,11... | collective-permute-start | bytes 589832 | tf_op jit(solution)/shard_map/ppermute | solution.py:161
  129.1 1.8 %fusion.28 = (f32[256]{0:T(256)S(1)}, f32[256]{0:T(256)S(1)}, f32[256,384]{1,0:T(8,128)}) fusion(f32[256,768]{1,0:T(8,128)} %copy-done.2, s32[]{:T(128)S(6)} %select_n.123, f32[384]{0:T(512)S(1)} %dynamic_slice.23, bf16[256,384]{1,0:T(8,128)(2,1)S(1)} %collective-permute-done.13, f32[256,768]{1,0:T(8,128)S(1)} %fusion.3, pred[]{:T(512)S(6)} %eq.13), kind=kLoop, calls=%fused_computation.94 | loop fusion | flops 687616 | bytes 1773061 | tf_op jit(solution)/shard_map/reduce_sum | solution.py:167
  130.9 2.0 %collective-permute-start.14 = (f32[256,2]{0,1:T(2,128)S(1)}, f32[256,2]{0,1:T(2,128)S(1)}, u32[]{:S(2)}, u32[]{:S(2)}) collective-permute-start(f32[256,2]{0,1:T(2,128)S(1)} %pad_maximum_fusion.2), channel_id=1, source_target_pairs={{0,1},{1,0},{2,3},{3,2},{4,5},{5,4},{6,7},{7,6},{8,9},{9,8},{10,11... | collective-permute-start | bytes 6152 | tf_op jit(solution)/shard_map/ppermute | solution.py:169
  135.3 1.6 fusion.14
  137.8 37.7 %all-to-all-done.1 = bf16[32,24,1536]{2,1,0:T(8,128)(2,1)S(1)} async-done(((bf16[32,24,1536]{2,1,0:T(8,128)(2,1)}), bf16[32,24,1536]{2,1,0:T(8,128)(2,1)S(1)}, u32[]{:S(2)}, u32[]{:S(2)}) %all-to-all-start.1) | async-done | bytes 2359328 | tf_op jit(solution)/shard_map/all_to_all | solution.py:149
  (107 shorter events, 31.0 us)
Async XLA Ops:
  0.6 22.8 %copy-start = (bf16[512,768]{1,0:T(8,128)(2,1)S(1)}, bf16[512,768]{1,0:T(8,128)(2,1)}, u32[]{:S(2)}) copy-start(bf16[512,768]{1,0:T(8,128)(2,1)} %param.11) | copy-start | bytes 2359300
  0.6 33.2 %copy-start.13 = (bf16[256,768]{1,0:T(8,128)(2,1)S(1)}, bf16[256,768]{1,0:T(8,128)(2,1)}, u32[]{:S(2)}) copy-start(bf16[256,768]{1,0:T(8,128)(2,1)} %param.10) | copy-start | bytes 1179652
  0.7 33.2 %copy-start.10 = (f32[7,7,768]{2,1,0:T(8,128)S(1)}, f32[7,7,768]{2,1,0:T(8,128)}, u32[]{:S(2)}) copy-start(f32[7,7,768]{2,1,0:T(8,128)} %param.15) | copy-start | bytes 451588
  2.3 46.9 %copy-start.8 = (bf16[24,1536]{1,0:T(8,128)(2,1)}, bf16[24,1536]{1,0:T(8,128)(2,1)S(1)}, u32[]{:S(2)}) copy-start(bf16[24,1536]{1,0:T(8,128)(2,1)S(1)} %constant_dynamic-update-slice_fusion) | copy-start | bytes 221188
  2.3 37.4 %collective-permute-start.2 = (bf16[24,1536]{1,0:T(8,128)(2,1)S(1)}, bf16[24,1536]{1,0:T(8,128)(2,1)S(1)}, u32[]{:S(2)}, u32[]{:S(2)}) collective-permute-start(bf16[24,1536]{1,0:T(8,128)(2,1)S(1)} %constant_dynamic-update-slice_fusion), channel_id=1, source_target_pairs={{0,2},{2,4},{4,6},{6,0},{8,10},{10,12},{12,14},{14,8},{16,18},{18,... | collective-permute-start | bytes 221192 | tf_op jit(solution)/shard_map/ppermute | solution.py:47
  5.7 37.5 %collective-permute-start.1 = (bf16[24,1536]{1,0:T(8,128)(2,1)S(1)}, bf16[24,1536]{1,0:T(8,128)(2,1)S(1)}, u32[]{:S(2)}, u32[]{:S(2)}) collective-permute-start(bf16[24,1536]{1,0:T(8,128)(2,1)S(1)} %constant_dynamic-update-slice_fusion), channel_id=1, source_target_pairs={{0,6},{2,0},{4,2},{6,4},{8,14},{10,8},{12,10},{14,12},{16,22},{18,... | collective-permute-start | bytes 221192 | tf_op jit(solution)/shard_map/ppermute | solution.py:47
  23.5 22.2 %copy-start.12 = (f32[768]{0:T(1024)S(1)}, f32[768]{0:T(1024)}, u32[]{:S(2)}) copy-start(f32[768]{0:T(1024)} %param.16) | copy-start | bytes 9220
  26.1 51.3 %all-to-all-start = ((bf16[16,16,384]{2,1,0:T(8,128)(2,1)}), bf16[16,16,384]{2,1,0:T(8,128)(2,1)S(1)}, u32[]{:S(2)}, u32[]{:S(2)}) async-start(bf16[16,16,384]{2,1,0:T(8,128)(2,1)} %bitcast.8), calls=%async_computation | async-start | bytes 393216 | tf_op jit(solution)/shard_map/all_to_all | solution.py:112
  39.8 6.8 %collective-permute-start.3 = (bf16[12,1536]{1,0:T(8,128)(2,1)S(1)}, bf16[12,1536]{1,0:T(8,128)(2,1)S(1)}, u32[]{:S(2)}, u32[]{:S(2)}) collective-permute-start(bf16[12,1536]{1,0:T(8,128)(2,1)S(1)} %slice.52), channel_id=1, source_target_pairs={{0,2},{2,4},{4,6},{6,0},{8,10},{10,12},{12,14},{14,8},{16,18},{18,... | collective-permute-start | bytes 110600 | tf_op jit(solution)/shard_map/ppermute | solution.py:47
  43.2 6.0 %collective-permute-start.4 = (bf16[12,1536]{1,0:T(8,128)(2,1)S(1)}, bf16[12,1536]{1,0:T(8,128)(2,1)S(1)}, u32[]{:S(2)}, u32[]{:S(2)}) collective-permute-start(bf16[12,1536]{1,0:T(8,128)(2,1)S(1)} %slice.53), channel_id=1, source_target_pairs={{0,6},{2,0},{4,2},{6,4},{8,14},{10,8},{12,10},{14,12},{16,22},{18,... | collective-permute-start | bytes 110600 | tf_op jit(solution)/shard_map/ppermute | solution.py:47
  45.8 64.6 %copy-start.2 = (f32[256,768]{1,0:T(8,128)}, f32[256,768]{1,0:T(8,128)S(1)}, u32[]{:S(2)}) copy-start(f32[256,768]{1,0:T(8,128)S(1)} %get-tuple-element.6) | copy-start | bytes 2359300
  50.0 10.0 %collective-permute-start.5 = (bf16[4,24,1536]{2,1,0:T(8,128)(2,1)}, bf16[4,24,1536]{2,1,0:T(8,128)(2,1)S(1)}, u32[]{:S(2)}, u32[]{:S(2)}) collective-permute-start(bf16[4,24,1536]{2,1,0:T(8,128)(2,1)} %pad_maximum_fusion.1), channel_id=1, source_target_pairs={{0,56},{2,58},{4,60},{6,62},{8,0},{10,2},{12,4},{14,6},{16,8},{18,... | collective-permute-start | bytes 884744 | tf_op jit(solution)/shard_map/ppermute | solution.py:47
  55.3 10.1 %collective-permute-start.9 = (bf16[4,24,1536]{2,1,0:T(8,128)(2,1)}, bf16[4,24,1536]{2,1,0:T(8,128)(2,1)S(1)}, u32[]{:S(2)}, u32[]{:S(2)}) collective-permute-start(bf16[4,24,1536]{2,1,0:T(8,128)(2,1)} %pad_maximum_fusion.1), channel_id=1, source_target_pairs={{0,8},{2,10},{4,12},{6,14},{8,16},{10,18},{12,20},{14,22},{16,24},... | collective-permute-start | bytes 884744 | tf_op jit(solution)/shard_map/ppermute | solution.py:47
  57.5 42.3 %copy-start.9 = (bf16[24,1536]{1,0:T(8,128)(2,1)S(1)}, bf16[24,1536]{1,0:T(8,128)(2,1)}, u32[]{:S(2)}) copy-start(bf16[24,1536]{1,0:T(8,128)(2,1)} %copy-done.8) | copy-start | bytes 221188
  59.9 8.2 %copy-start.6 = (bf16[4,24,1536]{2,1,0:T(8,128)(2,1)}, bf16[4,24,1536]{2,1,0:T(8,128)(2,1)S(1)}, u32[]{:S(2)}) copy-start(bf16[4,24,1536]{2,1,0:T(8,128)(2,1)S(1)} %collective-permute-done.5) | copy-start | bytes 884740
  59.9 9.7 %collective-permute-start.6 = (bf16[4,24,1536]{2,1,0:T(8,128)(2,1)S(1)}, bf16[4,24,1536]{2,1,0:T(8,128)(2,1)}, u32[]{:S(2)}, u32[]{:S(2)}) collective-permute-start(bf16[4,24,1536]{2,1,0:T(8,128)(2,1)S(1)} %collective-permute-done.5), channel_id=1, source_target_pairs={{0,56},{2,58},{4,60},{6,62},{8,0},{10,2},{12,4},{14,6},{16,8},{18,... | collective-permute-start | bytes 884744 | tf_op jit(solution)/shard_map/ppermute | solution.py:47
  65.4 9.9 %copy-start.4 = (bf16[4,24,1536]{2,1,0:T(8,128)(2,1)}, bf16[4,24,1536]{2,1,0:T(8,128)(2,1)S(1)}, u32[]{:S(2)}) copy-start(bf16[4,24,1536]{2,1,0:T(8,128)(2,1)S(1)} %collective-permute-done.9) | copy-start | bytes 884740
  65.4 9.9 %collective-permute-start.10 = (bf16[4,24,1536]{2,1,0:T(8,128)(2,1)S(1)}, bf16[4,24,1536]{2,1,0:T(8,128)(2,1)}, u32[]{:S(2)}, u32[]{:S(2)}) collective-permute-start(bf16[4,24,1536]{2,1,0:T(8,128)(2,1)S(1)} %collective-permute-done.9), channel_id=1, source_target_pairs={{0,8},{2,10},{4,12},{6,14},{8,16},{10,18},{12,20},{14,22},{16,24},... | collective-permute-start | bytes 884744 | tf_op jit(solution)/shard_map/ppermute | solution.py:47
  69.6 17.9 %collective-permute-start.7 = (bf16[4,24,1536]{2,1,0:T(8,128)(2,1)}, bf16[4,24,1536]{2,1,0:T(8,128)(2,1)S(1)}, u32[]{:S(2)}, u32[]{:S(2)}) collective-permute-start(bf16[4,24,1536]{2,1,0:T(8,128)(2,1)} %collective-permute-done.6), channel_id=1, source_target_pairs={{0,56},{2,58},{4,60},{6,62},{8,0},{10,2},{12,4},{14,6},{16,8},{18,... | collective-permute-start | bytes 884744 | tf_op jit(solution)/shard_map/ppermute | solution.py:47
  75.4 23.7 %copy-start.5 = (bf16[4,24,1536]{2,1,0:T(8,128)(2,1)S(1)}, bf16[4,24,1536]{2,1,0:T(8,128)(2,1)}, u32[]{:S(2)}) copy-start(bf16[4,24,1536]{2,1,0:T(8,128)(2,1)} %copy-done.4) | copy-start | bytes 884740
  75.4 10.2 %collective-permute-start.11 = (bf16[4,24,1536]{2,1,0:T(8,128)(2,1)}, bf16[4,24,1536]{2,1,0:T(8,128)(2,1)S(1)}, u32[]{:S(2)}, u32[]{:S(2)}) collective-permute-start(bf16[4,24,1536]{2,1,0:T(8,128)(2,1)} %collective-permute-done.10), channel_id=1, source_target_pairs={{0,8},{2,10},{4,12},{6,14},{8,16},{10,18},{12,20},{14,22},{16,24},... | collective-permute-start | bytes 884744 | tf_op jit(solution)/shard_map/ppermute | solution.py:47
  77.4 23.1 %copy-start.7 = (bf16[4,24,1536]{2,1,0:T(8,128)(2,1)S(1)}, bf16[4,24,1536]{2,1,0:T(8,128)(2,1)}, u32[]{:S(2)}) copy-start(bf16[4,24,1536]{2,1,0:T(8,128)(2,1)} %copy-done.6) | copy-start | bytes 884740
  77.6 3.6 %collective-permute-start = (bf16[256,384]{1,0:T(8,128)(2,1)S(1)}, bf16[256,384]{1,0:T(8,128)(2,1)S(1)}, u32[]{:S(2)}, u32[]{:S(2)}) collective-permute-start(bf16[256,384]{1,0:T(8,128)(2,1)S(1)} %bitcast_select_fusion), channel_id=1, source_target_pairs={{0,1},{1,0},{2,3},{3,2},{4,5},{5,4},{6,7},{7,6},{8,9},{9,8},{10,11... | collective-permute-start | bytes 589832 | tf_op jit(solution)/shard_map/ppermute | solution.py:115
  85.6 8.8 %collective-permute-start.12 = (bf16[4,12,1536]{2,1,0:T(8,128)(2,1)S(1)}, bf16[4,12,1536]{2,1,0:T(8,128)(2,1)S(1)}, u32[]{:S(2)}, u32[]{:S(2)}) collective-permute-start(bf16[4,12,1536]{2,1,0:T(8,128)(2,1)S(1)} %slice.55), channel_id=1, source_target_pairs={{0,8},{2,10},{4,12},{6,14},{8,16},{10,18},{12,20},{14,22},{16,24},... | collective-permute-start | bytes 442376 | tf_op jit(solution)/shard_map/ppermute | solution.py:47
  87.6 8.3 %collective-permute-start.8 = (bf16[4,12,1536]{2,1,0:T(8,128)(2,1)S(1)}, bf16[4,12,1536]{2,1,0:T(8,128)(2,1)S(1)}, u32[]{:S(2)}, u32[]{:S(2)}) collective-permute-start(bf16[4,12,1536]{2,1,0:T(8,128)(2,1)S(1)} %slice.54), channel_id=1, source_target_pairs={{0,56},{2,58},{4,60},{6,62},{8,0},{10,2},{12,4},{14,6},{16,8},{18,... | collective-permute-start | bytes 442376 | tf_op jit(solution)/shard_map/ppermute | solution.py:47
  109.6 1.4 copy-start.14
  110.4 1.7 copy-start.1
  111.5 0.8 copy-start.3
  114.4 61.1 %all-to-all-start.1 = ((bf16[32,24,1536]{2,1,0:T(8,128)(2,1)}), bf16[32,24,1536]{2,1,0:T(8,128)(2,1)S(1)}, u32[]{:S(2)}, u32[]{:S(2)}) async-start(bf16[32,24,1536]{2,1,0:T(8,128)(2,1)} %pad_maximum_fusion), calls=%async_computation.1 | async-start | bytes 4718592 | tf_op jit(solution)/shard_map/all_to_all | solution.py:149
  123.8 9.2 %copy-start.11 = (f32[7,7,768]{2,1,0:T(8,128)S(1)}, f32[7,7,768]{2,1,0:T(8,128)}, u32[]{:S(2)}) copy-start(f32[7,7,768]{2,1,0:T(8,128)} %param.15) | copy-start | bytes 451588
  125.8 3.3 %collective-permute-start.13 = (bf16[256,384]{1,0:T(8,128)(2,1)S(1)}, bf16[256,384]{1,0:T(8,128)(2,1)S(1)}, u32[]{:S(2)}, u32[]{:S(2)}) collective-permute-start(bf16[256,384]{1,0:T(8,128)(2,1)S(1)} %select_convert_fusion), channel_id=1, source_target_pairs={{0,1},{1,0},{2,3},{3,2},{4,5},{5,4},{6,7},{7,6},{8,9},{9,8},{10,11... | collective-permute-start | bytes 589832 | tf_op jit(solution)/shard_map/ppermute | solution.py:161
  130.9 3.0 %collective-permute-start.14 = (f32[256,2]{0,1:T(2,128)S(1)}, f32[256,2]{0,1:T(2,128)S(1)}, u32[]{:S(2)}, u32[]{:S(2)}) collective-permute-start(f32[256,2]{0,1:T(2,128)S(1)} %pad_maximum_fusion.2), channel_id=1, source_target_pairs={{0,1},{1,0},{2,3},{3,2},{4,5},{5,4},{6,7},{7,6},{8,9},{9,8},{10,11... | collective-permute-start | bytes 6152 | tf_op jit(solution)/shard_map/ppermute | solution.py:169

commit v3 on v1

--- a/solution.py
+++ b/solution.py
@@ -41,7 +41,9 @@
     weight_out,
 ):
     groups = lax.axis_size("dp")
-    shards = lax.axis_size("fsdp")
+    height = lax.axis_size("fy")
+    width = lax.axis_size("fx")
+    shards = height * width
     row_count = tile_rows.shape[0]
     channels = tile_rows.shape[1]
     block_rows = row_count // groups
@@ -63,8 +65,10 @@
 
     hid = weight_in.shape[1]
     both = jnp.concatenate([weight_in, weight_out], axis=1)
-    both_tiled = jnp.broadcast_to(both[None], (shards,) + both.shape)
-    both_full = lax.all_to_all(both_tiled, "fsdp", split_axis=0, concat_axis=0).reshape(
+    y_tiled = jnp.broadcast_to(both[None], (height,) + both.shape)
+    y_block = lax.all_to_all(y_tiled, "fy", split_axis=0, concat_axis=0)
+    x_tiled = jnp.broadcast_to(y_block[:, None], (height, width) + both.shape)
+    both_full = lax.all_to_all(x_tiled, "fx", split_axis=1, concat_axis=1, tiled=True).reshape(
         shards * both.shape[0], both.shape[1]
     )
     w_in_full = both_full[:, :hid]
@@ -92,9 +96,11 @@
         scaled, hidden, (((0,), (0,)), ((), ())), preferred_element_type=jnp.float32
     )
     terms = jnp.concatenate([term_in, term_out], axis=1).astype(jnp.bfloat16)
-    terms = terms.reshape(shards, channels // shards, 2 * hid)
-    gathered = lax.all_to_all(terms, "fsdp", split_axis=0, concat_axis=0)
-    totals = jnp.sum(gathered.astype(jnp.float32), axis=0)
+    terms = terms.reshape(height, width, channels // shards, 2 * hid)
+    x_parts = lax.all_to_all(terms, "fx", split_axis=1, concat_axis=1, tiled=True)
+    x_sums = jnp.sum(x_parts.astype(jnp.float32), axis=1).astype(jnp.bfloat16)
+    y_parts = lax.all_to_all(x_sums, "fy", split_axis=0, concat_axis=0, tiled=True)
+    totals = jnp.sum(y_parts.astype(jnp.float32), axis=0)
     grad_in = totals[:, :hid] / ACCUM
     grad_outw = totals[:, hid:] / ACCUM
 
@@ -125,18 +131,32 @@
     return (grad_tiles, grad_in, grad_outw)
 
 
+def x_width(mesh):
+    group = mesh.devices[0, :, 0]
+    try:
+        return len({d.coords[0] for d in group})
+    except (AttributeError, TypeError, IndexError):
+        return 4
+
+
 def solution(mesh):
+    dp, fsdp, llm = mesh.devices.shape
+    width = x_width(mesh)
+    split = jax.sharding.Mesh(
+        mesh.devices.reshape(dp, fsdp // width, width, llm), ("dp", "fy", "fx", "llm")
+    )
+    rows = ("dp", "fy", "fx")
     in_specs = (
-        P(("dp", "fsdp"), None),
-        P(("dp", "fsdp"), None),
-        P(("dp", "fsdp"), None),
-        P(("dp", "fsdp"), None),
-        P(("dp", "fsdp")),
+        P(rows, None),
+        P(rows, None),
+        P(rows, None),
+        P(rows, None),
+        P(rows),
         P(),
         P(),
         P(),
-        P("fsdp", "llm"),
-        P("fsdp", "llm"),
+        P(("fy", "fx"), "llm"),
+        P(("fy", "fx"), "llm"),
     )
-    out_specs = (P(("dp", "fsdp"), "llm"), P(("dp", "fsdp"), "llm"), P(("dp", "fsdp"), "llm"))
-    return jax.shard_map(body, mesh=mesh, in_specs=in_specs, out_specs=out_specs, check_vma=False)
+    out_specs = (P(rows, "llm"), P(rows, "llm"), P(rows, "llm"))
+    return jax.shard_map(body, mesh=split, in_specs=in_specs, out_specs=out_specs, check_vma=False)

time: 178 us -> 160 us (0.90)
  the two profiles are of different devices: /device:TPU:80 before, /device:TPU:64 now
where the time goes in v3:
time: 160 us; the launch traced here: 159 us
  waiting for transfers between devices  55.6 us (35%)
  starting transfers between devices  37.7 us (24%)
  blocking collectives  25.3 us (16%)
  other arithmetic  15.3 us (10%)
  local copies, waits for them, and re-layouts  12.4 us (8%)
  matrix products  11.3 us (7%)
  between operations  1.67 us (1%)
    all_to_all x1, blocking collectives, body(): y_block = lax.all_to_all(y_tiled, 'fy', split_axis=0, concat_axis=0)  25.3 us
    all_to_all x1, starting transfers between devices, body(): lax.all_to_all(out_half, 'dp', split_axis=0, concat_axis=0, tiled=True)  18.4 us
    all_to_all x1, waiting for transfers between devices, body(): lax.all_to_all(terms, 'fx', split_axis=1, concat_axis=1, tiled=True)  17.5 us
    all_to_all x1, waiting for transfers between devices, body(): lax.all_to_all(out_half, 'dp', split_axis=0, concat_axis=0, tiled=True)  15.8 us
    all_to_all x1, waiting for transfers between devices, body(): lax.all_to_all(x_sums, 'fy', split_axis=0, concat_axis=0, tiled=True)  12.6 us
    all_to_all x1, waiting for transfers between devices, body(): lax.all_to_all(x_tiled, 'fx', split_axis=1, concat_axis=1, tiled=True)  8.34 us
    conv_general_dilated x2, matrix products, depthwise(): lax.conv_general_dilated(images, kernel[:, :, None, :], (1, 1), 'SAME', d...  7.21 us
    all_to_all x1, starting transfers between devices, body(): lax.all_to_all(x_sums, 'fy', split_axis=0, concat_axis=0, tiled=True)  5.36 us
  transfers between devices with their start and end apart: 7, of which 5 were waited for; matrix products, arithmetic and copies ran while one was open for 15% of the time, Pallas kernels for 0%

profile of v3, /device:TPU:64, one launch (start us, length us, event | category | flops | bytes accessed | tf_op | source)
XLA Modules:
  0.0 159.2 jit_solution(1803567126326054938)
XLA Ops:
  0.6 0.7 fusion.21
  3.2 1.3 reduce.6
  4.9 1.2 gather_fusion
  6.8 0.8 dynamic-slice_select_fusion
  7.6 18.4 %all-to-all-start = ((bf16[16,16,384]{2,1,0:T(8,128)(2,1)}), bf16[16,16,384]{2,1,0:T(8,128)(2,1)S(1)}, u32[]{:S(2)}, u32[]{:S(2)}) async-start(bf16[16,16,384]{2,1,0:T(8,128)(2,1)} %bitcast.8), calls=%async_computation | async-start | bytes 393216 | tf_op jit(solution)/shard_map/all_to_all | solution.py:58
  26.0 15.8 %all-to-all-done = bf16[16,16,384]{2,1,0:T(8,128)(2,1)S(1)} async-done(((bf16[16,16,384]{2,1,0:T(8,128)(2,1)}), bf16[16,16,384]{2,1,0:T(8,128)(2,1)S(1)}, u32[]{:S(2)}, u32[]{:S(2)}) %all-to-all-start) | async-done | bytes 196640 | tf_op jit(solution)/shard_map/all_to_all | solution.py:58
  41.8 25.3 %all_to_all.32 = bf16[8,24,1536]{2,1,0:T(8,128)(2,1)S(1)} all-to-all(bf16[8,24,1536]{2,1,0:T(8,128)(2,1)S(1)} %broadcast_in_dim.68), channel_id=1, replica_groups=mesh['dp'=16,'fy'=8,'fx'=4,'llm'=2] {'fy'}, dimensions={0} | all-to-all | bytes 1179648 | tf_op jit(solution)/shard_map/all_to_all | solution.py:69
  67.1 1.6 %broadcast_in_dim.69 = bf16[8,4,24,1536]{3,2,0,1:T(8,128)(2,1)} broadcast(bf16[8,24,1536]{2,1,0:T(8,128)(2,1)S(1)} %all_to_all.32), dimensions={0,2,3} | broadcast | bytes 2949120 | tf_op jit(solution)/shard_map/broadcast_in_dim | solution.py:70
  68.7 4.4 %all-to-all-start.2 = ((bf16[8,4,24,1536]{3,2,0,1:T(8,128)(2,1)}), bf16[8,4,24,1536]{3,2,0,1:T(8,128)(2,1)S(1)}, u32[]{:S(2)}, u32[]{:S(2)}) async-start(bf16[8,4,24,1536]{3,2,0,1:T(8,128)(2,1)} %broadcast_in_dim.69), calls=%async_computation.2 | async-start | bytes 4718592 | tf_op jit(solution)/shard_map/all_to_all | solution.py:71
  73.2 5.6 %fusion.27 = (f32[4,8,8]{0,2,1:T(8,128)S(1)}, f32[4,8,8,768]{3,0,2,1:T(4,128)}) fusion(f32[7,7,1,768]{3,1,0,2:T(8,128)S(1)} %bitcast.58, bf16[4,8,8,768]{3,2,1,0:T(8,128)(2,1)} %bitcast.66), kind=kOutput, calls=%fused_computation.71 | convolution fusion | flops 71565056 | bytes 1331200 | tf_op jit(solution)/shard_map/conv_general_dilated | solution.py:11
  79.1 2.2 %copy.65 = f32[4,8,8,768]{3,2,1,0:T(8,128)} copy(f32[4,8,8,768]{3,0,2,1:T(4,128)} %get-tuple-element.15) | data formatting | bytes 1572864 | tf_op jit(solution)/shard_map/conv_general_dilated | solution.py:11
  81.3 1.5 multiply_reduce_fusion
  83.8 1.9 %collective-permute-start = (bf16[256,384]{1,0:T(8,128)(2,1)S(1)}, bf16[256,384]{1,0:T(8,128)(2,1)}, u32[]{:S(2)}, u32[]{:S(2)}) collective-permute-start(bf16[256,384]{1,0:T(8,128)(2,1)S(1)} %bitcast_select_fusion), channel_id=1, source_target_pairs={{0,1},{1,0},{2,3},{3,2},{4,5},{5,4},{6,7},{7,6},{8,9},{9,8},{10,11... | collective-permute-start | bytes 589832 | tf_op jit(solution)/shard_map/ppermute | solution.py:61
  85.7 2.4 %fusion.18 = (bf16[768,256]{0,1:T(8,128)(2,1)}, f32[256,768]{1,0:T(8,128)}) fusion(f32[768]{0:T(1024)S(1)} %copy-done.11, f32[256]{0:T(256)S(1)} %rsqrt.12, f32[256]{0:T(256)S(1)} %div.32, f32[4,8,8,768]{3,2,1,0:T(8,128)} %copy.65), kind=kLoop, calls=%fused_computation.42 | loop fusion | flops 786432 | bytes 1971200 | tf_op jit(solution)/shard_map/dot_general | solution.py:92
  88.1 1.9 %copy.69 = bf16[768,256]{1,0:T(8,128)(2,1)} copy(bf16[768,256]{0,1:T(8,128)(2,1)} %get-tuple-element.5) | data formatting | bytes 786432 | tf_op jit(solution)/shard_map/dot_general | solution.py:92
  90.0 1.7 %broadcast_select_fusion.2 = (bf16[256,384]{1,0:T(8,128)(2,1)S(1)}, bf16[256,384]{1,0:T(8,128)(2,1)}) fusion(bf16[256,384]{1,0:T(8,128)(2,1)} %collective-permute-done, pred[]{:T(512)S(6)} %eq.2, bf16[16,16,384]{2,1,0:T(8,128)(2,1)S(1)} %all-to-all-done, pred[256]{0:T(512)(128)(4,1)S(1)} %fusion.20), kind=kLoop, calls=%fused_computation.40 | loop fusion | flops 294912 | bytes 786689 | tf_op jit(solution)/shard_map/jit(_where)/select_n | solution.py:62
  91.7 8.3 %all-to-all-done.2 = bf16[8,4,24,1536]{3,2,0,1:T(8,128)(2,1)S(1)} async-done(((bf16[8,4,24,1536]{3,2,0,1:T(8,128)(2,1)}), bf16[8,4,24,1536]{3,2,0,1:T(8,128)(2,1)S(1)}, u32[]{:S(2)}, u32[]{:S(2)}) %all-to-all-start.2) | async-done | bytes 2359328 | tf_op jit(solution)/shard_map/all_to_all | solution.py:71
  100.3 0.9 copy-done.2
  104.1 1.6 %copy.70 = bf16[8,4,24,1536]{3,2,0,1:T(8,128)(2,1)} copy(bf16[8,4,24,1536]{3,2,1,0:T(8,128)(2,1)S(1)} %pad_maximum_fusion) | data formatting | bytes 4718592 | tf_op jit(solution)/shard_map/concatenate | solution.py:98
  105.8 3.6 %all-to-all-start.3 = ((bf16[8,4,24,1536]{3,2,0,1:T(8,128)(2,1)}), bf16[8,4,24,1536]{3,2,0,1:T(8,128)(2,1)S(1)}, u32[]{:S(2)}, u32[]{:S(2)}) async-start(bf16[8,4,24,1536]{3,2,0,1:T(8,128)(2,1)} %copy.70), calls=%async_computation.3 | async-start | bytes 4718592 | tf_op jit(solution)/shard_map/all_to_all | solution.py:100
  109.4 2.0 %fusion.2 = f32[256,768]{1,0:T(8,128)S(1)} fusion(bf16[256,768]{1,0:T(8,128)(2,1)} %copy-done.4, bf16[768,1536]{1,0:T(8,128)(2,1)} %bitcast.51), kind=kOutput, calls=%fused_computation.10 | convolution fusion | flops 301989888 | bytes 2359296 | tf_op jit(solution)/shard_map/dot_general | solution.py:107
  111.4 1.9 %collective-permute-start.1 = (bf16[256,384]{1,0:T(8,128)(2,1)S(1)}, bf16[256,384]{1,0:T(8,128)(2,1)S(1)}, u32[]{:S(2)}, u32[]{:S(2)}) collective-permute-start(bf16[256,384]{1,0:T(8,128)(2,1)S(1)} %select_convert_fusion), channel_id=1, source_target_pairs={{0,1},{1,0},{2,3},{3,2},{4,5},{5,4},{6,7},{7,6},{8,9},{9,8},{10,11... | collective-permute-start | bytes 589832 | tf_op jit(solution)/shard_map/ppermute | solution.py:114
  113.5 1.3 collective-permute-done.1
  114.8 0.8 fusion.25
  115.6 2.0 %collective-permute-start.2 = (f32[256,2]{0,1:T(2,128)S(1)}, f32[256,2]{0,1:T(2,128)S(1)}, u32[]{:S(2)}, u32[]{:S(2)}) collective-permute-start(f32[256,2]{0,1:T(2,128)S(1)} %pad_maximum_fusion.2), channel_id=1, source_target_pairs={{0,1},{1,0},{2,3},{3,2},{4,5},{5,4},{6,7},{7,6},{8,9},{9,8},{10,11... | collective-permute-start | bytes 6152 | tf_op jit(solution)/shard_map/ppermute | solution.py:122
  117.8 17.5 %all-to-all-done.3 = bf16[8,4,24,1536]{3,2,0,1:T(8,128)(2,1)S(1)} async-done(((bf16[8,4,24,1536]{3,2,0,1:T(8,128)(2,1)}), bf16[8,4,24,1536]{3,2,0,1:T(8,128)(2,1)S(1)}, u32[]{:S(2)}, u32[]{:S(2)}) %all-to-all-start.3) | async-done | bytes 2359328 | tf_op jit(solution)/shard_map/all_to_all | solution.py:100
  135.3 1.3 reduce_sum.61
  136.7 5.4 %all-to-all-start.4 = ((bf16[8,24,1536]{2,1,0:T(8,128)(2,1)}), bf16[8,24,1536]{2,1,0:T(8,128)(2,1)S(1)}, u32[]{:S(2)}, u32[]{:S(2)}) async-start(bf16[8,24,1536]{2,1,0:T(8,128)(2,1)} %reduce_sum.61), calls=%async_computation.4 | async-start | bytes 1179648 | tf_op jit(solution)/shard_map/all_to_all | solution.py:102
  142.1 1.3 subtract_multiply_fusion
  143.4 1.6 %fusion.13 = f32[4,8,8,384]{3,0,2,1:T(4,128)S(1)} fusion(f32[4,8,8,384]{3,2,1,0:T(8,128)S(1)} %bitcast.52, f32[7,7,1,384]{3,1,0,2:T(8,128)S(1)} %bitcast.57), kind=kOutput, calls=%fused_computation.28 | convolution fusion | flops 35684352 | bytes 861696 | tf_op jit(solution)/shard_map/conv_general_dilated | solution.py:11
  145.0 0.8 fusion.12
  145.8 12.6 %all-to-all-done.4 = bf16[8,24,1536]{2,1,0:T(8,128)(2,1)S(1)} async-done(((bf16[8,24,1536]{2,1,0:T(8,128)(2,1)}), bf16[8,24,1536]{2,1,0:T(8,128)(2,1)S(1)}, u32[]{:S(2)}, u32[]{:S(2)}) %all-to-all-start.4) | async-done | bytes 589856 | tf_op jit(solution)/shard_map/all_to_all | solution.py:102
  (65 shorter events, 7.7 us)
Async XLA Ops:
  0.6 4.2 %copy-start = (bf16[512,768]{1,0:T(8,128)(2,1)S(1)}, bf16[512,768]{1,0:T(8,128)(2,1)}, u32[]{:S(2)}) copy-start(bf16[512,768]{1,0:T(8,128)(2,1)} %param.11) | copy-start | bytes 2359300
  4.9 21.1 %copy-start.9 = (bf16[24,768]{1,0:T(8,128)(2,1)S(1)}, bf16[24,768]{1,0:T(8,128)(2,1)}, u32[]{:S(2)}) copy-start(bf16[24,768]{1,0:T(8,128)(2,1)} %param.19) | copy-start | bytes 110596
  4.9 21.1 %copy-start.10 = (bf16[24,768]{1,0:T(8,128)(2,1)S(1)}, bf16[24,768]{1,0:T(8,128)(2,1)}, u32[]{:S(2)}) copy-start(bf16[24,768]{1,0:T(8,128)(2,1)} %param.18) | copy-start | bytes 110596
  7.6 34.2 %all-to-all-start = ((bf16[16,16,384]{2,1,0:T(8,128)(2,1)}), bf16[16,16,384]{2,1,0:T(8,128)(2,1)S(1)}, u32[]{:S(2)}, u32[]{:S(2)}) async-start(bf16[16,16,384]{2,1,0:T(8,128)(2,1)} %bitcast.8), calls=%async_computation | async-start | bytes 393216 | tf_op jit(solution)/shard_map/all_to_all | solution.py:58
  68.7 4.4 %copy-start.7 = (f32[7,7,768]{2,1,0:T(8,128)S(1)}, f32[7,7,768]{2,1,0:T(8,128)}, u32[]{:S(2)}) copy-start(f32[7,7,768]{2,1,0:T(8,128)} %param.15) | copy-start | bytes 451588
  68.7 31.3 %all-to-all-start.2 = ((bf16[8,4,24,1536]{3,2,0,1:T(8,128)(2,1)}), bf16[8,4,24,1536]{3,2,0,1:T(8,128)(2,1)S(1)}, u32[]{:S(2)}, u32[]{:S(2)}) async-start(bf16[8,4,24,1536]{3,2,0,1:T(8,128)(2,1)} %broadcast_in_dim.69), calls=%async_computation.2 | async-start | bytes 4718592 | tf_op jit(solution)/shard_map/all_to_all | solution.py:71
  73.2 12.5 %copy-start.11 = (f32[768]{0:T(1024)S(1)}, f32[768]{0:T(1024)}, u32[]{:S(2)}) copy-start(f32[768]{0:T(1024)} %param.16) | copy-start | bytes 9220
  83.8 6.2 %collective-permute-start = (bf16[256,384]{1,0:T(8,128)(2,1)S(1)}, bf16[256,384]{1,0:T(8,128)(2,1)}, u32[]{:S(2)}, u32[]{:S(2)}) collective-permute-start(bf16[256,384]{1,0:T(8,128)(2,1)S(1)} %bitcast_select_fusion), channel_id=1, source_target_pairs={{0,1},{1,0},{2,3},{3,2},{4,5},{5,4},{6,7},{7,6},{8,9},{9,8},{10,11... | collective-permute-start | bytes 589832 | tf_op jit(solution)/shard_map/ppermute | solution.py:61
  100.1 1.1 copy-start.2
  100.3 2.0 %copy-start.1 = (bf16[8,4,24,1536]{3,2,1,0:T(8,128)(2,1)}, bf16[8,4,24,1536]{3,2,1,0:T(8,128)(2,1)S(1)}, u32[]{:S(2)}) copy-start(bf16[8,4,24,1536]{3,2,1,0:T(8,128)(2,1)S(1)} %copy.64) | copy-start | bytes 7077892
  100.3 1.4 copy-start.6
  100.3 1.4 copy-start.12
  102.3 1.6 %copy-start.4 = (bf16[256,768]{1,0:T(8,128)(2,1)}, bf16[256,768]{1,0:T(8,128)(2,1)S(1)}, u32[]{:S(2)}) copy-start(bf16[256,768]{1,0:T(8,128)(2,1)S(1)} %fusion) | copy-start | bytes 1179652
  102.3 1.1 copy-start.5
  105.8 29.6 %all-to-all-start.3 = ((bf16[8,4,24,1536]{3,2,0,1:T(8,128)(2,1)}), bf16[8,4,24,1536]{3,2,0,1:T(8,128)(2,1)S(1)}, u32[]{:S(2)}, u32[]{:S(2)}) async-start(bf16[8,4,24,1536]{3,2,0,1:T(8,128)(2,1)} %copy.70), calls=%async_computation.3 | async-start | bytes 4718592 | tf_op jit(solution)/shard_map/all_to_all | solution.py:100
  109.4 5.4 %copy-start.3 = (f32[256,768]{1,0:T(8,128)S(1)}, f32[256,768]{1,0:T(8,128)}, u32[]{:S(2)}) copy-start(f32[256,768]{1,0:T(8,128)} %get-tuple-element.6) | copy-start | bytes 2359300
  109.4 8.3 %copy-start.8 = (f32[7,7,768]{2,1,0:T(8,128)S(1)}, f32[7,7,768]{2,1,0:T(8,128)}, u32[]{:S(2)}) copy-start(f32[7,7,768]{2,1,0:T(8,128)} %param.15) | copy-start | bytes 451588
  111.4 3.3 %collective-permute-start.1 = (bf16[256,384]{1,0:T(8,128)(2,1)S(1)}, bf16[256,384]{1,0:T(8,128)(2,1)S(1)}, u32[]{:S(2)}, u32[]{:S(2)}) collective-permute-start(bf16[256,384]{1,0:T(8,128)(2,1)S(1)} %select_convert_fusion), channel_id=1, source_target_pairs={{0,1},{1,0},{2,3},{3,2},{4,5},{5,4},{6,7},{7,6},{8,9},{9,8},{10,11... | collective-permute-start | bytes 589832 | tf_op jit(solution)/shard_map/ppermute | solution.py:114
  115.6 26.4 %collective-permute-start.2 = (f32[256,2]{0,1:T(2,128)S(1)}, f32[256,2]{0,1:T(2,128)S(1)}, u32[]{:S(2)}, u32[]{:S(2)}) collective-permute-start(f32[256,2]{0,1:T(2,128)S(1)} %pad_maximum_fusion.2), channel_id=1, source_target_pairs={{0,1},{1,0},{2,3},{3,2},{4,5},{5,4},{6,7},{7,6},{8,9},{9,8},{10,11... | collective-permute-start | bytes 6152 | tf_op jit(solution)/shard_map/ppermute | solution.py:122
  136.7 21.8 %all-to-all-start.4 = ((bf16[8,24,1536]{2,1,0:T(8,128)(2,1)}), bf16[8,24,1536]{2,1,0:T(8,128)(2,1)S(1)}, u32[]{:S(2)}, u32[]{:S(2)}) async-start(bf16[8,24,1536]{2,1,0:T(8,128)(2,1)} %reduce_sum.61), calls=%async_computation.4 | async-start | bytes 1179648 | tf_op jit(solution)/shard_map/all_to_all | solution.py:102

commit v4 on v3

--- a/solution.py
+++ b/solution.py
@@ -65,8 +65,7 @@
 
     hid = weight_in.shape[1]
     both = jnp.concatenate([weight_in, weight_out], axis=1)
-    y_tiled = jnp.broadcast_to(both[None], (height,) + both.shape)
-    y_block = lax.all_to_all(y_tiled, "fy", split_axis=0, concat_axis=0)
+    y_block = lax.all_gather(both, "fy", axis=0)
     x_tiled = jnp.broadcast_to(y_block[:, None], (height, width) + both.shape)
     both_full = lax.all_to_all(x_tiled, "fx", split_axis=1, concat_axis=1, tiled=True).reshape(
         shards * both.shape[0], both.shape[1]

time: 160 us -> 141 us (0.88)
  waiting for transfers between devices: 55.6 us -> 34.7 us
  blocking collectives: 25.3 us -> 27.1 us
    all_gather x0 -> x1, blocking collectives: none -> 27.1 us  [body(): y_block = lax.all_gather(both, 'fy', axis=0)]
    all_to_all x1 -> x0, blocking collectives: 25.3 us -> none  [body(): y_block = lax.all_to_all(y_tiled, 'fy', split_axis=0, concat_axis=0)]
    all_to_all x1, waiting for transfers between devices: 15.8 us -> 0.01 us  [body(): lax.all_to_all(out_half, 'dp', split_axis=0, concat_axis=0, tiled=True)]
    all_to_all x1, waiting for transfers between devices: 8.34 us -> 4.87 us  [body(): lax.all_to_all(x_tiled, 'fx', split_axis=1, concat_axis=1, tiled=True)]
    all_to_all x1, waiting for transfers between devices: 12.6 us -> 10.9 us  [body(): lax.all_to_all(x_sums, 'fy', split_axis=0, concat_axis=0, tiled=True)]
  transfers between devices with their start and end apart: 7 -> 7, of which waited for: 5 -> 4; matrix products, arithmetic and copies ran while one was open for 15% -> 17% of each run, Pallas kernels for 0% -> 0%
where the time goes in v4:
time: 141 us; the launch traced here: 140 us
  starting transfers between devices  37.8 us (27%)
  waiting for transfers between devices  34.7 us (25%)
  blocking collectives  27.1 us (19%)
  other arithmetic  15.3 us (11%)
  local copies, waits for them, and re-layouts  12.3 us (9%)
  matrix products  11.3 us (8%)
  between operations  1.67 us (1%)
    all_gather x1, blocking collectives, body(): y_block = lax.all_gather(both, 'fy', axis=0)  27.1 us
    all_to_all x1, starting transfers between devices, body(): lax.all_to_all(out_half, 'dp', split_axis=0, concat_axis=0, tiled=True)  18.4 us
    all_to_all x1, waiting for transfers between devices, body(): lax.all_to_all(terms, 'fx', split_axis=1, concat_axis=1, tiled=True)  17.7 us
    all_to_all x1, waiting for transfers between devices, body(): lax.all_to_all(x_sums, 'fy', split_axis=0, concat_axis=0, tiled=True)  10.9 us
    conv_general_dilated x2, matrix products, depthwise(): lax.conv_general_dilated(images, kernel[:, :, None, :], (1, 1), 'SAME', d...  7.21 us
    all_to_all x1, starting transfers between devices, body(): lax.all_to_all(x_sums, 'fy', split_axis=0, concat_axis=0, tiled=True)  5.44 us
    all_to_all x1, waiting for transfers between devices, body(): lax.all_to_all(x_tiled, 'fx', split_axis=1, concat_axis=1, tiled=True)  4.87 us
    all_to_all x1, starting transfers between devices, body(): lax.all_to_all(x_tiled, 'fx', split_axis=1, concat_axis=1, tiled=True)  4.42 us
  transfers between devices with their start and end apart: 7, of which 4 were waited for; matrix products, arithmetic and copies ran while one was open for 17% of the time, Pallas kernels for 0%

profile of v4, /device:TPU:64, one launch (start us, length us, event | category | flops | bytes accessed | tf_op | source)
XLA Modules:
  0.0 140.2 jit_solution(11639083253575791596)
XLA Ops:
  0.6 0.7 fusion.21
  2.0 0.7 compare_select_fusion.1
  3.2 1.3 reduce.6
  4.9 1.2 gather_fusion
  6.8 0.8 dynamic-slice_select_fusion
  7.6 18.4 %all-to-all-start = ((bf16[16,16,384]{2,1,0:T(8,128)(2,1)}), bf16[16,16,384]{2,1,0:T(8,128)(2,1)S(1)}, u32[]{:S(2)}, u32[]{:S(2)}) async-start(bf16[16,16,384]{2,1,0:T(8,128)(2,1)} %bitcast.8), calls=%async_computation | async-start | bytes 393216 | tf_op jit(solution)/shard_map/all_to_all | solution.py:58
  26.0 27.1 %all-gather = bf16[192,1536]{1,0:T(8,128)(2,1)S(1)} all-gather(bf16[24,1536]{1,0:T(8,128)(2,1)S(1)} %pad_maximum_fusion.1), channel_id=2, replica_groups=mesh['dp'=16,'fy'=8,'fx'=4,'llm'=2] {'fy'}, dimensions={0}, use_global_device_ids=true | all-gather | bytes 663552 | tf_op jit(solution)/shard_map/all_gather | solution.py:68
  53.1 1.6 %broadcast_in_dim.62 = bf16[8,4,24,1536]{3,2,0,1:T(8,128)(2,1)} broadcast(bf16[8,24,1536]{2,1,0:T(8,128)(2,1)S(1)} %bitcast.53), dimensions={0,2,3} | broadcast | bytes 2949120 | tf_op jit(solution)/shard_map/broadcast_in_dim | solution.py:69
  54.8 4.4 %all-to-all-start.1 = ((bf16[8,4,24,1536]{3,2,0,1:T(8,128)(2,1)}), bf16[8,4,24,1536]{3,2,0,1:T(8,128)(2,1)S(1)}, u32[]{:S(2)}, u32[]{:S(2)}) async-start(bf16[8,4,24,1536]{3,2,0,1:T(8,128)(2,1)} %broadcast_in_dim.62), calls=%async_computation.1 | async-start | bytes 4718592 | tf_op jit(solution)/shard_map/all_to_all | solution.py:70
  59.2 5.6 %fusion.27 = (f32[4,8,8]{0,2,1:T(8,128)S(1)}, f32[4,8,8,768]{3,0,2,1:T(4,128)}) fusion(f32[7,7,1,768]{3,1,0,2:T(8,128)S(1)} %bitcast.60, bf16[4,8,8,768]{3,2,1,0:T(8,128)(2,1)} %bitcast.68), kind=kOutput, calls=%fused_computation.71 | convolution fusion | flops 71565056 | bytes 1331200 | tf_op jit(solution)/shard_map/conv_general_dilated | solution.py:11
  65.1 2.2 %copy.65 = f32[4,8,8,768]{3,2,1,0:T(8,128)} copy(f32[4,8,8,768]{3,0,2,1:T(4,128)} %get-tuple-element.15) | data formatting | bytes 1572864 | tf_op jit(solution)/shard_map/conv_general_dilated | solution.py:11
  67.3 1.5 %multiply_reduce_fusion = f32[4,8,8]{0,2,1:T(8,128)S(1)} fusion(f32[4,8,8,768]{3,0,2,1:T(4,128)} %get-tuple-element.15, f32[4,8,8]{0,2,1:T(8,128)S(1)} %copy.62), kind=kLoop, calls=%fused_computation.24 | loop fusion | flops 589568 | bytes 788480 | tf_op jit(solution)/shard_map/reduce_sum | solution.py:81
  69.8 1.9 %collective-permute-start = (bf16[256,384]{1,0:T(8,128)(2,1)S(1)}, bf16[256,384]{1,0:T(8,128)(2,1)}, u32[]{:S(2)}, u32[]{:S(2)}) collective-permute-start(bf16[256,384]{1,0:T(8,128)(2,1)S(1)} %bitcast_select_fusion), channel_id=1, source_target_pairs={{0,1},{1,0},{2,3},{3,2},{4,5},{5,4},{6,7},{7,6},{8,9},{9,8},{10,11... | collective-permute-start | bytes 589832 | tf_op jit(solution)/shard_map/ppermute | solution.py:61
  71.7 2.4 %fusion.18 = (bf16[768,256]{0,1:T(8,128)(2,1)}, f32[256,768]{1,0:T(8,128)}) fusion(f32[768]{0:T(1024)S(1)} %copy-done.11, f32[256]{0:T(256)S(1)} %rsqrt.12, f32[256]{0:T(256)S(1)} %div.32, f32[4,8,8,768]{3,2,1,0:T(8,128)} %copy.65), kind=kLoop, calls=%fused_computation.42 | loop fusion | flops 786432 | bytes 1971200 | tf_op jit(solution)/shard_map/dot_general | solution.py:91
  74.1 1.9 %copy.69 = bf16[768,256]{1,0:T(8,128)(2,1)} copy(bf16[768,256]{0,1:T(8,128)(2,1)} %get-tuple-element.5) | data formatting | bytes 786432 | tf_op jit(solution)/shard_map/dot_general | solution.py:91
  76.0 1.7 %broadcast_select_fusion.2 = (bf16[256,384]{1,0:T(8,128)(2,1)S(1)}, bf16[256,384]{1,0:T(8,128)(2,1)}) fusion(bf16[256,384]{1,0:T(8,128)(2,1)} %collective-permute-done, pred[]{:T(512)S(6)} %eq.2, bf16[16,16,384]{2,1,0:T(8,128)(2,1)S(1)} %all-to-all-done, pred[256]{0:T(512)(128)(4,1)S(1)} %fusion.20), kind=kLoop, calls=%fused_computation.40 | loop fusion | flops 294912 | bytes 786689 | tf_op jit(solution)/shard_map/jit(_where)/select_n | solution.py:62
  77.8 4.9 %all-to-all-done.1 = bf16[8,4,24,1536]{3,2,0,1:T(8,128)(2,1)S(1)} async-done(((bf16[8,4,24,1536]{3,2,0,1:T(8,128)(2,1)}), bf16[8,4,24,1536]{3,2,0,1:T(8,128)(2,1)S(1)}, u32[]{:S(2)}, u32[]{:S(2)}) %all-to-all-start.1) | async-done | bytes 2359328 | tf_op jit(solution)/shard_map/all_to_all | solution.py:70
  82.9 0.9 copy-done.2
  86.7 1.6 %copy.70 = bf16[8,4,24,1536]{3,2,0,1:T(8,128)(2,1)} copy(bf16[8,4,24,1536]{3,2,1,0:T(8,128)(2,1)S(1)} %pad_maximum_fusion) | data formatting | bytes 4718592 | tf_op jit(solution)/shard_map/concatenate | solution.py:97
  88.3 3.6 %all-to-all-start.2 = ((bf16[8,4,24,1536]{3,2,0,1:T(8,128)(2,1)}), bf16[8,4,24,1536]{3,2,0,1:T(8,128)(2,1)S(1)}, u32[]{:S(2)}, u32[]{:S(2)}) async-start(bf16[8,4,24,1536]{3,2,0,1:T(8,128)(2,1)} %copy.70), calls=%async_computation.2 | async-start | bytes 4718592 | tf_op jit(solution)/shard_map/all_to_all | solution.py:99
  92.0 2.0 %fusion.2 = f32[256,768]{1,0:T(8,128)S(1)} fusion(bf16[256,768]{1,0:T(8,128)(2,1)} %copy-done.4, bf16[768,1536]{1,0:T(8,128)(2,1)} %bitcast.52), kind=kOutput, calls=%fused_computation.10 | convolution fusion | flops 301989888 | bytes 2359296 | tf_op jit(solution)/shard_map/dot_general | solution.py:106
  94.0 1.9 %collective-permute-start.1 = (bf16[256,384]{1,0:T(8,128)(2,1)S(1)}, bf16[256,384]{1,0:T(8,128)(2,1)S(1)}, u32[]{:S(2)}, u32[]{:S(2)}) collective-permute-start(bf16[256,384]{1,0:T(8,128)(2,1)S(1)} %select_convert_fusion), channel_id=1, source_target_pairs={{0,1},{1,0},{2,3},{3,2},{4,5},{5,4},{6,7},{7,6},{8,9},{9,8},{10,11... | collective-permute-start | bytes 589832 | tf_op jit(solution)/shard_map/ppermute | solution.py:113
  96.0 1.3 collective-permute-done.1
  97.3 0.8 fusion.25
  98.1 2.0 %collective-permute-start.2 = (f32[256,2]{0,1:T(2,128)S(1)}, f32[256,2]{0,1:T(2,128)S(1)}, u32[]{:S(2)}, u32[]{:S(2)}) collective-permute-start(f32[256,2]{0,1:T(2,128)S(1)} %pad_maximum_fusion.2), channel_id=1, source_target_pairs={{0,1},{1,0},{2,3},{3,2},{4,5},{5,4},{6,7},{7,6},{8,9},{9,8},{10,11... | collective-permute-start | bytes 6152 | tf_op jit(solution)/shard_map/ppermute | solution.py:121
  100.4 17.7 %all-to-all-done.2 = bf16[8,4,24,1536]{3,2,0,1:T(8,128)(2,1)S(1)} async-done(((bf16[8,4,24,1536]{3,2,0,1:T(8,128)(2,1)}), bf16[8,4,24,1536]{3,2,0,1:T(8,128)(2,1)S(1)}, u32[]{:S(2)}, u32[]{:S(2)}) %all-to-all-start.2) | async-done | bytes 2359328 | tf_op jit(solution)/shard_map/all_to_all | solution.py:99
  118.0 1.3 reduce_sum.61
  119.4 5.4 %all-to-all-start.3 = ((bf16[8,24,1536]{2,1,0:T(8,128)(2,1)}), bf16[8,24,1536]{2,1,0:T(8,128)(2,1)S(1)}, u32[]{:S(2)}, u32[]{:S(2)}) async-start(bf16[8,24,1536]{2,1,0:T(8,128)(2,1)} %reduce_sum.61), calls=%async_computation.3 | async-start | bytes 1179648 | tf_op jit(solution)/shard_map/all_to_all | solution.py:101
  124.8 1.3 subtract_multiply_fusion
  126.1 1.6 %fusion.13 = f32[4,8,8,384]{3,0,2,1:T(4,128)S(1)} fusion(f32[4,8,8,384]{3,2,1,0:T(8,128)S(1)} %bitcast.54, f32[7,7,1,384]{3,1,0,2:T(8,128)S(1)} %bitcast.59), kind=kOutput, calls=%fused_computation.28 | convolution fusion | flops 35684352 | bytes 861696 | tf_op jit(solution)/shard_map/conv_general_dilated | solution.py:11
  127.8 0.8 fusion.12
  128.6 10.9 %all-to-all-done.3 = bf16[8,24,1536]{2,1,0:T(8,128)(2,1)S(1)} async-done(((bf16[8,24,1536]{2,1,0:T(8,128)(2,1)}), bf16[8,24,1536]{2,1,0:T(8,128)(2,1)S(1)}, u32[]{:S(2)}, u32[]{:S(2)}) %all-to-all-start.3) | async-done | bytes 589856 | tf_op jit(solution)/shard_map/all_to_all | solution.py:101
  (64 shorter events, 6.9 us)
Async XLA Ops:
  0.6 4.2 %copy-start = (bf16[512,768]{1,0:T(8,128)(2,1)S(1)}, bf16[512,768]{1,0:T(8,128)(2,1)}, u32[]{:S(2)}) copy-start(bf16[512,768]{1,0:T(8,128)(2,1)} %param.11) | copy-start | bytes 2359300
  4.9 21.1 %copy-start.9 = (bf16[24,768]{1,0:T(8,128)(2,1)S(1)}, bf16[24,768]{1,0:T(8,128)(2,1)}, u32[]{:S(2)}) copy-start(bf16[24,768]{1,0:T(8,128)(2,1)} %param.19) | copy-start | bytes 110596
  4.9 21.1 %copy-start.10 = (bf16[24,768]{1,0:T(8,128)(2,1)S(1)}, bf16[24,768]{1,0:T(8,128)(2,1)}, u32[]{:S(2)}) copy-start(bf16[24,768]{1,0:T(8,128)(2,1)} %param.18) | copy-start | bytes 110596
  7.6 45.6 %all-to-all-start = ((bf16[16,16,384]{2,1,0:T(8,128)(2,1)}), bf16[16,16,384]{2,1,0:T(8,128)(2,1)S(1)}, u32[]{:S(2)}, u32[]{:S(2)}) async-start(bf16[16,16,384]{2,1,0:T(8,128)(2,1)} %bitcast.8), calls=%async_computation | async-start | bytes 393216 | tf_op jit(solution)/shard_map/all_to_all | solution.py:58
  54.8 4.4 %copy-start.7 = (f32[7,7,768]{2,1,0:T(8,128)S(1)}, f32[7,7,768]{2,1,0:T(8,128)}, u32[]{:S(2)}) copy-start(f32[7,7,768]{2,1,0:T(8,128)} %param.15) | copy-start | bytes 451588
  54.8 27.9 %all-to-all-start.1 = ((bf16[8,4,24,1536]{3,2,0,1:T(8,128)(2,1)}), bf16[8,4,24,1536]{3,2,0,1:T(8,128)(2,1)S(1)}, u32[]{:S(2)}, u32[]{:S(2)}) async-start(bf16[8,4,24,1536]{3,2,0,1:T(8,128)(2,1)} %broadcast_in_dim.62), calls=%async_computation.1 | async-start | bytes 4718592 | tf_op jit(solution)/shard_map/all_to_all | solution.py:70
  59.2 12.5 %copy-start.11 = (f32[768]{0:T(1024)S(1)}, f32[768]{0:T(1024)}, u32[]{:S(2)}) copy-start(f32[768]{0:T(1024)} %param.16) | copy-start | bytes 9220
  69.8 6.2 %collective-permute-start = (bf16[256,384]{1,0:T(8,128)(2,1)S(1)}, bf16[256,384]{1,0:T(8,128)(2,1)}, u32[]{:S(2)}, u32[]{:S(2)}) collective-permute-start(bf16[256,384]{1,0:T(8,128)(2,1)S(1)} %bitcast_select_fusion), channel_id=1, source_target_pairs={{0,1},{1,0},{2,3},{3,2},{4,5},{5,4},{6,7},{7,6},{8,9},{9,8},{10,11... | collective-permute-start | bytes 589832 | tf_op jit(solution)/shard_map/ppermute | solution.py:61
  82.6 1.1 copy-start.2
  82.8 2.0 %copy-start.1 = (bf16[8,4,24,1536]{3,2,1,0:T(8,128)(2,1)}, bf16[8,4,24,1536]{3,2,1,0:T(8,128)(2,1)S(1)}, u32[]{:S(2)}) copy-start(bf16[8,4,24,1536]{3,2,1,0:T(8,128)(2,1)S(1)} %copy.64) | copy-start | bytes 7077892
  82.9 1.4 copy-start.6
  82.9 1.4 copy-start.12
  84.9 1.6 %copy-start.4 = (bf16[256,768]{1,0:T(8,128)(2,1)}, bf16[256,768]{1,0:T(8,128)(2,1)S(1)}, u32[]{:S(2)}) copy-start(bf16[256,768]{1,0:T(8,128)(2,1)S(1)} %fusion) | copy-start | bytes 1179652
  84.9 1.1 copy-start.5
  88.3 29.7 %all-to-all-start.2 = ((bf16[8,4,24,1536]{3,2,0,1:T(8,128)(2,1)}), bf16[8,4,24,1536]{3,2,0,1:T(8,128)(2,1)S(1)}, u32[]{:S(2)}, u32[]{:S(2)}) async-start(bf16[8,4,24,1536]{3,2,0,1:T(8,128)(2,1)} %copy.70), calls=%async_computation.2 | async-start | bytes 4718592 | tf_op jit(solution)/shard_map/all_to_all | solution.py:99
  91.9 5.4 %copy-start.3 = (f32[256,768]{1,0:T(8,128)S(1)}, f32[256,768]{1,0:T(8,128)}, u32[]{:S(2)}) copy-start(f32[256,768]{1,0:T(8,128)} %get-tuple-element.6) | copy-start | bytes 2359300
  91.9 8.3 %copy-start.8 = (f32[7,7,768]{2,1,0:T(8,128)S(1)}, f32[7,7,768]{2,1,0:T(8,128)}, u32[]{:S(2)}) copy-start(f32[7,7,768]{2,1,0:T(8,128)} %param.15) | copy-start | bytes 451588
  94.0 3.3 %collective-permute-start.1 = (bf16[256,384]{1,0:T(8,128)(2,1)S(1)}, bf16[256,384]{1,0:T(8,128)(2,1)S(1)}, u32[]{:S(2)}, u32[]{:S(2)}) collective-permute-start(bf16[256,384]{1,0:T(8,128)(2,1)S(1)} %select_convert_fusion), channel_id=1, source_target_pairs={{0,1},{1,0},{2,3},{3,2},{4,5},{5,4},{6,7},{7,6},{8,9},{9,8},{10,11... | collective-permute-start | bytes 589832 | tf_op jit(solution)/shard_map/ppermute | solution.py:113
  98.1 26.7 %collective-permute-start.2 = (f32[256,2]{0,1:T(2,128)S(1)}, f32[256,2]{0,1:T(2,128)S(1)}, u32[]{:S(2)}, u32[]{:S(2)}) collective-permute-start(f32[256,2]{0,1:T(2,128)S(1)} %pad_maximum_fusion.2), channel_id=1, source_target_pairs={{0,1},{1,0},{2,3},{3,2},{4,5},{5,4},{6,7},{7,6},{8,9},{9,8},{10,11... | collective-permute-start | bytes 6152 | tf_op jit(solution)/shard_map/ppermute | solution.py:121
  119.4 20.1 %all-to-all-start.3 = ((bf16[8,24,1536]{2,1,0:T(8,128)(2,1)}), bf16[8,24,1536]{2,1,0:T(8,128)(2,1)S(1)}, u32[]{:S(2)}, u32[]{:S(2)}) async-start(bf16[8,24,1536]{2,1,0:T(8,128)(2,1)} %reduce_sum.61), calls=%async_computation.3 | async-start | bytes 1179648 | tf_op jit(solution)/shard_map/all_to_all | solution.py:101

commit v5 on v4

--- a/solution.py
+++ b/solution.py
@@ -25,6 +25,12 @@
     return (hidden_in * cumulative, cumulative + hidden_in * density)
 
 
+def to_xy(values, height, width):
+    lead = values.shape[:-1]
+    grid = values.reshape(lead + (height, width, -1))
+    return jnp.swapaxes(grid, -3, -2).reshape(lead + (values.shape[-1],))
+
+
 SWAP = [(0, 1), (1, 0)]
 
 
@@ -50,11 +56,11 @@
     half_width = channels // lax.axis_size("llm")
     core_index = lax.axis_index("llm")
 
-    visual = jnp.take(grad_seq, visual_pos[0], axis=0)
-    outgoing = jnp.take(visual.reshape(groups, block_rows, channels), assign[0], axis=0).reshape(
-        row_count, channels
-    )
-    out_half = lax.dynamic_slice_in_dim(outgoing, core_index * half_width, half_width, 1)
+    source_rows = jnp.take(
+        visual_pos[0].reshape(groups, block_rows), assign[0], axis=0, mode="clip"
+    ).reshape(row_count)
+    seq_half = lax.dynamic_slice_in_dim(grad_seq, core_index * half_width, half_width, 1)
+    out_half = jnp.take(seq_half, source_rows, axis=0, mode="clip")
     arrived_half = lax.all_to_all(out_half, "dp", split_axis=0, concat_axis=0, tiled=True)
     present = jnp.arange(row_count) // (SIDE * SIDE) < tile_count[0]
     mine_half = jnp.where(present[:, None], arrived_half, jnp.zeros_like(arrived_half))
@@ -66,8 +72,8 @@
     hid = weight_in.shape[1]
     both = jnp.concatenate([weight_in, weight_out], axis=1)
     y_block = lax.all_gather(both, "fy", axis=0)
-    x_tiled = jnp.broadcast_to(y_block[:, None], (height, width) + both.shape)
-    both_full = lax.all_to_all(x_tiled, "fx", split_axis=1, concat_axis=1, tiled=True).reshape(
+    x_tiled = jnp.broadcast_to(y_block[None], (width,) + y_block.shape)
+    both_full = lax.all_to_all(x_tiled, "fx", split_axis=0, concat_axis=0, tiled=True).reshape(
         shards * both.shape[0], both.shape[1]
     )
     w_in_full = both_full[:, :hid]
@@ -81,10 +87,12 @@
     inv_std = lax.rsqrt(jnp.mean(centred * centred, axis=1, keepdims=True) + 1e-06)
     unit = centred * inv_std
     normed = (unit * norm_gain).astype(jnp.bfloat16)
+    normed = to_xy(normed, height, width)
     hidden_in = jnp.dot(normed, w_in_full, preferred_element_type=jnp.float32)
     activated, slope = gelu_parts(hidden_in)
     hidden = activated.astype(jnp.bfloat16)
     scaled = (grad_out.astype(jnp.float32) * layer_scale).astype(jnp.bfloat16)
+    scaled = to_xy(scaled, height, width)
     grad_hidden = jnp.dot(scaled, w_out_full, preferred_element_type=jnp.float32)
     grad_pre = (grad_hidden * slope).astype(jnp.bfloat16)
 
@@ -95,9 +103,9 @@
         scaled, hidden, (((0,), (0,)), ((), ())), preferred_element_type=jnp.float32
     )
     terms = jnp.concatenate([term_in, term_out], axis=1).astype(jnp.bfloat16)
-    terms = terms.reshape(height, width, channels // shards, 2 * hid)
-    x_parts = lax.all_to_all(terms, "fx", split_axis=1, concat_axis=1, tiled=True)
-    x_sums = jnp.sum(x_parts.astype(jnp.float32), axis=1).astype(jnp.bfloat16)
+    terms = terms.reshape(width, height, channels // shards, 2 * hid)
+    x_parts = lax.all_to_all(terms, "fx", split_axis=0, concat_axis=0, tiled=True)
+    x_sums = jnp.sum(x_parts.astype(jnp.float32), axis=0).astype(jnp.bfloat16)
     y_parts = lax.all_to_all(x_sums, "fy", split_axis=0, concat_axis=0, tiled=True)
     totals = jnp.sum(y_parts.astype(jnp.float32), axis=0)
     grad_in = totals[:, :hid] / ACCUM
@@ -106,6 +114,7 @@
     grad_part = lax.dot_general(
         grad_pre, w_in_full, (((1,), (1,)), ((), ())), preferred_element_type=jnp.float32
     )
+    grad_part = to_xy(grad_part, width, height)
     part_lo = grad_part[:, :half_width]
     part_hi = grad_part[:, half_width:]
     keep = jnp.where(core_index == 0, part_lo, part_hi)

time: 141 us -> 145 us (1.028)
  waiting for transfers between devices: 34.7 us -> 24.2 us
  local copies, waits for them, and re-layouts: 12.3 us -> 22 us
  other arithmetic: 15.3 us -> 17.3 us
  matrix products: 11.3 us -> 12.8 us
    all_to_all x2, waiting for transfers between devices: 22.5 us -> 13.2 us  [the longest x1 7.19 us: body(): lax.all_to_all(terms, 'fx', split_axis=0, concat_axis=0, tiled=True)]
    reshape x0 -> x1, local copies, waits for them, and re-layouts: none -> 6.82 us  [body(): mixed = depthwise(tile_rows.astype(jnp.float32).reshape(-1, SIDE, SIDE, c...]
    transpose x0 -> x2, other arithmetic: none -> 3.23 us  [to_xy(): return jnp.swapaxes(grid, -3, -2).reshape(lead + (values.shape[-1],))]
    unnamed x27 -> x37, local copies, waits for them, and re-layouts: 2 us -> 4.42 us
    dot_general x1 -> x0, other arithmetic: 2.39 us -> none  [body(): lax.dot_general(normed, grad_pre, (((0,), (0,)), ((), ())), preferred_ele...]
    select_n x4 -> x0, other arithmetic: 2.3 us -> none  [the longest x2 1.52 us: body(): jnp.take(visual.reshape(groups, block_rows, channels), assign[0], axis=0)]
    rev x1, local copies, waits for them, and re-layouts: 0.12 us -> 2.14 us  [body(): kernel_half[::-1, ::-1]]
    conv_general_dilated x2, local copies, waits for them, and re-layouts: 2.19 us -> 0.18 us  [depthwise(): lax.conv_general_dilated(images, kernel[:, :, None, :], (1, 1), 'SAME', d...]
  transfers between devices with their start and end apart: 7 -> 7, of which waited for: 4 -> 4; matrix products, arithmetic and copies ran while one was open for 17% -> 26% of each run, Pallas kernels for 0% -> 0%
where the time goes in v5:
time: 145 us; the launch traced here: 144 us
  starting transfers between devices  38.4 us (26%)
  blocking collectives  27.3 us (19%)
  waiting for transfers between devices  24.2 us (17%)
  local copies, waits for them, and re-layouts  22 us (15%)
  other arithmetic  17.3 us (12%)
  matrix products  12.8 us (9%)
  between operations  1.71 us (1%)
    all_gather x1, blocking collectives, body(): y_block = lax.all_gather(both, 'fy', axis=0)  27.3 us
    all_to_all x1, starting transfers between devices, body(): lax.all_to_all(out_half, 'dp', split_axis=0, concat_axis=0, tiled=True)  18.4 us
    all_to_all x1, waiting for transfers between devices, body(): lax.all_to_all(x_sums, 'fy', split_axis=0, concat_axis=0, tiled=True)  9.57 us
    all_to_all x1, waiting for transfers between devices, body(): lax.all_to_all(terms, 'fx', split_axis=0, concat_axis=0, tiled=True)  7.19 us
    reshape x1, local copies, waits for them, and re-layouts, body(): mixed = depthwise(tile_rows.astype(jnp.float32).reshape(-1, SIDE, SIDE, c...  6.82 us
    conv_general_dilated x2, matrix products, depthwise(): lax.conv_general_dilated(images, kernel[:, :, None, :], (1, 1), 'SAME', d...  6.4 us
    all_to_all x1, waiting for transfers between devices, body(): lax.all_to_all(x_tiled, 'fx', split_axis=0, concat_axis=0, tiled=True)  6.06 us
    all_to_all x1, starting transfers between devices, body(): lax.all_to_all(x_sums, 'fy', split_axis=0, concat_axis=0, tiled=True)  5.62 us
  transfers between devices with their start and end apart: 7, of which 4 were waited for; matrix products, arithmetic and copies ran while one was open for 26% of the time, Pallas kernels for 0%

profile of v5, /device:TPU:64, one launch (start us, length us, event | category | flops | bytes accessed | tf_op | source)
XLA Modules:
  0.0 143.8 jit_solution(12886939749054441064)
XLA Ops:
  1.2 1.3 reduce.6
  4.0 1.8 %gather_fusion.1 = bf16[256,384]{1,0:T(8,128)(2,1)} fusion(bf16[512,384]{1,0:T(8,128)(2,1)S(1)} %constant_dynamic-slice_fusion.1, s32[1024]{0:T(1024)S(1)} %pad_clamp_fusion), kind=kCustom, calls=%fused_computation.1 | custom fusion | bytes 394240 | tf_op jit(solution)/shard_map/jit(_take)/gather | solution.py:63
  5.8 18.4 %all-to-all-start = ((bf16[16,16,384]{2,1,0:T(8,128)(2,1)}), bf16[16,16,384]{2,1,0:T(8,128)(2,1)S(1)}, u32[]{:S(2)}, u32[]{:S(2)}) async-start(bf16[16,16,384]{2,1,0:T(8,128)(2,1)} %bitcast.2), calls=%async_computation | async-start | bytes 393216 | tf_op jit(solution)/shard_map/all_to_all | solution.py:64
  24.3 4.8 %fusion.30 = (f32[4,8,8]{0,2,1:T(8,128)S(1)}, f32[4,8,8,768]{3,0,2,1:T(4,128)S(1)}) fusion(f32[7,7,1,768]{3,1,0,2:T(8,128)S(1)} %bitcast.75, bf16[4,8,8,768]{3,2,1,0:T(8,128)(2,1)S(1)} %bitcast.83), kind=kOutput, calls=%fused_computation.67 | convolution fusion | flops 71565056 | bytes 1331200 | tf_op jit(solution)/shard_map/conv_general_dilated | solution.py:11
  29.2 27.3 %all-gather = bf16[192,1536]{1,0:T(8,128)(2,1)S(1)} all-gather(bf16[24,1536]{1,0:T(8,128)(2,1)S(1)} %pad_maximum_fusion.1), channel_id=2, replica_groups=mesh['dp'=16,'fy'=8,'fx'=4,'llm'=2] {'fy'}, dimensions={0}, use_global_device_ids=true | all-gather | bytes 663552 | tf_op jit(solution)/shard_map/all_gather | solution.py:74
  56.5 1.7 %broadcast_in_dim.42 = bf16[4,8,24,1536]{3,2,1,0:T(8,128)(2,1)} broadcast(bf16[8,24,1536]{2,1,0:T(8,128)(2,1)S(1)} %bitcast.68), dimensions={1,2,3} | broadcast | bytes 2949120 | tf_op jit(solution)/shard_map/broadcast_in_dim | solution.py:75
  58.2 4.5 %all-to-all-start.1 = ((bf16[4,8,24,1536]{3,2,1,0:T(8,128)(2,1)}), bf16[4,8,24,1536]{3,2,1,0:T(8,128)(2,1)}, u32[]{:S(2)}, u32[]{:S(2)}) async-start(bf16[4,8,24,1536]{3,2,1,0:T(8,128)(2,1)} %broadcast_in_dim.42), calls=%async_computation.1 | async-start | bytes 4718592 | tf_op jit(solution)/shard_map/all_to_all | solution.py:76
  64.3 6.8 %reshape.123 = f32[256,8,4,24]{3,2,1,0:T(4,128)} reshape(f32[4,8,8,768]{3,2,1,0:T(8,128)S(1)} %copy.91) | data formatting | bytes 1572864 | tf_op jit(solution)/shard_map/reshape | solution.py:84
  72.1 2.0 %collective-permute-start = (bf16[256,384]{1,0:T(8,128)(2,1)}, bf16[256,384]{1,0:T(8,128)(2,1)}, u32[]{:S(2)}, u32[]{:S(2)}) collective-permute-start(bf16[256,384]{1,0:T(8,128)(2,1)} %bitcast_select_fusion), channel_id=1, source_target_pairs={{0,1},{1,0},{2,3},{3,2},{4,5},{5,4},{6,7},{7,6},{8,9},{9,8},{10,11... | collective-permute-start | bytes 589832 | tf_op jit(solution)/shard_map/ppermute | solution.py:67
  74.1 3.1 %fusion = bf16[256,4,8,24]{3,1,2,0:T(4,128)(2,1)S(1)} fusion(f32[256,8,4,24]{3,2,1,0:T(4,128)} %reshape.123, f32[8,4,24]{2,1,0:T(4,128)S(1)} %mul.118, f32[256]{0:T(256)S(1)} %rsqrt.12, f32[256]{0:T(256)S(1)} %div.32), kind=kLoop, calls=%fused_computation.4 | loop fusion | flops 786432 | bytes 1184768 | tf_op jit(solution)/shard_map/transpose | solution.py:31
  77.3 1.5 %copy.92 = bf16[256,4,8,24]{0,3,2,1:T(8,128)(2,1)S(1)} copy(bf16[256,4,8,24]{3,1,2,0:T(4,128)(2,1)S(1)} %fusion) | data formatting | bytes 786432 | tf_op jit(solution)/shard_map/transpose | solution.py:31
  78.8 1.1 broadcast_select_fusion.1
  80.4 6.1 %all-to-all-done.1 = bf16[4,8,24,1536]{3,2,1,0:T(8,128)(2,1)} async-done(((bf16[4,8,24,1536]{3,2,1,0:T(8,128)(2,1)}), bf16[4,8,24,1536]{3,2,1,0:T(8,128)(2,1)}, u32[]{:S(2)}, u32[]{:S(2)}) %all-to-all-start.1) | async-done | bytes 2359328 | tf_op jit(solution)/shard_map/all_to_all | solution.py:76
  86.4 1.8 %fusion.5 = f32[256,768]{1,0:T(8,128)S(1)} fusion(bf16[256,768]{0,1:T(8,128)(2,1)S(1)} %bitcast.70, bf16[768,1536]{1,0:T(8,128)(2,1)} %bitcast.11), kind=kOutput, calls=%fused_computation.14 | convolution fusion | flops 301989888 | bytes 2359296 | tf_op jit(solution)/shard_map/dot_general | solution.py:91
  88.7 1.9 %fusion.1 = bf16[256,768]{1,0:T(8,128)(2,1)S(1)} fusion(bf16[256,768]{0,1:T(8,128)(2,1)S(1)} %bitcast.73, bf16[768,1536]{1,0:T(8,128)(2,1)} %bitcast.11, f32[256,768]{1,0:T(8,128)S(1)} %fusion.5), kind=kOutput, calls=%fused_computation.8 | convolution fusion | flops 303955968 | bytes 2752512 | tf_op jit(solution)/shard_map/dot_general | solution.py:96
  91.8 1.6 %pad_maximum_fusion = bf16[4,8,24,1536]{3,2,1,0:T(8,128)(2,1)} fusion(bf16[4,8,24,768]{3,2,1,0:T(8,128)(2,1)S(1)} %convolution_convert_fusion, bf16[4,8,24,768]{3,2,1,0:T(8,128)(2,1)S(1)} %convolution_convert_fusion.1), kind=kLoop, calls=%fused_computation.3 | loop fusion | flops 4718592 | bytes 4718592 | tf_op jit(solution)/shard_map/concatenate | solution.py:105
  93.5 3.8 %all-to-all-start.2 = ((bf16[4,8,24,1536]{3,2,1,0:T(8,128)(2,1)}), bf16[4,8,24,1536]{3,2,1,0:T(8,128)(2,1)S(1)}, u32[]{:S(2)}, u32[]{:S(2)}) async-start(bf16[4,8,24,1536]{3,2,1,0:T(8,128)(2,1)} %pad_maximum_fusion), calls=%async_computation.2 | async-start | bytes 4718592 | tf_op jit(solution)/shard_map/all_to_all | solution.py:107
  97.2 1.8 %fusion.3 = f32[256,768]{0,1:T(8,128)S(1)} fusion(bf16[256,768]{1,0:T(8,128)(2,1)S(1)} %copy-done.5, bf16[768,1536]{1,0:T(8,128)(2,1)} %bitcast.11), kind=kOutput, calls=%fused_computation.12 | convolution fusion | flops 301989888 | bytes 2359296 | tf_op jit(solution)/shard_map/dot_general | solution.py:114
  100.0 1.2 copy.104
  101.2 1.9 %copy.105 = f32[256,384]{1,0:T(8,128)} copy(f32[256,384]{0,1:T(8,128)} %get-tuple-element.10) | data formatting | bytes 786432
  103.1 1.1 select_convert_fusion
  104.2 1.9 %collective-permute-start.1 = (bf16[256,384]{1,0:T(8,128)(2,1)S(1)}, bf16[256,384]{1,0:T(8,128)(2,1)S(1)}, u32[]{:S(2)}, u32[]{:S(2)}) collective-permute-start(bf16[256,384]{1,0:T(8,128)(2,1)S(1)} %select_convert_fusion), channel_id=1, source_target_pairs={{0,1},{1,0},{2,3},{3,2},{4,5},{5,4},{6,7},{7,6},{8,9},{9,8},{10,11... | collective-permute-start | bytes 589832 | tf_op jit(solution)/shard_map/ppermute | solution.py:122
  106.2 1.3 collective-permute-done.1
  107.5 1.8 %fusion.28 = (f32[256]{0:T(256)S(1)}, f32[256]{0:T(256)S(1)}, f32[256,384]{1,0:T(8,128)}) fusion(f32[256]{0:T(256)S(1)} %rsqrt.12, f32[256]{0:T(256)S(1)} %div.32, f32[256,768]{1,0:T(8,128)} %bitcast.64, s32[]{:T(128)S(6)} %select_n.42, f32[384]{0:T(512)S(1)} %dynamic_slice.13, bf16[256,384]{1,0:T(8,128)(2,1)S(1)} %collective-permute-done.1, ...), kind=kLoop, calls=%fused_computation.65 | loop fusion | flops 884224 | bytes 1775109 | tf_op jit(solution)/shard_map/reduce_sum | solution.py:128
  109.9 2.2 %collective-permute-start.2 = (f32[256,2]{0,1:T(2,128)}, f32[256,2]{0,1:T(2,128)}, u32[]{:S(2)}, u32[]{:S(2)}) collective-permute-start(f32[256,2]{0,1:T(2,128)} %pad_maximum_fusion.2), channel_id=1, source_target_pairs={{0,1},{1,0},{2,3},{3,2},{4,5},{5,4},{6,7},{7,6},{8,9},{9,8},{10,11... | collective-permute-start | bytes 6152 | tf_op jit(solution)/shard_map/ppermute | solution.py:130
  112.8 2.1 %rev.3 = f32[7,7,384]{2,1,0:T(8,128)} reverse(f32[7,7,384]{2,1,0:T(8,128)} %constant_dynamic-slice_fusion), dimensions={0,1} | reverse | bytes 150528 | tf_op jit(solution)/shard_map/rev | solution.py:136
  114.9 7.2 %all-to-all-done.2 = bf16[4,8,24,1536]{3,2,1,0:T(8,128)(2,1)S(1)} async-done(((bf16[4,8,24,1536]{3,2,1,0:T(8,128)(2,1)}), bf16[4,8,24,1536]{3,2,1,0:T(8,128)(2,1)S(1)}, u32[]{:S(2)}, u32[]{:S(2)}) %all-to-all-start.2) | async-done | bytes 2359328 | tf_op jit(solution)/shard_map/all_to_all | solution.py:107
  122.1 1.3 reduce_sum.61
  123.4 5.6 %all-to-all-start.3 = ((bf16[8,24,1536]{2,1,0:T(8,128)(2,1)}), bf16[8,24,1536]{2,1,0:T(8,128)(2,1)S(1)}, u32[]{:S(2)}, u32[]{:S(2)}) async-start(bf16[8,24,1536]{2,1,0:T(8,128)(2,1)} %reduce_sum.61), calls=%async_computation.3 | async-start | bytes 1179648 | tf_op jit(solution)/shard_map/all_to_all | solution.py:109
  129.7 1.2 subtract_multiply_fusion
  131.0 1.6 %fusion.19 = f32[4,8,8,384]{3,0,2,1:T(4,128)S(1)} fusion(f32[4,8,8,384]{3,2,1,0:T(8,128)S(1)} %bitcast.69, f32[7,7,1,384]{3,1,0,2:T(8,128)S(1)} %bitcast.74), kind=kOutput, calls=%fused_computation.33 | convolution fusion | flops 35684352 | bytes 861696 | tf_op jit(solution)/shard_map/conv_general_dilated | solution.py:11
  133.4 9.6 %all-to-all-done.3 = bf16[8,24,1536]{2,1,0:T(8,128)(2,1)S(1)} async-done(((bf16[8,24,1536]{2,1,0:T(8,128)(2,1)}), bf16[8,24,1536]{2,1,0:T(8,128)(2,1)S(1)}, u32[]{:S(2)}, u32[]{:S(2)}) %all-to-all-start.3) | async-done | bytes 589856 | tf_op jit(solution)/shard_map/all_to_all | solution.py:109
  (75 shorter events, 10.9 us)
Async XLA Ops:
  0.6 3.3 %copy-start = (bf16[512,768]{1,0:T(8,128)(2,1)S(1)}, bf16[512,768]{1,0:T(8,128)(2,1)}, u32[]{:S(2)}) copy-start(bf16[512,768]{1,0:T(8,128)(2,1)} %param.11) | copy-start | bytes 2359300
  0.6 23.6 %copy-start.16 = (bf16[256,768]{1,0:T(8,128)(2,1)S(1)}, bf16[256,768]{1,0:T(8,128)(2,1)}, u32[]{:S(2)}) copy-start(bf16[256,768]{1,0:T(8,128)(2,1)} %param.10) | copy-start | bytes 1179652
  0.7 23.6 %copy-start.8 = (f32[7,7,768]{2,1,0:T(8,128)S(1)}, f32[7,7,768]{2,1,0:T(8,128)}, u32[]{:S(2)}) copy-start(f32[7,7,768]{2,1,0:T(8,128)} %param.15) | copy-start | bytes 451588
  4.0 25.2 %copy-start.10 = (bf16[24,768]{1,0:T(8,128)(2,1)S(1)}, bf16[24,768]{1,0:T(8,128)(2,1)}, u32[]{:S(2)}) copy-start(bf16[24,768]{1,0:T(8,128)(2,1)} %param.19) | copy-start | bytes 110596
  4.0 25.2 %copy-start.11 = (bf16[24,768]{1,0:T(8,128)(2,1)S(1)}, bf16[24,768]{1,0:T(8,128)(2,1)}, u32[]{:S(2)}) copy-start(bf16[24,768]{1,0:T(8,128)(2,1)} %param.18) | copy-start | bytes 110596
  5.8 50.7 %all-to-all-start = ((bf16[16,16,384]{2,1,0:T(8,128)(2,1)}), bf16[16,16,384]{2,1,0:T(8,128)(2,1)S(1)}, u32[]{:S(2)}, u32[]{:S(2)}) async-start(bf16[16,16,384]{2,1,0:T(8,128)(2,1)} %bitcast.2), calls=%async_computation | async-start | bytes 393216 | tf_op jit(solution)/shard_map/all_to_all | solution.py:64
  56.5 22.3 %copy-start.2 = (bf16[16,16,384]{2,1,0:T(8,128)(2,1)}, bf16[16,16,384]{2,1,0:T(8,128)(2,1)S(1)}, u32[]{:S(2)}) copy-start(bf16[16,16,384]{2,1,0:T(8,128)(2,1)S(1)} %all-to-all-done) | copy-start | bytes 589828
  58.2 28.2 %all-to-all-start.1 = ((bf16[4,8,24,1536]{3,2,1,0:T(8,128)(2,1)}), bf16[4,8,24,1536]{3,2,1,0:T(8,128)(2,1)}, u32[]{:S(2)}, u32[]{:S(2)}) async-start(bf16[4,8,24,1536]{3,2,1,0:T(8,128)(2,1)} %broadcast_in_dim.42), calls=%async_computation.1 | async-start | bytes 4718592 | tf_op jit(solution)/shard_map/all_to_all | solution.py:76
  63.7 7.4 %copy-start.1 = (f32[4,8,8,768]{3,2,1,0:T(8,128)}, f32[4,8,8,768]{3,2,1,0:T(8,128)S(1)}, u32[]{:S(2)}) copy-start(f32[4,8,8,768]{3,2,1,0:T(8,128)S(1)} %copy.91) | copy-start | bytes 2359300
  64.3 6.8 %copy-start.12 = (f32[768]{0:T(1024)S(1)}, f32[768]{0:T(1024)}, u32[]{:S(2)}) copy-start(f32[768]{0:T(1024)} %param.16) | copy-start | bytes 9220
  71.3 7.5 %copy-start.13 = (pred[256]{0:T(512)(128)(4,1)}, pred[256]{0:T(512)(128)(4,1)S(1)}, u32[]{:S(2)}) copy-start(pred[256]{0:T(512)(128)(4,1)S(1)} %fusion.25) | copy-start | bytes 772
  72.1 5.1 %copy-start.15 = (f32[768]{0:T(1024)S(1)}, f32[768]{0:T(1024)}, u32[]{:S(2)}) copy-start(f32[768]{0:T(1024)} %param.17) | copy-start | bytes 9220
  72.1 6.7 %collective-permute-start = (bf16[256,384]{1,0:T(8,128)(2,1)}, bf16[256,384]{1,0:T(8,128)(2,1)}, u32[]{:S(2)}, u32[]{:S(2)}) collective-permute-start(bf16[256,384]{1,0:T(8,128)(2,1)} %bitcast_select_fusion), channel_id=1, source_target_pairs={{0,1},{1,0},{2,3},{3,2},{4,5},{5,4},{6,7},{7,6},{8,9},{9,8},{10,11... | collective-permute-start | bytes 589832 | tf_op jit(solution)/shard_map/ppermute | solution.py:67
  90.6 0.7 copy-start.4
  93.5 3.8 %copy-start.5 = (bf16[256,768]{1,0:T(8,128)(2,1)S(1)}, bf16[256,768]{1,0:T(8,128)(2,1)}, u32[]{:S(2)}) copy-start(bf16[256,768]{1,0:T(8,128)(2,1)} %copy-done.4) | copy-start | bytes 1179652
  93.5 28.6 %all-to-all-start.2 = ((bf16[4,8,24,1536]{3,2,1,0:T(8,128)(2,1)}), bf16[4,8,24,1536]{3,2,1,0:T(8,128)(2,1)S(1)}, u32[]{:S(2)}, u32[]{:S(2)}) async-start(bf16[4,8,24,1536]{3,2,1,0:T(8,128)(2,1)} %pad_maximum_fusion), calls=%async_computation.2 | async-start | bytes 4718592 | tf_op jit(solution)/shard_map/all_to_all | solution.py:107
  103.1 9.0 %copy-start.9 = (f32[7,7,768]{2,1,0:T(8,128)S(1)}, f32[7,7,768]{2,1,0:T(8,128)}, u32[]{:S(2)}) copy-start(f32[7,7,768]{2,1,0:T(8,128)} %param.15) | copy-start | bytes 451588
  104.2 3.3 %collective-permute-start.1 = (bf16[256,384]{1,0:T(8,128)(2,1)S(1)}, bf16[256,384]{1,0:T(8,128)(2,1)S(1)}, u32[]{:S(2)}, u32[]{:S(2)}) collective-permute-start(bf16[256,384]{1,0:T(8,128)(2,1)S(1)} %select_convert_fusion), channel_id=1, source_target_pairs={{0,1},{1,0},{2,3},{3,2},{4,5},{5,4},{6,7},{7,6},{8,9},{9,8},{10,11... | collective-permute-start | bytes 589832 | tf_op jit(solution)/shard_map/ppermute | solution.py:122
  109.4 20.4 %copy-start.6 = (f32[256,384]{1,0:T(8,128)S(1)}, f32[256,384]{1,0:T(8,128)}, u32[]{:S(2)}) copy-start(f32[256,384]{1,0:T(8,128)} %get-tuple-element.8) | copy-start | bytes 1179652
  109.9 19.1 %collective-permute-start.2 = (f32[256,2]{0,1:T(2,128)}, f32[256,2]{0,1:T(2,128)}, u32[]{:S(2)}, u32[]{:S(2)}) collective-permute-start(f32[256,2]{0,1:T(2,128)} %pad_maximum_fusion.2), channel_id=1, source_target_pairs={{0,1},{1,0},{2,3},{3,2},{4,5},{5,4},{6,7},{7,6},{8,9},{9,8},{10,11... | collective-permute-start | bytes 6152 | tf_op jit(solution)/shard_map/ppermute | solution.py:130
  123.4 7.6 %copy-start.7 = (f32[7,7,384]{2,1,0:T(8,128)S(1)}, f32[7,7,384]{2,1,0:T(8,128)}, u32[]{:S(2)}) copy-start(f32[7,7,384]{2,1,0:T(8,128)} %rev.3) | copy-start | bytes 225796
  123.4 9.2 %copy-start.3 = (bf16[16,16,384]{2,1,0:T(8,128)(2,1)S(1)}, bf16[16,16,384]{2,1,0:T(8,128)(2,1)}, u32[]{:S(2)}) copy-start(bf16[16,16,384]{2,1,0:T(8,128)(2,1)} %copy-done.2) | copy-start | bytes 589828
  123.4 9.2 %copy-start.14 = (pred[256]{0:T(512)(128)(4,1)S(1)}, pred[256]{0:T(512)(128)(4,1)}, u32[]{:S(2)}) copy-start(pred[256]{0:T(512)(128)(4,1)} %copy-done.13) | copy-start | bytes 772
  123.4 19.6 %all-to-all-start.3 = ((bf16[8,24,1536]{2,1,0:T(8,128)(2,1)}), bf16[8,24,1536]{2,1,0:T(8,128)(2,1)S(1)}, u32[]{:S(2)}, u32[]{:S(2)}) async-start(bf16[8,24,1536]{2,1,0:T(8,128)(2,1)} %reduce_sum.61), calls=%async_computation.3 | async-start | bytes 1179648 | tf_op jit(solution)/shard_map/all_to_all | solution.py:109

commit v6 on v4

--- a/solution.py
+++ b/solution.py
@@ -50,11 +50,11 @@
     half_width = channels // lax.axis_size("llm")
     core_index = lax.axis_index("llm")
 
-    visual = jnp.take(grad_seq, visual_pos[0], axis=0)
-    outgoing = jnp.take(visual.reshape(groups, block_rows, channels), assign[0], axis=0).reshape(
-        row_count, channels
-    )
-    out_half = lax.dynamic_slice_in_dim(outgoing, core_index * half_width, half_width, 1)
+    source_rows = jnp.take(
+        visual_pos[0].reshape(groups, block_rows), assign[0], axis=0, mode="clip"
+    ).reshape(row_count)
+    seq_half = lax.dynamic_slice_in_dim(grad_seq, core_index * half_width, half_width, 1)
+    out_half = jnp.take(seq_half, source_rows, axis=0, mode="clip")
     arrived_half = lax.all_to_all(out_half, "dp", split_axis=0, concat_axis=0, tiled=True)
     present = jnp.arange(row_count) // (SIDE * SIDE) < tile_count[0]
     mine_half = jnp.where(present[:, None], arrived_half, jnp.zeros_like(arrived_half))

time: 141 us -> 139 us (0.986)
  other arithmetic: 15.3 us -> 13 us
    select_n x4 -> x0, other arithmetic: 2.3 us -> none  [the longest x2 1.52 us: body(): jnp.take(visual.reshape(groups, block_rows, channels), assign[0], axis=0)]
where the time goes in v6:
time: 139 us
  starting transfers between devices  37.8 us (27%)
  waiting for transfers between devices  34.7 us (25%)
  blocking collectives  27.1 us (19%)
  other arithmetic  13 us (9%)
  local copies, waits for them, and re-layouts  12.9 us (9%)
  matrix products  11.3 us (8%)
  between operations  1.66 us (1%)
    all_gather x1, blocking collectives, body(): y_block = lax.all_gather(both, 'fy', axis=0)  27.1 us
    all_to_all x1, starting transfers between devices, body(): lax.all_to_all(out_half, 'dp', split_axis=0, concat_axis=0, tiled=True)  18.4 us
    all_to_all x1, waiting for transfers between devices, body(): lax.all_to_all(terms, 'fx', split_axis=1, concat_axis=1, tiled=True)  17.7 us
    all_to_all x1, waiting for transfers between devices, body(): lax.all_to_all(x_sums, 'fy', split_axis=0, concat_axis=0, tiled=True)  10.9 us
    conv_general_dilated x2, matrix products, depthwise(): lax.conv_general_dilated(images, kernel[:, :, None, :], (1, 1), 'SAME', d...  7.21 us
    all_to_all x1, starting transfers between devices, body(): lax.all_to_all(x_sums, 'fy', split_axis=0, concat_axis=0, tiled=True)  5.46 us
    all_to_all x1, waiting for transfers between devices, body(): lax.all_to_all(x_tiled, 'fx', split_axis=1, concat_axis=1, tiled=True)  4.87 us
    all_to_all x1, starting transfers between devices, body(): lax.all_to_all(x_tiled, 'fx', split_axis=1, concat_axis=1, tiled=True)  4.42 us
  transfers between devices with their start and end apart: 7, of which 4 were waited for; matrix products, arithmetic and copies ran while one was open for 17% of the time, Pallas kernels for 0%

profile of v6, /device:TPU:64, one launch (start us, length us, event | category | flops | bytes accessed | tf_op | source)
XLA Modules:
  0.0 138.5 jit_solution(10475245802287796415)
XLA Ops:
  1.2 1.3 reduce.6
  2.6 0.7 pad_clamp_fusion.1
  4.0 1.8 %gather_fusion.1 = bf16[256,384]{1,0:T(8,128)(2,1)} fusion(bf16[512,384]{1,0:T(8,128)(2,1)S(1)} %constant_dynamic-slice_fusion.1, s32[1024]{0:T(1024)S(1)} %pad_clamp_fusion), kind=kCustom, calls=%fused_computation.1 | custom fusion | bytes 394240 | tf_op jit(solution)/shard_map/jit(_take)/gather | solution.py:57
  5.8 18.4 %all-to-all-start = ((bf16[16,16,384]{2,1,0:T(8,128)(2,1)}), bf16[16,16,384]{2,1,0:T(8,128)(2,1)S(1)}, u32[]{:S(2)}, u32[]{:S(2)}) async-start(bf16[16,16,384]{2,1,0:T(8,128)(2,1)} %bitcast.2), calls=%async_computation | async-start | bytes 393216 | tf_op jit(solution)/shard_map/all_to_all | solution.py:58
  24.3 27.1 %all-gather = bf16[192,1536]{1,0:T(8,128)(2,1)S(1)} all-gather(bf16[24,1536]{1,0:T(8,128)(2,1)S(1)} %pad_maximum_fusion.1), channel_id=2, replica_groups=mesh['dp'=16,'fy'=8,'fx'=4,'llm'=2] {'fy'}, dimensions={0}, use_global_device_ids=true | all-gather | bytes 663552 | tf_op jit(solution)/shard_map/all_gather | solution.py:68
  51.4 1.6 %broadcast_in_dim.42 = bf16[8,4,24,1536]{3,2,0,1:T(8,128)(2,1)} broadcast(bf16[8,24,1536]{2,1,0:T(8,128)(2,1)S(1)} %bitcast.43), dimensions={0,2,3} | broadcast | bytes 2949120 | tf_op jit(solution)/shard_map/broadcast_in_dim | solution.py:69
  53.0 4.4 %all-to-all-start.1 = ((bf16[8,4,24,1536]{3,2,0,1:T(8,128)(2,1)}), bf16[8,4,24,1536]{3,2,0,1:T(8,128)(2,1)S(1)}, u32[]{:S(2)}, u32[]{:S(2)}) async-start(bf16[8,4,24,1536]{3,2,0,1:T(8,128)(2,1)} %broadcast_in_dim.42), calls=%async_computation.1 | async-start | bytes 4718592 | tf_op jit(solution)/shard_map/all_to_all | solution.py:70
  57.5 5.6 %fusion.26 = (f32[4,8,8]{0,2,1:T(8,128)S(1)}, f32[4,8,8,768]{3,0,2,1:T(4,128)}) fusion(f32[7,7,1,768]{3,1,0,2:T(8,128)S(1)} %bitcast.48, bf16[4,8,8,768]{3,2,1,0:T(8,128)(2,1)} %bitcast.56), kind=kOutput, calls=%fused_computation.63 | convolution fusion | flops 71565056 | bytes 1331200 | tf_op jit(solution)/shard_map/conv_general_dilated | solution.py:11
  63.4 2.2 %copy.65 = f32[4,8,8,768]{3,2,1,0:T(8,128)} copy(f32[4,8,8,768]{3,0,2,1:T(4,128)} %get-tuple-element.15) | data formatting | bytes 1572864 | tf_op jit(solution)/shard_map/conv_general_dilated | solution.py:11
  65.5 1.5 %multiply_reduce_fusion = f32[4,8,8]{0,2,1:T(8,128)S(1)} fusion(f32[4,8,8,768]{3,0,2,1:T(4,128)} %get-tuple-element.15, f32[4,8,8]{0,2,1:T(8,128)S(1)} %copy.62), kind=kLoop, calls=%fused_computation.24 | loop fusion | flops 589568 | bytes 788480 | tf_op jit(solution)/shard_map/reduce_sum | solution.py:81
  68.0 1.9 %collective-permute-start = (bf16[256,384]{1,0:T(8,128)(2,1)S(1)}, bf16[256,384]{1,0:T(8,128)(2,1)}, u32[]{:S(2)}, u32[]{:S(2)}) collective-permute-start(bf16[256,384]{1,0:T(8,128)(2,1)S(1)} %bitcast_select_fusion), channel_id=1, source_target_pairs={{0,1},{1,0},{2,3},{3,2},{4,5},{5,4},{6,7},{7,6},{8,9},{9,8},{10,11... | collective-permute-start | bytes 589832 | tf_op jit(solution)/shard_map/ppermute | solution.py:61
  70.0 2.4 %fusion.18 = (bf16[768,256]{0,1:T(8,128)(2,1)}, f32[256,768]{1,0:T(8,128)}) fusion(f32[768]{0:T(1024)S(1)} %copy-done.11, f32[256]{0:T(256)S(1)} %rsqrt.12, f32[256]{0:T(256)S(1)} %div.32, f32[4,8,8,768]{3,2,1,0:T(8,128)} %copy.65), kind=kLoop, calls=%fused_computation.40 | loop fusion | flops 786432 | bytes 1971200 | tf_op jit(solution)/shard_map/dot_general | solution.py:91
  72.4 1.9 %copy.69 = bf16[768,256]{1,0:T(8,128)(2,1)} copy(bf16[768,256]{0,1:T(8,128)(2,1)} %get-tuple-element.5) | data formatting | bytes 786432 | tf_op jit(solution)/shard_map/dot_general | solution.py:91
  74.3 1.7 %broadcast_select_fusion.1 = (bf16[256,384]{1,0:T(8,128)(2,1)S(1)}, bf16[256,384]{1,0:T(8,128)(2,1)}) fusion(bf16[256,384]{1,0:T(8,128)(2,1)} %collective-permute-done, pred[]{:T(512)S(6)} %eq.2, bf16[16,16,384]{2,1,0:T(8,128)(2,1)S(1)} %all-to-all-done, pred[256]{0:T(512)(128)(4,1)S(1)} %fusion.20), kind=kLoop, calls=%fused_computation.38 | loop fusion | flops 294912 | bytes 786689 | tf_op jit(solution)/shard_map/jit(_where)/select_n | solution.py:62
  76.0 4.9 %all-to-all-done.1 = bf16[8,4,24,1536]{3,2,0,1:T(8,128)(2,1)S(1)} async-done(((bf16[8,4,24,1536]{3,2,0,1:T(8,128)(2,1)}), bf16[8,4,24,1536]{3,2,0,1:T(8,128)(2,1)S(1)}, u32[]{:S(2)}, u32[]{:S(2)}) %all-to-all-start.1) | async-done | bytes 2359328 | tf_op jit(solution)/shard_map/all_to_all | solution.py:70
  81.1 0.9 copy-done.2
  83.1 0.6 convolution_convert_fusion
  84.9 1.6 %copy.70 = bf16[8,4,24,1536]{3,2,0,1:T(8,128)(2,1)} copy(bf16[8,4,24,1536]{3,2,1,0:T(8,128)(2,1)S(1)} %pad_maximum_fusion) | data formatting | bytes 4718592 | tf_op jit(solution)/shard_map/concatenate | solution.py:97
  86.6 3.6 %all-to-all-start.2 = ((bf16[8,4,24,1536]{3,2,0,1:T(8,128)(2,1)}), bf16[8,4,24,1536]{3,2,0,1:T(8,128)(2,1)S(1)}, u32[]{:S(2)}, u32[]{:S(2)}) async-start(bf16[8,4,24,1536]{3,2,0,1:T(8,128)(2,1)} %copy.70), calls=%async_computation.2 | async-start | bytes 4718592 | tf_op jit(solution)/shard_map/all_to_all | solution.py:99
  90.2 2.0 %fusion.2 = f32[256,768]{1,0:T(8,128)S(1)} fusion(bf16[256,768]{1,0:T(8,128)(2,1)} %copy-done.4, bf16[768,1536]{1,0:T(8,128)(2,1)} %bitcast.42), kind=kOutput, calls=%fused_computation.10 | convolution fusion | flops 301989888 | bytes 2359296 | tf_op jit(solution)/shard_map/dot_general | solution.py:106
  92.2 1.9 %collective-permute-start.1 = (bf16[256,384]{1,0:T(8,128)(2,1)S(1)}, bf16[256,384]{1,0:T(8,128)(2,1)S(1)}, u32[]{:S(2)}, u32[]{:S(2)}) collective-permute-start(bf16[256,384]{1,0:T(8,128)(2,1)S(1)} %select_convert_fusion), channel_id=1, source_target_pairs={{0,1},{1,0},{2,3},{3,2},{4,5},{5,4},{6,7},{7,6},{8,9},{9,8},{10,11... | collective-permute-start | bytes 589832 | tf_op jit(solution)/shard_map/ppermute | solution.py:113
  94.3 1.3 collective-permute-done.1
  95.6 0.8 fusion.24
  96.4 2.0 %collective-permute-start.2 = (f32[256,2]{0,1:T(2,128)S(1)}, f32[256,2]{0,1:T(2,128)S(1)}, u32[]{:S(2)}, u32[]{:S(2)}) collective-permute-start(f32[256,2]{0,1:T(2,128)S(1)} %pad_maximum_fusion.2), channel_id=1, source_target_pairs={{0,1},{1,0},{2,3},{3,2},{4,5},{5,4},{6,7},{7,6},{8,9},{9,8},{10,11... | collective-permute-start | bytes 6152 | tf_op jit(solution)/shard_map/ppermute | solution.py:121
  98.6 17.7 %all-to-all-done.2 = bf16[8,4,24,1536]{3,2,0,1:T(8,128)(2,1)S(1)} async-done(((bf16[8,4,24,1536]{3,2,0,1:T(8,128)(2,1)}), bf16[8,4,24,1536]{3,2,0,1:T(8,128)(2,1)S(1)}, u32[]{:S(2)}, u32[]{:S(2)}) %all-to-all-start.2) | async-done | bytes 2359328 | tf_op jit(solution)/shard_map/all_to_all | solution.py:99
  116.3 1.3 reduce_sum.61
  117.6 5.5 %all-to-all-start.3 = ((bf16[8,24,1536]{2,1,0:T(8,128)(2,1)}), bf16[8,24,1536]{2,1,0:T(8,128)(2,1)S(1)}, u32[]{:S(2)}, u32[]{:S(2)}) async-start(bf16[8,24,1536]{2,1,0:T(8,128)(2,1)} %reduce_sum.61), calls=%async_computation.3 | async-start | bytes 1179648 | tf_op jit(solution)/shard_map/all_to_all | solution.py:101
  123.1 1.3 subtract_multiply_fusion
  124.4 1.6 %fusion.13 = f32[4,8,8,384]{3,0,2,1:T(4,128)S(1)} fusion(f32[4,8,8,384]{3,2,1,0:T(8,128)S(1)} %bitcast.44, f32[7,7,1,384]{3,1,0,2:T(8,128)S(1)} %bitcast.47), kind=kOutput, calls=%fused_computation.28 | convolution fusion | flops 35684352 | bytes 861696 | tf_op jit(solution)/shard_map/conv_general_dilated | solution.py:11
  126.1 0.8 fusion.12
  126.9 10.9 %all-to-all-done.3 = bf16[8,24,1536]{2,1,0:T(8,128)(2,1)S(1)} async-done(((bf16[8,24,1536]{2,1,0:T(8,128)(2,1)}), bf16[8,24,1536]{2,1,0:T(8,128)(2,1)S(1)}, u32[]{:S(2)}, u32[]{:S(2)}) %all-to-all-start.3) | async-done | bytes 589856 | tf_op jit(solution)/shard_map/all_to_all | solution.py:101
  137.8 0.7 slice_multiply_fusion
  (58 shorter events, 4.9 us)
Async XLA Ops:
  0.6 3.3 %copy-start = (bf16[512,768]{1,0:T(8,128)(2,1)S(1)}, bf16[512,768]{1,0:T(8,128)(2,1)}, u32[]{:S(2)}) copy-start(bf16[512,768]{1,0:T(8,128)(2,1)} %param.11) | copy-start | bytes 2359300
  0.6 23.6 %copy-start.9 = (bf16[24,768]{1,0:T(8,128)(2,1)S(1)}, bf16[24,768]{1,0:T(8,128)(2,1)}, u32[]{:S(2)}) copy-start(bf16[24,768]{1,0:T(8,128)(2,1)} %param.19) | copy-start | bytes 110596
  0.7 23.6 %copy-start.10 = (bf16[24,768]{1,0:T(8,128)(2,1)S(1)}, bf16[24,768]{1,0:T(8,128)(2,1)}, u32[]{:S(2)}) copy-start(bf16[24,768]{1,0:T(8,128)(2,1)} %param.18) | copy-start | bytes 110596
  5.8 45.6 %all-to-all-start = ((bf16[16,16,384]{2,1,0:T(8,128)(2,1)}), bf16[16,16,384]{2,1,0:T(8,128)(2,1)S(1)}, u32[]{:S(2)}, u32[]{:S(2)}) async-start(bf16[16,16,384]{2,1,0:T(8,128)(2,1)} %bitcast.2), calls=%async_computation | async-start | bytes 393216 | tf_op jit(solution)/shard_map/all_to_all | solution.py:58
  53.0 4.4 %copy-start.7 = (f32[7,7,768]{2,1,0:T(8,128)S(1)}, f32[7,7,768]{2,1,0:T(8,128)}, u32[]{:S(2)}) copy-start(f32[7,7,768]{2,1,0:T(8,128)} %param.15) | copy-start | bytes 451588
  53.0 27.9 %all-to-all-start.1 = ((bf16[8,4,24,1536]{3,2,0,1:T(8,128)(2,1)}), bf16[8,4,24,1536]{3,2,0,1:T(8,128)(2,1)S(1)}, u32[]{:S(2)}, u32[]{:S(2)}) async-start(bf16[8,4,24,1536]{3,2,0,1:T(8,128)(2,1)} %broadcast_in_dim.42), calls=%async_computation.1 | async-start | bytes 4718592 | tf_op jit(solution)/shard_map/all_to_all | solution.py:70
  57.5 12.5 %copy-start.11 = (f32[768]{0:T(1024)S(1)}, f32[768]{0:T(1024)}, u32[]{:S(2)}) copy-start(f32[768]{0:T(1024)} %param.16) | copy-start | bytes 9220
  68.0 6.2 %collective-permute-start = (bf16[256,384]{1,0:T(8,128)(2,1)S(1)}, bf16[256,384]{1,0:T(8,128)(2,1)}, u32[]{:S(2)}, u32[]{:S(2)}) collective-permute-start(bf16[256,384]{1,0:T(8,128)(2,1)S(1)} %bitcast_select_fusion), channel_id=1, source_target_pairs={{0,1},{1,0},{2,3},{3,2},{4,5},{5,4},{6,7},{7,6},{8,9},{9,8},{10,11... | collective-permute-start | bytes 589832 | tf_op jit(solution)/shard_map/ppermute | solution.py:61
  80.9 1.1 copy-start.2
  81.1 2.0 %copy-start.1 = (bf16[8,4,24,1536]{3,2,1,0:T(8,128)(2,1)}, bf16[8,4,24,1536]{3,2,1,0:T(8,128)(2,1)S(1)}, u32[]{:S(2)}) copy-start(bf16[8,4,24,1536]{3,2,1,0:T(8,128)(2,1)S(1)} %copy.64) | copy-start | bytes 7077892
  81.1 1.4 %copy-start.6 = (bf16[256,384]{1,0:T(8,128)(2,1)S(1)}, bf16[256,384]{1,0:T(8,128)(2,1)}, u32[]{:S(2)}) copy-start(bf16[256,384]{1,0:T(8,128)(2,1)} %get-tuple-element.9) | copy-start | bytes 589828
  81.1 1.4 %copy-start.12 = (f32[768]{0:T(1024)S(1)}, f32[768]{0:T(1024)}, u32[]{:S(2)}) copy-start(f32[768]{0:T(1024)} %param.17) | copy-start | bytes 9220
  83.1 1.6 %copy-start.4 = (bf16[256,768]{1,0:T(8,128)(2,1)}, bf16[256,768]{1,0:T(8,128)(2,1)S(1)}, u32[]{:S(2)}) copy-start(bf16[256,768]{1,0:T(8,128)(2,1)S(1)} %fusion) | copy-start | bytes 1179652
  83.1 1.1 copy-start.5
  86.6 29.7 %all-to-all-start.2 = ((bf16[8,4,24,1536]{3,2,0,1:T(8,128)(2,1)}), bf16[8,4,24,1536]{3,2,0,1:T(8,128)(2,1)S(1)}, u32[]{:S(2)}, u32[]{:S(2)}) async-start(bf16[8,4,24,1536]{3,2,0,1:T(8,128)(2,1)} %copy.70), calls=%async_computation.2 | async-start | bytes 4718592 | tf_op jit(solution)/shard_map/all_to_all | solution.py:99
  90.2 5.4 %copy-start.3 = (f32[256,768]{1,0:T(8,128)S(1)}, f32[256,768]{1,0:T(8,128)}, u32[]{:S(2)}) copy-start(f32[256,768]{1,0:T(8,128)} %get-tuple-element.6) | copy-start | bytes 2359300
  90.2 8.3 %copy-start.8 = (f32[7,7,768]{2,1,0:T(8,128)S(1)}, f32[7,7,768]{2,1,0:T(8,128)}, u32[]{:S(2)}) copy-start(f32[7,7,768]{2,1,0:T(8,128)} %param.15) | copy-start | bytes 451588
  92.2 3.3 %collective-permute-start.1 = (bf16[256,384]{1,0:T(8,128)(2,1)S(1)}, bf16[256,384]{1,0:T(8,128)(2,1)S(1)}, u32[]{:S(2)}, u32[]{:S(2)}) collective-permute-start(bf16[256,384]{1,0:T(8,128)(2,1)S(1)} %select_convert_fusion), channel_id=1, source_target_pairs={{0,1},{1,0},{2,3},{3,2},{4,5},{5,4},{6,7},{7,6},{8,9},{9,8},{10,11... | collective-permute-start | bytes 589832 | tf_op jit(solution)/shard_map/ppermute | solution.py:113
  96.4 26.7 %collective-permute-start.2 = (f32[256,2]{0,1:T(2,128)S(1)}, f32[256,2]{0,1:T(2,128)S(1)}, u32[]{:S(2)}, u32[]{:S(2)}) collective-permute-start(f32[256,2]{0,1:T(2,128)S(1)} %pad_maximum_fusion.2), channel_id=1, source_target_pairs={{0,1},{1,0},{2,3},{3,2},{4,5},{5,4},{6,7},{7,6},{8,9},{9,8},{10,11... | collective-permute-start | bytes 6152 | tf_op jit(solution)/shard_map/ppermute | solution.py:121
  117.6 20.1 %all-to-all-start.3 = ((bf16[8,24,1536]{2,1,0:T(8,128)(2,1)}), bf16[8,24,1536]{2,1,0:T(8,128)(2,1)S(1)}, u32[]{:S(2)}, u32[]{:S(2)}) async-start(bf16[8,24,1536]{2,1,0:T(8,128)(2,1)} %reduce_sum.61), calls=%async_computation.3 | async-start | bytes 1179648 | tf_op jit(solution)/shard_map/all_to_all | solution.py:101

commit v7 on v6

--- a/solution.py
+++ b/solution.py
@@ -41,7 +41,7 @@
     weight_out,
 ):
     groups = lax.axis_size("dp")
-    height = lax.axis_size("fy")
+    height = lax.axis_size("fyh") * lax.axis_size("fyl")
     width = lax.axis_size("fx")
     shards = height * width
     row_count = tile_rows.shape[0]
@@ -65,7 +65,8 @@
 
     hid = weight_in.shape[1]
     both = jnp.concatenate([weight_in, weight_out], axis=1)
-    y_block = lax.all_gather(both, "fy", axis=0)
+    y_low = lax.all_gather(both, "fyl", axis=0)
+    y_block = lax.all_gather(y_low, "fyh", axis=0).reshape((height,) + both.shape)
     x_tiled = jnp.broadcast_to(y_block[:, None], (height, width) + both.shape)
     both_full = lax.all_to_all(x_tiled, "fx", split_axis=1, concat_axis=1, tiled=True).reshape(
         shards * both.shape[0], both.shape[1]
@@ -98,7 +99,7 @@
     terms = terms.reshape(height, width, channels // shards, 2 * hid)
     x_parts = lax.all_to_all(terms, "fx", split_axis=1, concat_axis=1, tiled=True)
     x_sums = jnp.sum(x_parts.astype(jnp.float32), axis=1).astype(jnp.bfloat16)
-    y_parts = lax.all_to_all(x_sums, "fy", split_axis=0, concat_axis=0, tiled=True)
+    y_parts = lax.all_to_all(x_sums, ("fyh", "fyl"), split_axis=0, concat_axis=0, tiled=True)
     totals = jnp.sum(y_parts.astype(jnp.float32), axis=0)
     grad_in = totals[:, :hid] / ACCUM
     grad_outw = totals[:, hid:] / ACCUM
@@ -141,10 +142,13 @@
 def solution(mesh):
     dp, fsdp, llm = mesh.devices.shape
     width = x_width(mesh)
+    height = fsdp // width
+    low = height // 2 if height % 2 == 0 else height
     split = jax.sharding.Mesh(
-        mesh.devices.reshape(dp, fsdp // width, width, llm), ("dp", "fy", "fx", "llm")
+        mesh.devices.reshape(dp, height // low, low, width, llm),
+        ("dp", "fyh", "fyl", "fx", "llm"),
     )
-    rows = ("dp", "fy", "fx")
+    rows = ("dp", "fyh", "fyl", "fx")
     in_specs = (
         P(rows, None),
         P(rows, None),
@@ -154,8 +158,8 @@
         P(),
         P(),
         P(),
-        P(("fy", "fx"), "llm"),
-        P(("fy", "fx"), "llm"),
+        P(("fyh", "fyl", "fx"), "llm"),
+        P(("fyh", "fyl", "fx"), "llm"),
     )
     out_specs = (P(rows, "llm"), P(rows, "llm"), P(rows, "llm"))
     return jax.shard_map(body, mesh=split, in_specs=in_specs, out_specs=out_specs, check_vma=False)

time: 139 us -> 149 us (1.072)
  the two profiles are of different devices: /device:TPU:64 before, /device:TPU:2 now
where the time goes in v7:
time: 149 us; the launch traced here: 148 us
  starting transfers between devices  46.1 us (31%)
  waiting for transfers between devices  32.8 us (22%)
  blocking collectives  30.6 us (21%)
  other arithmetic  13 us (9%)
  local copies, waits for them, and re-layouts  12.9 us (9%)
  matrix products  11.3 us (8%)
  between operations  1.65 us (1%)
    all_to_all x1, starting transfers between devices, body(): lax.all_to_all(out_half, 'dp', split_axis=0, concat_axis=0, tiled=True)  18.9 us
    all_gather x1, blocking collectives, body(): lax.all_gather(y_low, 'fyh', axis=0).reshape((height,) + both.shape)  16.4 us
    all_to_all x1, waiting for transfers between devices, body(): lax.all_to_all(terms, 'fx', split_axis=1, concat_axis=1, tiled=True)  15.7 us
    all_gather x1, blocking collectives, body(): y_low = lax.all_gather(both, 'fyl', axis=0)  14.2 us
    all_to_all x1, waiting for transfers between devices, body(): lax.all_to_all(x_sums, ('fyh', 'fyl'), split_axis=0, concat_axis=0, tiled...  11.8 us
    all_to_all x1, starting transfers between devices, body(): lax.all_to_all(x_sums, ('fyh', 'fyl'), split_axis=0, concat_axis=0, tiled...  11.3 us
    conv_general_dilated x2, matrix products, depthwise(): lax.conv_general_dilated(images, kernel[:, :, None, :], (1, 1), 'SAME', d...  7.21 us
    all_to_all x1, starting transfers between devices, body(): lax.all_to_all(terms, 'fx', split_axis=1, concat_axis=1, tiled=True)  5.06 us
  transfers between devices with their start and end apart: 7, of which 4 were waited for; matrix products, arithmetic and copies ran while one was open for 16% of the time, Pallas kernels for 0%

profile of v7, /device:TPU:2, one launch (start us, length us, event | category | flops | bytes accessed | tf_op | source)
XLA Modules:
  0.0 148.3 jit_solution(14852120379580214104)
XLA Ops:
  1.2 1.3 reduce.6
  2.6 0.7 pad_clamp_fusion.1
  4.0 1.8 %gather_fusion.1 = bf16[256,384]{1,0:T(8,128)(2,1)} fusion(bf16[512,384]{1,0:T(8,128)(2,1)S(1)} %constant_dynamic-slice_fusion.1, s32[1024]{0:T(1024)S(1)} %pad_clamp_fusion), kind=kCustom, calls=%fused_computation.1 | custom fusion | bytes 394240 | tf_op jit(solution)/shard_map/jit(_take)/gather | solution.py:57
  5.8 18.9 %all-to-all-start = ((bf16[16,16,384]{2,1,0:T(8,128)(2,1)}), bf16[16,16,384]{2,1,0:T(8,128)(2,1)S(1)}, u32[]{:S(2)}, u32[]{:S(2)}) async-start(bf16[16,16,384]{2,1,0:T(8,128)(2,1)} %bitcast.2), calls=%async_computation | async-start | bytes 393216 | tf_op jit(solution)/shard_map/all_to_all | solution.py:58
  24.7 14.2 %all-gather = bf16[96,1536]{1,0:T(8,128)(2,1)S(1)} all-gather(bf16[24,1536]{1,0:T(8,128)(2,1)S(1)} %pad_maximum_fusion.1), channel_id=2, replica_groups=mesh['dp'=16,'fyh'=2,'fyl'=4,'fx'=4,'llm'=2] {'fyl'}, dimensions={0}, use_global_device_ids=true | all-gather | bytes 368640 | tf_op jit(solution)/shard_map/all_gather | solution.py:68
  38.9 16.4 %all-gather.1 = bf16[8,24,1536]{2,1,0:T(8,128)(2,1)S(1)} all-gather(bf16[4,24,1536]{2,1,0:T(8,128)(2,1)S(1)} %bitcast.45), channel_id=3, replica_groups=mesh['dp'=16,'fyh'=2,'fyl'=4,'fx'=4,'llm'=2] {'fyh'}, dimensions={0}, use_global_device_ids=true | all-gather | bytes 884736 | tf_op jit(solution)/shard_map/all_gather | solution.py:69
  55.3 1.6 %broadcast_in_dim.44 = bf16[8,4,24,1536]{3,2,0,1:T(8,128)(2,1)} broadcast(bf16[8,24,1536]{2,1,0:T(8,128)(2,1)S(1)} %all-gather.1), dimensions={0,2,3} | broadcast | bytes 2949120 | tf_op jit(solution)/shard_map/broadcast_in_dim | solution.py:70
  56.9 5.0 %all-to-all-start.1 = ((bf16[8,4,24,1536]{3,2,0,1:T(8,128)(2,1)}), bf16[8,4,24,1536]{3,2,0,1:T(8,128)(2,1)S(1)}, u32[]{:S(2)}, u32[]{:S(2)}) async-start(bf16[8,4,24,1536]{3,2,0,1:T(8,128)(2,1)} %broadcast_in_dim.44), calls=%async_computation.1 | async-start | bytes 4718592 | tf_op jit(solution)/shard_map/all_to_all | solution.py:71
  61.8 5.6 %fusion.26 = (f32[4,8,8]{0,2,1:T(8,128)S(1)}, f32[4,8,8,768]{3,0,2,1:T(4,128)}) fusion(f32[7,7,1,768]{3,1,0,2:T(8,128)S(1)} %bitcast.48, bf16[4,8,8,768]{3,2,1,0:T(8,128)(2,1)} %bitcast.56), kind=kOutput, calls=%fused_computation.63 | convolution fusion | flops 71565056 | bytes 1331200 | tf_op jit(solution)/shard_map/conv_general_dilated | solution.py:11
  67.8 2.2 %copy.65 = f32[4,8,8,768]{3,2,1,0:T(8,128)} copy(f32[4,8,8,768]{3,0,2,1:T(4,128)} %get-tuple-element.15) | data formatting | bytes 1572864 | tf_op jit(solution)/shard_map/conv_general_dilated | solution.py:11
  69.9 1.5 multiply_reduce_fusion
  72.4 1.9 %collective-permute-start = (bf16[256,384]{1,0:T(8,128)(2,1)S(1)}, bf16[256,384]{1,0:T(8,128)(2,1)}, u32[]{:S(2)}, u32[]{:S(2)}) collective-permute-start(bf16[256,384]{1,0:T(8,128)(2,1)S(1)} %bitcast_select_fusion), channel_id=1, source_target_pairs={{0,1},{1,0},{2,3},{3,2},{4,5},{5,4},{6,7},{7,6},{8,9},{9,8},{10,11... | collective-permute-start | bytes 589832 | tf_op jit(solution)/shard_map/ppermute | solution.py:61
  74.4 2.4 %fusion.18 = (bf16[768,256]{0,1:T(8,128)(2,1)}, f32[256,768]{1,0:T(8,128)}) fusion(f32[768]{0:T(1024)S(1)} %copy-done.11, f32[256]{0:T(256)S(1)} %rsqrt.12, f32[256]{0:T(256)S(1)} %div.32, f32[4,8,8,768]{3,2,1,0:T(8,128)} %copy.65), kind=kLoop, calls=%fused_computation.40 | loop fusion | flops 786432 | bytes 1971200 | tf_op jit(solution)/shard_map/dot_general | solution.py:92
  76.8 1.9 %copy.69 = bf16[768,256]{1,0:T(8,128)(2,1)} copy(bf16[768,256]{0,1:T(8,128)(2,1)} %get-tuple-element.5) | data formatting | bytes 786432 | tf_op jit(solution)/shard_map/dot_general | solution.py:92
  78.7 1.7 %broadcast_select_fusion.1 = (bf16[256,384]{1,0:T(8,128)(2,1)S(1)}, bf16[256,384]{1,0:T(8,128)(2,1)}) fusion(bf16[256,384]{1,0:T(8,128)(2,1)} %collective-permute-done, pred[]{:T(512)S(6)} %eq.2, bf16[16,16,384]{2,1,0:T(8,128)(2,1)S(1)} %all-to-all-done, pred[256]{0:T(512)(128)(4,1)S(1)} %fusion.20), kind=kLoop, calls=%fused_computation.38 | loop fusion | flops 294912 | bytes 786689 | tf_op jit(solution)/shard_map/jit(_where)/select_n | solution.py:62
  80.4 4.0 %all-to-all-done.1 = bf16[8,4,24,1536]{3,2,0,1:T(8,128)(2,1)S(1)} async-done(((bf16[8,4,24,1536]{3,2,0,1:T(8,128)(2,1)}), bf16[8,4,24,1536]{3,2,0,1:T(8,128)(2,1)S(1)}, u32[]{:S(2)}, u32[]{:S(2)}) %all-to-all-start.1) | async-done | bytes 2359328 | tf_op jit(solution)/shard_map/all_to_all | solution.py:71
  84.7 0.9 copy-done.2
  88.5 1.6 %copy.70 = bf16[8,4,24,1536]{3,2,0,1:T(8,128)(2,1)} copy(bf16[8,4,24,1536]{3,2,1,0:T(8,128)(2,1)S(1)} %pad_maximum_fusion) | data formatting | bytes 4718592 | tf_op jit(solution)/shard_map/concatenate | solution.py:98
  90.1 5.1 %all-to-all-start.2 = ((bf16[8,4,24,1536]{3,2,0,1:T(8,128)(2,1)}), bf16[8,4,24,1536]{3,2,0,1:T(8,128)(2,1)S(1)}, u32[]{:S(2)}, u32[]{:S(2)}) async-start(bf16[8,4,24,1536]{3,2,0,1:T(8,128)(2,1)} %copy.70), calls=%async_computation.2 | async-start | bytes 4718592 | tf_op jit(solution)/shard_map/all_to_all | solution.py:100
  95.2 2.0 %fusion.2 = f32[256,768]{1,0:T(8,128)S(1)} fusion(bf16[256,768]{1,0:T(8,128)(2,1)} %copy-done.4, bf16[768,1536]{1,0:T(8,128)(2,1)} %bitcast.42), kind=kOutput, calls=%fused_computation.10 | convolution fusion | flops 301989888 | bytes 2359296 | tf_op jit(solution)/shard_map/dot_general | solution.py:107
  97.2 1.9 %collective-permute-start.1 = (bf16[256,384]{1,0:T(8,128)(2,1)S(1)}, bf16[256,384]{1,0:T(8,128)(2,1)S(1)}, u32[]{:S(2)}, u32[]{:S(2)}) collective-permute-start(bf16[256,384]{1,0:T(8,128)(2,1)S(1)} %select_convert_fusion), channel_id=1, source_target_pairs={{0,1},{1,0},{2,3},{3,2},{4,5},{5,4},{6,7},{7,6},{8,9},{9,8},{10,11... | collective-permute-start | bytes 589832 | tf_op jit(solution)/shard_map/ppermute | solution.py:114
  99.2 1.3 collective-permute-done.1
  100.5 0.8 fusion.24
  101.4 2.0 %collective-permute-start.2 = (f32[256,2]{0,1:T(2,128)S(1)}, f32[256,2]{0,1:T(2,128)S(1)}, u32[]{:S(2)}, u32[]{:S(2)}) collective-permute-start(f32[256,2]{0,1:T(2,128)S(1)} %pad_maximum_fusion.2), channel_id=1, source_target_pairs={{0,1},{1,0},{2,3},{3,2},{4,5},{5,4},{6,7},{7,6},{8,9},{9,8},{10,11... | collective-permute-start | bytes 6152 | tf_op jit(solution)/shard_map/ppermute | solution.py:122
  103.6 15.7 %all-to-all-done.2 = bf16[8,4,24,1536]{3,2,0,1:T(8,128)(2,1)S(1)} async-done(((bf16[8,4,24,1536]{3,2,0,1:T(8,128)(2,1)}), bf16[8,4,24,1536]{3,2,0,1:T(8,128)(2,1)S(1)}, u32[]{:S(2)}, u32[]{:S(2)}) %all-to-all-start.2) | async-done | bytes 2359328 | tf_op jit(solution)/shard_map/all_to_all | solution.py:100
  119.2 1.3 reduce_sum.61
  120.6 11.3 %all-to-all-start.3 = ((bf16[8,24,1536]{2,1,0:T(8,128)(2,1)}), bf16[8,24,1536]{2,1,0:T(8,128)(2,1)S(1)}, u32[]{:S(2)}, u32[]{:S(2)}) async-start(bf16[8,24,1536]{2,1,0:T(8,128)(2,1)} %reduce_sum.61), calls=%async_computation.3 | async-start | bytes 1179648 | tf_op jit(solution)/shard_map/all_to_all | solution.py:102
  131.9 1.3 subtract_multiply_fusion
  133.2 1.6 %fusion.13 = f32[4,8,8,384]{3,0,2,1:T(4,128)S(1)} fusion(f32[4,8,8,384]{3,2,1,0:T(8,128)S(1)} %bitcast.43, f32[7,7,1,384]{3,1,0,2:T(8,128)S(1)} %bitcast.47), kind=kOutput, calls=%fused_computation.28 | convolution fusion | flops 35684352 | bytes 861696 | tf_op jit(solution)/shard_map/conv_general_dilated | solution.py:11
  134.9 0.8 fusion.12
  135.7 11.8 %all-to-all-done.3 = bf16[8,24,1536]{2,1,0:T(8,128)(2,1)S(1)} async-done(((bf16[8,24,1536]{2,1,0:T(8,128)(2,1)}), bf16[8,24,1536]{2,1,0:T(8,128)(2,1)S(1)}, u32[]{:S(2)}, u32[]{:S(2)}) %all-to-all-start.3) | async-done | bytes 589856 | tf_op jit(solution)/shard_map/all_to_all | solution.py:102
  147.6 0.7 slice_multiply_fusion
  (59 shorter events, 5.5 us)
Async XLA Ops:
  0.6 3.3 %copy-start = (bf16[512,768]{1,0:T(8,128)(2,1)S(1)}, bf16[512,768]{1,0:T(8,128)(2,1)}, u32[]{:S(2)}) copy-start(bf16[512,768]{1,0:T(8,128)(2,1)} %param.11) | copy-start | bytes 2359300
  0.6 24.0 %copy-start.9 = (bf16[24,768]{1,0:T(8,128)(2,1)S(1)}, bf16[24,768]{1,0:T(8,128)(2,1)}, u32[]{:S(2)}) copy-start(bf16[24,768]{1,0:T(8,128)(2,1)} %param.19) | copy-start | bytes 110596
  0.7 24.0 %copy-start.10 = (bf16[24,768]{1,0:T(8,128)(2,1)S(1)}, bf16[24,768]{1,0:T(8,128)(2,1)}, u32[]{:S(2)}) copy-start(bf16[24,768]{1,0:T(8,128)(2,1)} %param.18) | copy-start | bytes 110596
  5.8 49.5 %all-to-all-start = ((bf16[16,16,384]{2,1,0:T(8,128)(2,1)}), bf16[16,16,384]{2,1,0:T(8,128)(2,1)S(1)}, u32[]{:S(2)}, u32[]{:S(2)}) async-start(bf16[16,16,384]{2,1,0:T(8,128)(2,1)} %bitcast.2), calls=%async_computation | async-start | bytes 393216 | tf_op jit(solution)/shard_map/all_to_all | solution.py:58
  56.9 5.0 %copy-start.7 = (f32[7,7,768]{2,1,0:T(8,128)S(1)}, f32[7,7,768]{2,1,0:T(8,128)}, u32[]{:S(2)}) copy-start(f32[7,7,768]{2,1,0:T(8,128)} %param.15) | copy-start | bytes 451588
  56.9 27.6 %all-to-all-start.1 = ((bf16[8,4,24,1536]{3,2,0,1:T(8,128)(2,1)}), bf16[8,4,24,1536]{3,2,0,1:T(8,128)(2,1)S(1)}, u32[]{:S(2)}, u32[]{:S(2)}) async-start(bf16[8,4,24,1536]{3,2,0,1:T(8,128)(2,1)} %broadcast_in_dim.44), calls=%async_computation.1 | async-start | bytes 4718592 | tf_op jit(solution)/shard_map/all_to_all | solution.py:71
  61.8 12.5 %copy-start.11 = (f32[768]{0:T(1024)S(1)}, f32[768]{0:T(1024)}, u32[]{:S(2)}) copy-start(f32[768]{0:T(1024)} %param.16) | copy-start | bytes 9220
  72.4 6.2 %collective-permute-start = (bf16[256,384]{1,0:T(8,128)(2,1)S(1)}, bf16[256,384]{1,0:T(8,128)(2,1)}, u32[]{:S(2)}, u32[]{:S(2)}) collective-permute-start(bf16[256,384]{1,0:T(8,128)(2,1)S(1)} %bitcast_select_fusion), channel_id=1, source_target_pairs={{0,1},{1,0},{2,3},{3,2},{4,5},{5,4},{6,7},{7,6},{8,9},{9,8},{10,11... | collective-permute-start | bytes 589832 | tf_op jit(solution)/shard_map/ppermute | solution.py:61
  84.4 1.1 copy-start.2
  84.7 2.0 %copy-start.1 = (bf16[8,4,24,1536]{3,2,1,0:T(8,128)(2,1)}, bf16[8,4,24,1536]{3,2,1,0:T(8,128)(2,1)S(1)}, u32[]{:S(2)}) copy-start(bf16[8,4,24,1536]{3,2,1,0:T(8,128)(2,1)S(1)} %copy.64) | copy-start | bytes 7077892
  84.7 1.4 copy-start.6
  84.7 1.4 copy-start.12
  86.7 1.6 %copy-start.4 = (bf16[256,768]{1,0:T(8,128)(2,1)}, bf16[256,768]{1,0:T(8,128)(2,1)S(1)}, u32[]{:S(2)}) copy-start(bf16[256,768]{1,0:T(8,128)(2,1)S(1)} %fusion) | copy-start | bytes 1179652
  86.7 1.1 copy-start.5
  90.1 29.1 %all-to-all-start.2 = ((bf16[8,4,24,1536]{3,2,0,1:T(8,128)(2,1)}), bf16[8,4,24,1536]{3,2,0,1:T(8,128)(2,1)S(1)}, u32[]{:S(2)}, u32[]{:S(2)}) async-start(bf16[8,4,24,1536]{3,2,0,1:T(8,128)(2,1)} %copy.70), calls=%async_computation.2 | async-start | bytes 4718592 | tf_op jit(solution)/shard_map/all_to_all | solution.py:100
  95.2 5.4 %copy-start.3 = (f32[256,768]{1,0:T(8,128)S(1)}, f32[256,768]{1,0:T(8,128)}, u32[]{:S(2)}) copy-start(f32[256,768]{1,0:T(8,128)} %get-tuple-element.6) | copy-start | bytes 2359300
  95.2 8.3 %copy-start.8 = (f32[7,7,768]{2,1,0:T(8,128)S(1)}, f32[7,7,768]{2,1,0:T(8,128)}, u32[]{:S(2)}) copy-start(f32[7,7,768]{2,1,0:T(8,128)} %param.15) | copy-start | bytes 451588
  97.2 3.3 %collective-permute-start.1 = (bf16[256,384]{1,0:T(8,128)(2,1)S(1)}, bf16[256,384]{1,0:T(8,128)(2,1)S(1)}, u32[]{:S(2)}, u32[]{:S(2)}) collective-permute-start(bf16[256,384]{1,0:T(8,128)(2,1)S(1)} %select_convert_fusion), channel_id=1, source_target_pairs={{0,1},{1,0},{2,3},{3,2},{4,5},{5,4},{6,7},{7,6},{8,9},{9,8},{10,11... | collective-permute-start | bytes 589832 | tf_op jit(solution)/shard_map/ppermute | solution.py:114
  101.4 30.5 %collective-permute-start.2 = (f32[256,2]{0,1:T(2,128)S(1)}, f32[256,2]{0,1:T(2,128)S(1)}, u32[]{:S(2)}, u32[]{:S(2)}) collective-permute-start(f32[256,2]{0,1:T(2,128)S(1)} %pad_maximum_fusion.2), channel_id=1, source_target_pairs={{0,1},{1,0},{2,3},{3,2},{4,5},{5,4},{6,7},{7,6},{8,9},{9,8},{10,11... | collective-permute-start | bytes 6152 | tf_op jit(solution)/shard_map/ppermute | solution.py:122
  120.6 27.0 %all-to-all-start.3 = ((bf16[8,24,1536]{2,1,0:T(8,128)(2,1)}), bf16[8,24,1536]{2,1,0:T(8,128)(2,1)S(1)}, u32[]{:S(2)}, u32[]{:S(2)}) async-start(bf16[8,24,1536]{2,1,0:T(8,128)(2,1)} %reduce_sum.61), calls=%async_computation.3 | async-start | bytes 1179648 | tf_op jit(solution)/shard_map/all_to_all | solution.py:102

commit v8 on v6

--- a/solution.py
+++ b/solution.py
@@ -50,11 +50,13 @@
     half_width = channels // lax.axis_size("llm")
     core_index = lax.axis_index("llm")
 
-    source_rows = jnp.take(
-        visual_pos[0].reshape(groups, block_rows), assign[0], axis=0, mode="clip"
-    ).reshape(row_count)
+    flat = (assign[0][:, None] * block_rows + jnp.arange(block_rows)[None, :]).reshape(row_count)
+    source_rows = jnp.take(visual_pos, flat, axis=1, mode="clip")[0]
     seq_half = lax.dynamic_slice_in_dim(grad_seq, core_index * half_width, half_width, 1)
-    out_half = jnp.take(seq_half, source_rows, axis=0, mode="clip")
+    pick = source_rows[:, None] == jnp.arange(grad_seq.shape[0])[None, :]
+    out_half = jnp.dot(
+        pick.astype(seq_half.dtype), seq_half, preferred_element_type=jnp.float32
+    ).astype(seq_half.dtype)
     arrived_half = lax.all_to_all(out_half, "dp", split_axis=0, concat_axis=0, tiled=True)
     present = jnp.arange(row_count) // (SIDE * SIDE) < tile_count[0]
     mine_half = jnp.where(present[:, None], arrived_half, jnp.zeros_like(arrived_half))

time: 139 us -> 139 us (level)
  transfers between devices with their start and end apart: 7 -> 7, of which waited for: 4 -> 4; matrix products, arithmetic and copies ran while one was open for 17% -> 18% of each run, Pallas kernels for 0% -> 0%
where the time goes in v8:
time: 139 us; the launch traced here: 138 us
  starting transfers between devices  37.8 us (27%)
  waiting for transfers between devices  34.2 us (25%)
  blocking collectives  27.2 us (20%)
  other arithmetic  12.6 us (9%)
  matrix products  12.3 us (9%)
  local copies, waits for them, and re-layouts  11.9 us (9%)
  between operations  1.61 us (1%)
    all_gather x1, blocking collectives, body(): y_block = lax.all_gather(both, 'fy', axis=0)  27.2 us
    all_to_all x1, starting transfers between devices, body(): lax.all_to_all(out_half, 'dp', split_axis=0, concat_axis=0, tiled=True)  18.4 us
    all_to_all x1, waiting for transfers between devices, body(): lax.all_to_all(terms, 'fx', split_axis=1, concat_axis=1, tiled=True)  17.5 us
    all_to_all x1, waiting for transfers between devices, body(): lax.all_to_all(x_sums, 'fy', split_axis=0, concat_axis=0, tiled=True)  10.4 us
    conv_general_dilated x2, matrix products, depthwise(): lax.conv_general_dilated(images, kernel[:, :, None, :], (1, 1), 'SAME', d...  7.19 us
    all_to_all x1, starting transfers between devices, body(): lax.all_to_all(x_sums, 'fy', split_axis=0, concat_axis=0, tiled=True)  5.46 us
    all_to_all x1, waiting for transfers between devices, body(): lax.all_to_all(x_tiled, 'fx', split_axis=1, concat_axis=1, tiled=True)  4.97 us
    all_to_all x1, starting transfers between devices, body(): lax.all_to_all(x_tiled, 'fx', split_axis=1, concat_axis=1, tiled=True)  4.43 us
  transfers between devices with their start and end apart: 7, of which 4 were waited for; matrix products, arithmetic and copies ran while one was open for 18% of the time, Pallas kernels for 0%

profile of v8, /device:TPU:64, one launch (start us, length us, event | category | flops | bytes accessed | tf_op | source)
XLA Modules:
  0.0 137.6 jit_solution(12179241951312754078)
XLA Ops:
  0.7 0.7 multiply_bitcast_fusion
  1.5 2.0 %gather_fusion = s32[256]{0:T(256)S(1)} fusion(s32[256]{0:T(256)} %bitcast.42, s32[1024]{0:T(1024)S(1)} %pad_clamp_fusion), kind=kCustom, calls=%fused_computation | custom fusion | bytes 3072 | tf_op jit(solution)/shard_map/jit(_take)/gather | solution.py:54
  3.5 1.0 convolution_convert_fusion.2
  4.6 18.4 %all-to-all-start = ((bf16[16,16,384]{2,1,0:T(8,128)(2,1)}), bf16[16,16,384]{2,1,0:T(8,128)(2,1)S(1)}, u32[]{:S(2)}, u32[]{:S(2)}) async-start(bf16[16,16,384]{2,1,0:T(8,128)(2,1)} %bitcast.3), calls=%async_computation | async-start | bytes 393216 | tf_op jit(solution)/shard_map/all_to_all | solution.py:60
  23.0 0.8 pad_maximum_fusion.1
  23.8 27.2 %all-gather = bf16[192,1536]{1,0:T(8,128)(2,1)S(1)} all-gather(bf16[24,1536]{1,0:T(8,128)(2,1)S(1)} %pad_maximum_fusion.1), channel_id=2, replica_groups=mesh['dp'=16,'fy'=8,'fx'=4,'llm'=2] {'fy'}, dimensions={0}, use_global_device_ids=true | all-gather | bytes 663552 | tf_op jit(solution)/shard_map/all_gather | solution.py:70
  51.0 1.6 %broadcast_in_dim.21 = bf16[8,4,24,1536]{3,2,0,1:T(8,128)(2,1)} broadcast(bf16[8,24,1536]{2,1,0:T(8,128)(2,1)S(1)} %bitcast.46), dimensions={0,2,3} | broadcast | bytes 2949120 | tf_op jit(solution)/shard_map/broadcast_in_dim | solution.py:71
  52.6 4.4 %all-to-all-start.1 = ((bf16[8,4,24,1536]{3,2,0,1:T(8,128)(2,1)}), bf16[8,4,24,1536]{3,2,0,1:T(8,128)(2,1)S(1)}, u32[]{:S(2)}, u32[]{:S(2)}) async-start(bf16[8,4,24,1536]{3,2,0,1:T(8,128)(2,1)} %broadcast_in_dim.21), calls=%async_computation.1 | async-start | bytes 4718592 | tf_op jit(solution)/shard_map/all_to_all | solution.py:72
  57.0 5.6 %fusion.29 = (f32[4,8,8]{0,2,1:T(8,128)S(1)}, f32[4,8,8,768]{3,0,2,1:T(4,128)}) fusion(f32[7,7,1,768]{3,1,0,2:T(8,128)S(1)} %bitcast.51, bf16[4,8,8,768]{3,2,1,0:T(8,128)(2,1)} %bitcast.58), kind=kOutput, calls=%fused_computation.67 | convolution fusion | flops 71565056 | bytes 1331200 | tf_op jit(solution)/shard_map/conv_general_dilated | solution.py:11
  62.9 2.2 %copy.65 = f32[4,8,8,768]{3,2,1,0:T(8,128)} copy(f32[4,8,8,768]{3,0,2,1:T(4,128)} %get-tuple-element.15) | data formatting | bytes 1572864 | tf_op jit(solution)/shard_map/conv_general_dilated | solution.py:11
  65.1 1.5 %multiply_reduce_fusion = f32[4,8,8]{0,2,1:T(8,128)S(1)} fusion(f32[4,8,8,768]{3,0,2,1:T(4,128)} %get-tuple-element.15, f32[4,8,8]{0,2,1:T(8,128)S(1)} %copy.62), kind=kLoop, calls=%fused_computation.24 | loop fusion | flops 589568 | bytes 788480 | tf_op jit(solution)/shard_map/reduce_sum | solution.py:83
  67.6 1.9 %collective-permute-start = (bf16[256,384]{1,0:T(8,128)(2,1)S(1)}, bf16[256,384]{1,0:T(8,128)(2,1)}, u32[]{:S(2)}, u32[]{:S(2)}) collective-permute-start(bf16[256,384]{1,0:T(8,128)(2,1)S(1)} %bitcast_select_fusion), channel_id=1, source_target_pairs={{0,1},{1,0},{2,3},{3,2},{4,5},{5,4},{6,7},{7,6},{8,9},{9,8},{10,11... | collective-permute-start | bytes 589832 | tf_op jit(solution)/shard_map/ppermute | solution.py:63
  69.6 2.4 %fusion.20 = (bf16[768,256]{0,1:T(8,128)(2,1)}, f32[256,768]{1,0:T(8,128)}) fusion(f32[768]{0:T(1024)S(1)} %copy-done.9, f32[256]{0:T(256)S(1)} %rsqrt.12, f32[256]{0:T(256)S(1)} %div.32, f32[4,8,8,768]{3,2,1,0:T(8,128)} %copy.65), kind=kLoop, calls=%fused_computation.43 | loop fusion | flops 786432 | bytes 1971200 | tf_op jit(solution)/shard_map/dot_general | solution.py:93
  71.9 1.9 %copy.69 = bf16[768,256]{1,0:T(8,128)(2,1)} copy(bf16[768,256]{0,1:T(8,128)(2,1)} %get-tuple-element.5) | data formatting | bytes 786432 | tf_op jit(solution)/shard_map/dot_general | solution.py:93
  73.9 1.7 %broadcast_select_fusion.1 = (bf16[256,384]{1,0:T(8,128)(2,1)S(1)}, bf16[256,384]{1,0:T(8,128)(2,1)}) fusion(bf16[256,384]{1,0:T(8,128)(2,1)} %collective-permute-done, pred[]{:T(512)S(6)} %eq.25, bf16[16,16,384]{2,1,0:T(8,128)(2,1)S(1)} %all-to-all-done, pred[256]{0:T(512)(128)(4,1)S(1)} %fusion.22), kind=kLoop, calls=%fused_computation.41 | loop fusion | flops 294912 | bytes 786689 | tf_op jit(solution)/shard_map/jit(_where)/select_n | solution.py:64
  75.6 5.0 %all-to-all-done.1 = bf16[8,4,24,1536]{3,2,0,1:T(8,128)(2,1)S(1)} async-done(((bf16[8,4,24,1536]{3,2,0,1:T(8,128)(2,1)}), bf16[8,4,24,1536]{3,2,0,1:T(8,128)(2,1)S(1)}, u32[]{:S(2)}, u32[]{:S(2)}) %all-to-all-start.1) | async-done | bytes 2359328 | tf_op jit(solution)/shard_map/all_to_all | solution.py:72
  80.8 0.9 copy-done.2
  84.6 1.6 %copy.70 = bf16[8,4,24,1536]{3,2,0,1:T(8,128)(2,1)} copy(bf16[8,4,24,1536]{3,2,1,0:T(8,128)(2,1)S(1)} %pad_maximum_fusion) | data formatting | bytes 4718592 | tf_op jit(solution)/shard_map/concatenate | solution.py:99
  86.2 3.6 %all-to-all-start.2 = ((bf16[8,4,24,1536]{3,2,0,1:T(8,128)(2,1)}), bf16[8,4,24,1536]{3,2,0,1:T(8,128)(2,1)S(1)}, u32[]{:S(2)}, u32[]{:S(2)}) async-start(bf16[8,4,24,1536]{3,2,0,1:T(8,128)(2,1)} %copy.70), calls=%async_computation.2 | async-start | bytes 4718592 | tf_op jit(solution)/shard_map/all_to_all | solution.py:101
  89.9 2.0 %fusion.2 = f32[256,768]{1,0:T(8,128)S(1)} fusion(bf16[256,768]{1,0:T(8,128)(2,1)} %copy-done.4, bf16[768,1536]{1,0:T(8,128)(2,1)} %bitcast.45), kind=kOutput, calls=%fused_computation.10 | convolution fusion | flops 301989888 | bytes 2359296 | tf_op jit(solution)/shard_map/dot_general | solution.py:108
  91.9 1.9 %collective-permute-start.1 = (bf16[256,384]{1,0:T(8,128)(2,1)S(1)}, bf16[256,384]{1,0:T(8,128)(2,1)S(1)}, u32[]{:S(2)}, u32[]{:S(2)}) collective-permute-start(bf16[256,384]{1,0:T(8,128)(2,1)S(1)} %select_convert_fusion), channel_id=1, source_target_pairs={{0,1},{1,0},{2,3},{3,2},{4,5},{5,4},{6,7},{7,6},{8,9},{9,8},{10,11... | collective-permute-start | bytes 589832 | tf_op jit(solution)/shard_map/ppermute | solution.py:115
  93.9 1.3 collective-permute-done.1
  95.3 0.8 fusion.27
  96.1 2.0 %collective-permute-start.2 = (f32[256,2]{0,1:T(2,128)S(1)}, f32[256,2]{0,1:T(2,128)S(1)}, u32[]{:S(2)}, u32[]{:S(2)}) collective-permute-start(f32[256,2]{0,1:T(2,128)S(1)} %pad_maximum_fusion.2), channel_id=1, source_target_pairs={{0,1},{1,0},{2,3},{3,2},{4,5},{5,4},{6,7},{7,6},{8,9},{9,8},{10,11... | collective-permute-start | bytes 6152 | tf_op jit(solution)/shard_map/ppermute | solution.py:123
  98.3 17.5 %all-to-all-done.2 = bf16[8,4,24,1536]{3,2,0,1:T(8,128)(2,1)S(1)} async-done(((bf16[8,4,24,1536]{3,2,0,1:T(8,128)(2,1)}), bf16[8,4,24,1536]{3,2,0,1:T(8,128)(2,1)S(1)}, u32[]{:S(2)}, u32[]{:S(2)}) %all-to-all-start.2) | async-done | bytes 2359328 | tf_op jit(solution)/shard_map/all_to_all | solution.py:101
  115.9 1.3 reduce_sum.61
  117.2 5.5 %all-to-all-start.3 = ((bf16[8,24,1536]{2,1,0:T(8,128)(2,1)}), bf16[8,24,1536]{2,1,0:T(8,128)(2,1)S(1)}, u32[]{:S(2)}, u32[]{:S(2)}) async-start(bf16[8,24,1536]{2,1,0:T(8,128)(2,1)} %reduce_sum.61), calls=%async_computation.3 | async-start | bytes 1179648 | tf_op jit(solution)/shard_map/all_to_all | solution.py:103
  122.7 1.3 subtract_multiply_fusion
  124.0 1.6 %fusion.13 = f32[4,8,8,384]{3,0,2,1:T(4,128)S(1)} fusion(f32[4,8,8,384]{3,2,1,0:T(8,128)S(1)} %bitcast.47, f32[7,7,1,384]{3,1,0,2:T(8,128)S(1)} %bitcast.50), kind=kOutput, calls=%fused_computation.29 | convolution fusion | flops 35684352 | bytes 861696 | tf_op jit(solution)/shard_map/conv_general_dilated | solution.py:11
  125.6 0.8 fusion.12
  126.4 10.4 %all-to-all-done.3 = bf16[8,24,1536]{2,1,0:T(8,128)(2,1)S(1)} async-done(((bf16[8,24,1536]{2,1,0:T(8,128)(2,1)}), bf16[8,24,1536]{2,1,0:T(8,128)(2,1)S(1)}, u32[]{:S(2)}, u32[]{:S(2)}) %all-to-all-start.3) | async-done | bytes 589856 | tf_op jit(solution)/shard_map/all_to_all | solution.py:103
  136.9 0.7 slice_multiply_fusion
  (51 shorter events, 4.3 us)
Async XLA Ops:
  0.6 2.9 %copy-start = (bf16[512,768]{1,0:T(8,128)(2,1)S(1)}, bf16[512,768]{1,0:T(8,128)(2,1)}, u32[]{:S(2)}) copy-start(bf16[512,768]{1,0:T(8,128)(2,1)} %param.11) | copy-start | bytes 2359300
  4.6 46.4 %all-to-all-start = ((bf16[16,16,384]{2,1,0:T(8,128)(2,1)}), bf16[16,16,384]{2,1,0:T(8,128)(2,1)S(1)}, u32[]{:S(2)}, u32[]{:S(2)}) async-start(bf16[16,16,384]{2,1,0:T(8,128)(2,1)} %bitcast.3), calls=%async_computation | async-start | bytes 393216 | tf_op jit(solution)/shard_map/all_to_all | solution.py:60
  52.6 4.4 %copy-start.7 = (f32[7,7,768]{2,1,0:T(8,128)S(1)}, f32[7,7,768]{2,1,0:T(8,128)}, u32[]{:S(2)}) copy-start(f32[7,7,768]{2,1,0:T(8,128)} %param.15) | copy-start | bytes 451588
  52.6 28.0 %all-to-all-start.1 = ((bf16[8,4,24,1536]{3,2,0,1:T(8,128)(2,1)}), bf16[8,4,24,1536]{3,2,0,1:T(8,128)(2,1)S(1)}, u32[]{:S(2)}, u32[]{:S(2)}) async-start(bf16[8,4,24,1536]{3,2,0,1:T(8,128)(2,1)} %broadcast_in_dim.21), calls=%async_computation.1 | async-start | bytes 4718592 | tf_op jit(solution)/shard_map/all_to_all | solution.py:72
  57.0 12.5 %copy-start.9 = (f32[768]{0:T(1024)S(1)}, f32[768]{0:T(1024)}, u32[]{:S(2)}) copy-start(f32[768]{0:T(1024)} %param.16) | copy-start | bytes 9220
  67.6 6.3 %collective-permute-start = (bf16[256,384]{1,0:T(8,128)(2,1)S(1)}, bf16[256,384]{1,0:T(8,128)(2,1)}, u32[]{:S(2)}, u32[]{:S(2)}) collective-permute-start(bf16[256,384]{1,0:T(8,128)(2,1)S(1)} %bitcast_select_fusion), channel_id=1, source_target_pairs={{0,1},{1,0},{2,3},{3,2},{4,5},{5,4},{6,7},{7,6},{8,9},{9,8},{10,11... | collective-permute-start | bytes 589832 | tf_op jit(solution)/shard_map/ppermute | solution.py:63
  80.6 1.1 copy-start.2
  80.8 2.0 %copy-start.1 = (bf16[8,4,24,1536]{3,2,1,0:T(8,128)(2,1)}, bf16[8,4,24,1536]{3,2,1,0:T(8,128)(2,1)S(1)}, u32[]{:S(2)}) copy-start(bf16[8,4,24,1536]{3,2,1,0:T(8,128)(2,1)S(1)} %copy.64) | copy-start | bytes 7077892
  80.8 1.4 %copy-start.6 = (bf16[256,384]{1,0:T(8,128)(2,1)S(1)}, bf16[256,384]{1,0:T(8,128)(2,1)}, u32[]{:S(2)}) copy-start(bf16[256,384]{1,0:T(8,128)(2,1)} %get-tuple-element.9) | copy-start | bytes 589828
  80.8 1.4 %copy-start.10 = (f32[768]{0:T(1024)S(1)}, f32[768]{0:T(1024)}, u32[]{:S(2)}) copy-start(f32[768]{0:T(1024)} %param.17) | copy-start | bytes 9220
  82.8 1.6 %copy-start.4 = (bf16[256,768]{1,0:T(8,128)(2,1)}, bf16[256,768]{1,0:T(8,128)(2,1)S(1)}, u32[]{:S(2)}) copy-start(bf16[256,768]{1,0:T(8,128)(2,1)S(1)} %fusion) | copy-start | bytes 1179652
  82.8 1.1 copy-start.5
  86.2 29.6 %all-to-all-start.2 = ((bf16[8,4,24,1536]{3,2,0,1:T(8,128)(2,1)}), bf16[8,4,24,1536]{3,2,0,1:T(8,128)(2,1)S(1)}, u32[]{:S(2)}, u32[]{:S(2)}) async-start(bf16[8,4,24,1536]{3,2,0,1:T(8,128)(2,1)} %copy.70), calls=%async_computation.2 | async-start | bytes 4718592 | tf_op jit(solution)/shard_map/all_to_all | solution.py:101
  89.9 5.4 %copy-start.3 = (f32[256,768]{1,0:T(8,128)S(1)}, f32[256,768]{1,0:T(8,128)}, u32[]{:S(2)}) copy-start(f32[256,768]{1,0:T(8,128)} %get-tuple-element.6) | copy-start | bytes 2359300
  89.9 8.3 %copy-start.8 = (f32[7,7,768]{2,1,0:T(8,128)S(1)}, f32[7,7,768]{2,1,0:T(8,128)}, u32[]{:S(2)}) copy-start(f32[7,7,768]{2,1,0:T(8,128)} %param.15) | copy-start | bytes 451588
  91.9 3.3 %collective-permute-start.1 = (bf16[256,384]{1,0:T(8,128)(2,1)S(1)}, bf16[256,384]{1,0:T(8,128)(2,1)S(1)}, u32[]{:S(2)}, u32[]{:S(2)}) collective-permute-start(bf16[256,384]{1,0:T(8,128)(2,1)S(1)} %select_convert_fusion), channel_id=1, source_target_pairs={{0,1},{1,0},{2,3},{3,2},{4,5},{5,4},{6,7},{7,6},{8,9},{9,8},{10,11... | collective-permute-start | bytes 589832 | tf_op jit(solution)/shard_map/ppermute | solution.py:115
  96.1 26.5 %collective-permute-start.2 = (f32[256,2]{0,1:T(2,128)S(1)}, f32[256,2]{0,1:T(2,128)S(1)}, u32[]{:S(2)}, u32[]{:S(2)}) collective-permute-start(f32[256,2]{0,1:T(2,128)S(1)} %pad_maximum_fusion.2), channel_id=1, source_target_pairs={{0,1},{1,0},{2,3},{3,2},{4,5},{5,4},{6,7},{7,6},{8,9},{9,8},{10,11... | collective-permute-start | bytes 6152 | tf_op jit(solution)/shard_map/ppermute | solution.py:123
  117.2 19.7 %all-to-all-start.3 = ((bf16[8,24,1536]{2,1,0:T(8,128)(2,1)}), bf16[8,24,1536]{2,1,0:T(8,128)(2,1)S(1)}, u32[]{:S(2)}, u32[]{:S(2)}) async-start(bf16[8,24,1536]{2,1,0:T(8,128)(2,1)} %reduce_sum.61), calls=%async_computation.3 | async-start | bytes 1179648 | tf_op jit(solution)/shard_map/all_to_all | solution.py:103

commit v9 on v8

--- a/solution.py
+++ b/solution.py
@@ -23,6 +23,11 @@
     cumulative = 0.5 * (1.0 + lax.erf(hidden_in * 0.7071067811865476))
     density = jnp.exp(-0.5 * hidden_in * hidden_in) * 0.3989422804014327
     return (hidden_in * cumulative, cumulative + hidden_in * density)
+
+
+def rows_xy(values, height, width):
+    grid = values.reshape((height, width, -1) + values.shape[1:])
+    return jnp.swapaxes(grid, 0, 1).reshape(values.shape)
 
 
 SWAP = [(0, 1), (1, 0)]
@@ -90,16 +95,16 @@
     grad_hidden = jnp.dot(scaled, w_out_full, preferred_element_type=jnp.float32)
     grad_pre = (grad_hidden * slope).astype(jnp.bfloat16)
 
-    term_in = lax.dot_general(
-        normed, grad_pre, (((0,), (0,)), ((), ())), preferred_element_type=jnp.float32
+    term_in = jnp.dot(
+        rows_xy(normed.T, height, width), grad_pre, preferred_element_type=jnp.float32
     )
-    term_out = lax.dot_general(
-        scaled, hidden, (((0,), (0,)), ((), ())), preferred_element_type=jnp.float32
+    term_out = jnp.dot(
+        rows_xy(scaled.T, height, width), hidden, preferred_element_type=jnp.float32
     )
     terms = jnp.concatenate([term_in, term_out], axis=1).astype(jnp.bfloat16)
-    terms = terms.reshape(height, width, channels // shards, 2 * hid)
-    x_parts = lax.all_to_all(terms, "fx", split_axis=1, concat_axis=1, tiled=True)
-    x_sums = jnp.sum(x_parts.astype(jnp.float32), axis=1).astype(jnp.bfloat16)
+    terms = terms.reshape(width, height, channels // shards, 2 * hid)
+    x_parts = lax.all_to_all(terms, "fx", split_axis=0, concat_axis=0, tiled=True)
+    x_sums = jnp.sum(x_parts.astype(jnp.float32), axis=0).astype(jnp.bfloat16)
     y_parts = lax.all_to_all(x_sums, "fy", split_axis=0, concat_axis=0, tiled=True)
     totals = jnp.sum(y_parts.astype(jnp.float32), axis=0)
     grad_in = totals[:, :hid] / ACCUM

time: 139 us -> 145 us (1.043)
  waiting for transfers between devices: 34.2 us -> 37.6 us
  local copies, waits for them, and re-layouts: 11.9 us -> 13.5 us
  other arithmetic: 12.6 us -> 14.1 us
    transpose x0 -> x2, local copies, waits for them, and re-layouts: none -> 3.85 us  [the longest x1 1.94 us: body(): term_out = jnp.dot(rows_xy(scaled.T, height, width), hidden, preferred_el...]
    all_to_all x1, waiting for transfers between devices: 17.5 us -> 20.9 us  [body(): lax.all_to_all(terms, 'fx', split_axis=0, concat_axis=0, tiled=True)]
    all_to_all x1, waiting for transfers between devices: 4.97 us -> 1.64 us  [body(): lax.all_to_all(x_tiled, 'fx', split_axis=1, concat_axis=1, tiled=True)]
    all_to_all x1, waiting for transfers between devices: 10.4 us -> 13.7 us  [body(): lax.all_to_all(x_sums, 'fy', split_axis=0, concat_axis=0, tiled=True)]
    transpose x0 -> x2, other arithmetic: none -> 3.2 us  [the longest x1 2.39 us: body(): term_in = jnp.dot(rows_xy(normed.T, height, width), grad_pre, preferred_e...]
    dot_general x1 -> x0, other arithmetic: 2.39 us -> none  [body(): lax.dot_general(normed, grad_pre, (((0,), (0,)), ((), ())), preferred_ele...]
    dot_general x1 -> x0, local copies, waits for them, and re-layouts: 1.92 us -> none  [body(): lax.dot_general(normed, grad_pre, (((0,), (0,)), ((), ())), preferred_ele...]
    concatenate x1 -> x0, local copies, waits for them, and re-layouts: 1.62 us -> none  [body(): terms = jnp.concatenate([term_in, term_out], axis=1).astype(jnp.bfloat16)]
  transfers between devices with their start and end apart: 7 -> 7, of which waited for: 4 -> 4; matrix products, arithmetic and copies ran while one was open for 18% -> 19% of each run, Pallas kernels for 0% -> 0%
where the time goes in v9:
time: 145 us; the launch traced here: 144 us
  starting transfers between devices  37.8 us (26%)
  waiting for transfers between devices  37.6 us (26%)
  blocking collectives  27.2 us (19%)
  other arithmetic  14.1 us (10%)
  local copies, waits for them, and re-layouts  13.5 us (9%)
  matrix products  12.2 us (8%)
  between operations  1.6 us (1%)
    all_gather x1, blocking collectives, body(): y_block = lax.all_gather(both, 'fy', axis=0)  27.2 us
    all_to_all x1, waiting for transfers between devices, body(): lax.all_to_all(terms, 'fx', split_axis=0, concat_axis=0, tiled=True)  20.9 us
    all_to_all x1, starting transfers between devices, body(): lax.all_to_all(out_half, 'dp', split_axis=0, concat_axis=0, tiled=True)  18.4 us
    all_to_all x1, waiting for transfers between devices, body(): lax.all_to_all(x_sums, 'fy', split_axis=0, concat_axis=0, tiled=True)  13.7 us
    conv_general_dilated x2, matrix products, depthwise(): lax.conv_general_dilated(images, kernel[:, :, None, :], (1, 1), 'SAME', d...  7.2 us
    all_to_all x1, starting transfers between devices, body(): lax.all_to_all(x_sums, 'fy', split_axis=0, concat_axis=0, tiled=True)  5.46 us
    all_to_all x1, starting transfers between devices, body(): lax.all_to_all(x_tiled, 'fx', split_axis=1, concat_axis=1, tiled=True)  4.43 us
    all_to_all x1, starting transfers between devices, body(): lax.all_to_all(terms, 'fx', split_axis=0, concat_axis=0, tiled=True)  3.63 us
  transfers between devices with their start and end apart: 7, of which 4 were waited for; matrix products, arithmetic and copies ran while one was open for 19% of the time, Pallas kernels for 0%

profile of v9, /device:TPU:64, one launch (start us, length us, event | category | flops | bytes accessed | tf_op | source)
XLA Modules:
  0.0 144.1 jit_solution(769824047637645598)
XLA Ops:
  1.5 2.0 %gather_fusion = s32[256]{0:T(256)S(1)} fusion(s32[256]{0:T(256)} %bitcast.52, s32[1024]{0:T(1024)S(1)} %pad_clamp_fusion), kind=kCustom, calls=%fused_computation | custom fusion | bytes 3072 | tf_op jit(solution)/shard_map/jit(_take)/gather | solution.py:59
  3.5 1.0 convolution_convert_fusion.2
  4.6 18.4 %all-to-all-start = ((bf16[16,16,384]{2,1,0:T(8,128)(2,1)}), bf16[16,16,384]{2,1,0:T(8,128)(2,1)S(1)}, u32[]{:S(2)}, u32[]{:S(2)}) async-start(bf16[16,16,384]{2,1,0:T(8,128)(2,1)} %bitcast.3), calls=%async_computation | async-start | bytes 393216 | tf_op jit(solution)/shard_map/all_to_all | solution.py:65
  23.0 0.8 pad_maximum_fusion.1
  23.8 27.2 %all-gather = bf16[192,1536]{1,0:T(8,128)(2,1)S(1)} all-gather(bf16[24,1536]{1,0:T(8,128)(2,1)S(1)} %pad_maximum_fusion.1), channel_id=2, replica_groups=mesh['dp'=16,'fy'=8,'fx'=4,'llm'=2] {'fy'}, dimensions={0}, use_global_device_ids=true | all-gather | bytes 663552 | tf_op jit(solution)/shard_map/all_gather | solution.py:75
  51.0 1.6 %broadcast_in_dim.21 = bf16[8,4,24,1536]{3,2,0,1:T(8,128)(2,1)} broadcast(bf16[8,24,1536]{2,1,0:T(8,128)(2,1)S(1)} %bitcast.56), dimensions={0,2,3} | broadcast | bytes 2949120 | tf_op jit(solution)/shard_map/broadcast_in_dim | solution.py:76
  52.6 4.4 %all-to-all-start.1 = ((bf16[8,4,24,1536]{3,2,0,1:T(8,128)(2,1)}), bf16[8,4,24,1536]{3,2,0,1:T(8,128)(2,1)S(1)}, u32[]{:S(2)}, u32[]{:S(2)}) async-start(bf16[8,4,24,1536]{3,2,0,1:T(8,128)(2,1)} %broadcast_in_dim.21), calls=%async_computation.1 | async-start | bytes 4718592 | tf_op jit(solution)/shard_map/all_to_all | solution.py:77
  57.0 5.6 %fusion.33 = (f32[4,8,8]{0,2,1:T(8,128)S(1)}, f32[4,8,8,768]{3,0,2,1:T(4,128)}) fusion(f32[7,7,1,768]{3,1,0,2:T(8,128)S(1)} %bitcast.61, bf16[4,8,8,768]{3,2,1,0:T(8,128)(2,1)} %bitcast.68), kind=kOutput, calls=%fused_computation.70 | convolution fusion | flops 71565056 | bytes 1331200 | tf_op jit(solution)/shard_map/conv_general_dilated | solution.py:11
  63.5 2.2 %copy.75 = f32[4,8,8,768]{3,2,1,0:T(8,128)} copy(f32[4,8,8,768]{3,0,2,1:T(4,128)} %get-tuple-element.15) | data formatting | bytes 1572864 | tf_op jit(solution)/shard_map/conv_general_dilated | solution.py:11
  65.7 1.5 %multiply_reduce_fusion = f32[4,8,8]{0,2,1:T(8,128)S(1)} fusion(f32[4,8,8,768]{3,0,2,1:T(4,128)} %get-tuple-element.15, f32[4,8,8]{0,2,1:T(8,128)S(1)} %copy.72), kind=kLoop, calls=%fused_computation.24 | loop fusion | flops 589568 | bytes 788480 | tf_op jit(solution)/shard_map/reduce_sum | solution.py:88
  68.2 1.9 %collective-permute-start = (bf16[256,384]{1,0:T(8,128)(2,1)S(1)}, bf16[256,384]{1,0:T(8,128)(2,1)}, u32[]{:S(2)}, u32[]{:S(2)}) collective-permute-start(bf16[256,384]{1,0:T(8,128)(2,1)S(1)} %bitcast_select_fusion), channel_id=1, source_target_pairs={{0,1},{1,0},{2,3},{3,2},{4,5},{5,4},{6,7},{7,6},{8,9},{9,8},{10,11... | collective-permute-start | bytes 589832 | tf_op jit(solution)/shard_map/ppermute | solution.py:68
  70.2 2.4 %fusion.25 = (bf16[768,256]{0,1:T(8,128)(2,1)}, f32[256,768]{1,0:T(8,128)}) fusion(f32[768]{0:T(1024)S(1)} %copy-done.11, f32[256]{0:T(256)S(1)} %rsqrt.12, f32[256]{0:T(256)} %div.32, f32[4,8,8,768]{3,2,1,0:T(8,128)} %copy.75), kind=kLoop, calls=%fused_computation.47 | loop fusion | flops 786432 | bytes 1971200 | tf_op jit(solution)/shard_map/transpose | solution.py:99
  72.5 1.9 %copy.79 = bf16[768,256]{1,0:T(8,128)(2,1)} copy(bf16[768,256]{0,1:T(8,128)(2,1)} %get-tuple-element.5) | data formatting | bytes 786432 | tf_op jit(solution)/shard_map/transpose | solution.py:99
  74.5 1.1 broadcast_select_fusion.1
  76.2 0.8 fusion.23
  77.0 1.9 %copy.81 = bf16[768,256]{1,0:T(8,128)(2,1)} copy(bf16[768,256]{0,1:T(8,128)(2,1)} %fusion.23) | data formatting | bytes 786432 | tf_op jit(solution)/shard_map/transpose | solution.py:102
  78.9 1.6 %all-to-all-done.1 = bf16[8,4,24,1536]{3,2,0,1:T(8,128)(2,1)S(1)} async-done(((bf16[8,4,24,1536]{3,2,0,1:T(8,128)(2,1)}), bf16[8,4,24,1536]{3,2,0,1:T(8,128)(2,1)S(1)}, u32[]{:S(2)}, u32[]{:S(2)}) %all-to-all-start.1) | async-done | bytes 2359328 | tf_op jit(solution)/shard_map/all_to_all | solution.py:77
  80.8 0.9 copy-done.2
  84.5 1.6 %pad_maximum_fusion = bf16[4,8,24,1536]{3,2,1,0:T(8,128)(2,1)} fusion(bf16[4,8,24,768]{3,2,1,0:T(8,128)(2,1)S(1)} %convolution_convert_fusion, bf16[4,8,24,768]{3,2,1,0:T(8,128)(2,1)S(1)} %convolution_convert_fusion.1), kind=kLoop, calls=%fused_computation.1 | loop fusion | flops 4718592 | bytes 4718592 | tf_op jit(solution)/shard_map/concatenate | solution.py:104
  86.1 3.6 %all-to-all-start.2 = ((bf16[4,8,24,1536]{3,2,1,0:T(8,128)(2,1)}), bf16[4,8,24,1536]{3,2,1,0:T(8,128)(2,1)S(1)}, u32[]{:S(2)}, u32[]{:S(2)}) async-start(bf16[4,8,24,1536]{3,2,1,0:T(8,128)(2,1)} %pad_maximum_fusion), calls=%async_computation.2 | async-start | bytes 4718592 | tf_op jit(solution)/shard_map/all_to_all | solution.py:106
  89.7 2.0 %fusion.2 = f32[256,768]{1,0:T(8,128)S(1)} fusion(bf16[256,768]{1,0:T(8,128)(2,1)} %copy-done.5, bf16[768,1536]{1,0:T(8,128)(2,1)} %bitcast.55), kind=kOutput, calls=%fused_computation.10 | convolution fusion | flops 301989888 | bytes 2359296 | tf_op jit(solution)/shard_map/dot_general | solution.py:113
  91.8 1.9 %collective-permute-start.1 = (bf16[256,384]{1,0:T(8,128)(2,1)S(1)}, bf16[256,384]{1,0:T(8,128)(2,1)S(1)}, u32[]{:S(2)}, u32[]{:S(2)}) collective-permute-start(bf16[256,384]{1,0:T(8,128)(2,1)S(1)} %select_convert_fusion), channel_id=1, source_target_pairs={{0,1},{1,0},{2,3},{3,2},{4,5},{5,4},{6,7},{7,6},{8,9},{9,8},{10,11... | collective-permute-start | bytes 589832 | tf_op jit(solution)/shard_map/ppermute | solution.py:120
  93.8 1.3 collective-permute-done.1
  95.1 0.8 fusion.31
  95.9 2.0 %collective-permute-start.2 = (f32[256,2]{0,1:T(2,128)S(1)}, f32[256,2]{0,1:T(2,128)S(1)}, u32[]{:S(2)}, u32[]{:S(2)}) collective-permute-start(f32[256,2]{0,1:T(2,128)S(1)} %pad_maximum_fusion.2), channel_id=1, source_target_pairs={{0,1},{1,0},{2,3},{3,2},{4,5},{5,4},{6,7},{7,6},{8,9},{9,8},{10,11... | collective-permute-start | bytes 6152 | tf_op jit(solution)/shard_map/ppermute | solution.py:128
  98.1 20.9 %all-to-all-done.2 = bf16[4,8,24,1536]{3,2,1,0:T(8,128)(2,1)S(1)} async-done(((bf16[4,8,24,1536]{3,2,1,0:T(8,128)(2,1)}), bf16[4,8,24,1536]{3,2,1,0:T(8,128)(2,1)S(1)}, u32[]{:S(2)}, u32[]{:S(2)}) %all-to-all-start.2) | async-done | bytes 2359328 | tf_op jit(solution)/shard_map/all_to_all | solution.py:106
  119.0 1.3 reduce_sum.61
  120.3 5.5 %all-to-all-start.3 = ((bf16[8,24,1536]{2,1,0:T(8,128)(2,1)}), bf16[8,24,1536]{2,1,0:T(8,128)(2,1)S(1)}, u32[]{:S(2)}, u32[]{:S(2)}) async-start(bf16[8,24,1536]{2,1,0:T(8,128)(2,1)} %reduce_sum.61), calls=%async_computation.3 | async-start | bytes 1179648 | tf_op jit(solution)/shard_map/all_to_all | solution.py:108
  125.8 1.3 subtract_multiply_fusion
  127.1 1.6 %fusion.17 = f32[4,8,8,384]{3,0,2,1:T(4,128)S(1)} fusion(f32[4,8,8,384]{3,2,1,0:T(8,128)S(1)} %bitcast.58, f32[7,7,1,384]{3,1,0,2:T(8,128)S(1)} %bitcast.60), kind=kOutput, calls=%fused_computation.32 | convolution fusion | flops 35684352 | bytes 861696 | tf_op jit(solution)/shard_map/conv_general_dilated | solution.py:11
  128.8 0.8 fusion.14
  129.6 13.7 %all-to-all-done.3 = bf16[8,24,1536]{2,1,0:T(8,128)(2,1)S(1)} async-done(((bf16[8,24,1536]{2,1,0:T(8,128)(2,1)}), bf16[8,24,1536]{2,1,0:T(8,128)(2,1)S(1)}, u32[]{:S(2)}, u32[]{:S(2)}) %all-to-all-start.3) | async-done | bytes 589856 | tf_op jit(solution)/shard_map/all_to_all | solution.py:108
  (56 shorter events, 6.8 us)
Async XLA Ops:
  0.6 2.9 %copy-start = (bf16[512,768]{1,0:T(8,128)(2,1)S(1)}, bf16[512,768]{1,0:T(8,128)(2,1)}, u32[]{:S(2)}) copy-start(bf16[512,768]{1,0:T(8,128)(2,1)} %param.11) | copy-start | bytes 2359300
  4.6 46.4 %all-to-all-start = ((bf16[16,16,384]{2,1,0:T(8,128)(2,1)}), bf16[16,16,384]{2,1,0:T(8,128)(2,1)S(1)}, u32[]{:S(2)}, u32[]{:S(2)}) async-start(bf16[16,16,384]{2,1,0:T(8,128)(2,1)} %bitcast.3), calls=%async_computation | async-start | bytes 393216 | tf_op jit(solution)/shard_map/all_to_all | solution.py:65
  52.6 4.4 %copy-start.9 = (f32[7,7,768]{2,1,0:T(8,128)S(1)}, f32[7,7,768]{2,1,0:T(8,128)}, u32[]{:S(2)}) copy-start(f32[7,7,768]{2,1,0:T(8,128)} %param.15) | copy-start | bytes 451588
  52.6 28.0 %all-to-all-start.1 = ((bf16[8,4,24,1536]{3,2,0,1:T(8,128)(2,1)}), bf16[8,4,24,1536]{3,2,0,1:T(8,128)(2,1)S(1)}, u32[]{:S(2)}, u32[]{:S(2)}) async-start(bf16[8,4,24,1536]{3,2,0,1:T(8,128)(2,1)} %broadcast_in_dim.21), calls=%async_computation.1 | async-start | bytes 4718592 | tf_op jit(solution)/shard_map/all_to_all | solution.py:77
  57.0 13.1 %copy-start.11 = (f32[768]{0:T(1024)S(1)}, f32[768]{0:T(1024)}, u32[]{:S(2)}) copy-start(f32[768]{0:T(1024)} %param.16) | copy-start | bytes 9220
  65.7 10.5 %copy-start.12 = (f32[768]{0:T(1024)S(1)}, f32[768]{0:T(1024)}, u32[]{:S(2)}) copy-start(f32[768]{0:T(1024)} %param.17) | copy-start | bytes 9220
  68.2 6.2 %collective-permute-start = (bf16[256,384]{1,0:T(8,128)(2,1)S(1)}, bf16[256,384]{1,0:T(8,128)(2,1)}, u32[]{:S(2)}, u32[]{:S(2)}) collective-permute-start(bf16[256,384]{1,0:T(8,128)(2,1)S(1)} %bitcast_select_fusion), channel_id=1, source_target_pairs={{0,1},{1,0},{2,3},{3,2},{4,5},{5,4},{6,7},{7,6},{8,9},{9,8},{10,11... | collective-permute-start | bytes 589832 | tf_op jit(solution)/shard_map/ppermute | solution.py:68
  75.5 0.7 copy-start.7
  80.6 1.1 copy-start.2
  80.8 2.0 %copy-start.1 = (bf16[8,4,24,1536]{3,2,1,0:T(8,128)(2,1)}, bf16[8,4,24,1536]{3,2,1,0:T(8,128)(2,1)S(1)}, u32[]{:S(2)}) copy-start(bf16[8,4,24,1536]{3,2,1,0:T(8,128)(2,1)S(1)} %copy.74) | copy-start | bytes 7077892
  80.8 1.4 copy-start.8
  82.2 1.0 copy-start.4
  82.8 0.9 copy-start.5
  82.8 1.2 copy-start.6
  86.1 33.0 %all-to-all-start.2 = ((bf16[4,8,24,1536]{3,2,1,0:T(8,128)(2,1)}), bf16[4,8,24,1536]{3,2,1,0:T(8,128)(2,1)S(1)}, u32[]{:S(2)}, u32[]{:S(2)}) async-start(bf16[4,8,24,1536]{3,2,1,0:T(8,128)(2,1)} %pad_maximum_fusion), calls=%async_computation.2 | async-start | bytes 4718592 | tf_op jit(solution)/shard_map/all_to_all | solution.py:106
  89.7 5.4 %copy-start.3 = (f32[256,768]{1,0:T(8,128)S(1)}, f32[256,768]{1,0:T(8,128)}, u32[]{:S(2)}) copy-start(f32[256,768]{1,0:T(8,128)} %get-tuple-element.6) | copy-start | bytes 2359300
  89.7 8.3 %copy-start.10 = (f32[7,7,768]{2,1,0:T(8,128)S(1)}, f32[7,7,768]{2,1,0:T(8,128)}, u32[]{:S(2)}) copy-start(f32[7,7,768]{2,1,0:T(8,128)} %param.15) | copy-start | bytes 451588
  91.8 3.3 %collective-permute-start.1 = (bf16[256,384]{1,0:T(8,128)(2,1)S(1)}, bf16[256,384]{1,0:T(8,128)(2,1)S(1)}, u32[]{:S(2)}, u32[]{:S(2)}) collective-permute-start(bf16[256,384]{1,0:T(8,128)(2,1)S(1)} %select_convert_fusion), channel_id=1, source_target_pairs={{0,1},{1,0},{2,3},{3,2},{4,5},{5,4},{6,7},{7,6},{8,9},{9,8},{10,11... | collective-permute-start | bytes 589832 | tf_op jit(solution)/shard_map/ppermute | solution.py:120
  95.9 29.9 %collective-permute-start.2 = (f32[256,2]{0,1:T(2,128)S(1)}, f32[256,2]{0,1:T(2,128)S(1)}, u32[]{:S(2)}, u32[]{:S(2)}) collective-permute-start(f32[256,2]{0,1:T(2,128)S(1)} %pad_maximum_fusion.2), channel_id=1, source_target_pairs={{0,1},{1,0},{2,3},{3,2},{4,5},{5,4},{6,7},{7,6},{8,9},{9,8},{10,11... | collective-permute-start | bytes 6152 | tf_op jit(solution)/shard_map/ppermute | solution.py:128
  120.3 23.0 %all-to-all-start.3 = ((bf16[8,24,1536]{2,1,0:T(8,128)(2,1)}), bf16[8,24,1536]{2,1,0:T(8,128)(2,1)S(1)}, u32[]{:S(2)}, u32[]{:S(2)}) async-start(bf16[8,24,1536]{2,1,0:T(8,128)(2,1)} %reduce_sum.61), calls=%async_computation.3 | async-start | bytes 1179648 | tf_op jit(solution)/shard_map/all_to_all | solution.py:108

commit v10 on v8

--- a/solution.py
+++ b/solution.py
@@ -51,7 +51,8 @@
     core_index = lax.axis_index("llm")
 
     flat = (assign[0][:, None] * block_rows + jnp.arange(block_rows)[None, :]).reshape(row_count)
-    source_rows = jnp.take(visual_pos, flat, axis=1, mode="clip")[0]
+    chosen = flat[:, None] == jnp.arange(visual_pos.shape[1])[None, :]
+    source_rows = jnp.sum(jnp.where(chosen, visual_pos, 0), axis=1)
     seq_half = lax.dynamic_slice_in_dim(grad_seq, core_index * half_width, half_width, 1)
     pick = source_rows[:, None] == jnp.arange(grad_seq.shape[0])[None, :]
     out_half = jnp.dot(

time: 139 us -> 137 us (0.986)
  local copies, waits for them, and re-layouts: 11.9 us -> 9.84 us
    gather x1 -> x0, local copies, waits for them, and re-layouts: 1.98 us -> none  [body(): source_rows = jnp.take(visual_pos, flat, axis=1, mode='clip')[0]]
where the time goes in v10:
time: 137 us; the launch traced here: 136 us
  starting transfers between devices  37.8 us (28%)
  waiting for transfers between devices  34.2 us (25%)
  blocking collectives  27.2 us (20%)
  other arithmetic  13.3 us (10%)
  matrix products  12.3 us (9%)
  local copies, waits for them, and re-layouts  9.84 us (7%)
  between operations  1.62 us (1%)
    all_gather x1, blocking collectives, body(): y_block = lax.all_gather(both, 'fy', axis=0)  27.2 us
    all_to_all x1, starting transfers between devices, body(): lax.all_to_all(out_half, 'dp', split_axis=0, concat_axis=0, tiled=True)  18.4 us
    all_to_all x1, waiting for transfers between devices, body(): lax.all_to_all(terms, 'fx', split_axis=1, concat_axis=1, tiled=True)  17.5 us
    all_to_all x1, waiting for transfers between devices, body(): lax.all_to_all(x_sums, 'fy', split_axis=0, concat_axis=0, tiled=True)  10.3 us
    conv_general_dilated x2, matrix products, depthwise(): lax.conv_general_dilated(images, kernel[:, :, None, :], (1, 1), 'SAME', d...  7.19 us
    all_to_all x1, starting transfers between devices, body(): lax.all_to_all(x_sums, 'fy', split_axis=0, concat_axis=0, tiled=True)  5.47 us
    all_to_all x1, waiting for transfers between devices, body(): lax.all_to_all(x_tiled, 'fx', split_axis=1, concat_axis=1, tiled=True)  5.03 us
    all_to_all x1, starting transfers between devices, body(): lax.all_to_all(x_tiled, 'fx', split_axis=1, concat_axis=1, tiled=True)  4.42 us
  transfers between devices with their start and end apart: 7, of which 4 were waited for; matrix products, arithmetic and copies ran while one was open for 18% of the time, Pallas kernels for 0%

profile of v10, /device:TPU:64, one launch (start us, length us, event | category | flops | bytes accessed | tf_op | source)
XLA Modules:
  0.0 136.3 jit_solution(2156564164179876251)
XLA Ops:
  0.7 0.7 multiply_bitcast_fusion
  1.5 0.9 select_reduce_fusion
  2.4 1.0 convolution_convert_fusion.2
  3.4 18.4 %all-to-all-start = ((bf16[16,16,384]{2,1,0:T(8,128)(2,1)}), bf16[16,16,384]{2,1,0:T(8,128)(2,1)S(1)}, u32[]{:S(2)}, u32[]{:S(2)}) async-start(bf16[16,16,384]{2,1,0:T(8,128)(2,1)} %bitcast.3), calls=%async_computation | async-start | bytes 393216 | tf_op jit(solution)/shard_map/all_to_all | solution.py:61
  21.9 0.8 pad_maximum_fusion.1
  22.7 27.2 %all-gather = bf16[192,1536]{1,0:T(8,128)(2,1)S(1)} all-gather(bf16[24,1536]{1,0:T(8,128)(2,1)S(1)} %pad_maximum_fusion.1), channel_id=2, replica_groups=mesh['dp'=16,'fy'=8,'fx'=4,'llm'=2] {'fy'}, dimensions={0}, use_global_device_ids=true | all-gather | bytes 663552 | tf_op jit(solution)/shard_map/all_gather | solution.py:71
  49.9 1.6 %broadcast_in_dim.53 = bf16[8,4,24,1536]{3,2,0,1:T(8,128)(2,1)} broadcast(bf16[8,24,1536]{2,1,0:T(8,128)(2,1)S(1)} %bitcast.45), dimensions={0,2,3} | broadcast | bytes 2949120 | tf_op jit(solution)/shard_map/broadcast_in_dim | solution.py:72
  51.5 4.4 %all-to-all-start.1 = ((bf16[8,4,24,1536]{3,2,0,1:T(8,128)(2,1)}), bf16[8,4,24,1536]{3,2,0,1:T(8,128)(2,1)S(1)}, u32[]{:S(2)}, u32[]{:S(2)}) async-start(bf16[8,4,24,1536]{3,2,0,1:T(8,128)(2,1)} %broadcast_in_dim.53), calls=%async_computation.1 | async-start | bytes 4718592 | tf_op jit(solution)/shard_map/all_to_all | solution.py:73
  55.9 5.6 %fusion.29 = (f32[4,8,8]{0,2,1:T(8,128)S(1)}, f32[4,8,8,768]{3,0,2,1:T(4,128)}) fusion(f32[7,7,1,768]{3,1,0,2:T(8,128)S(1)} %bitcast.50, bf16[4,8,8,768]{3,2,1,0:T(8,128)(2,1)} %bitcast.58), kind=kOutput, calls=%fused_computation.67 | convolution fusion | flops 71565056 | bytes 1331200 | tf_op jit(solution)/shard_map/conv_general_dilated | solution.py:11
  61.8 2.2 %copy.65 = f32[4,8,8,768]{3,2,1,0:T(8,128)} copy(f32[4,8,8,768]{3,0,2,1:T(4,128)} %get-tuple-element.15) | data formatting | bytes 1572864 | tf_op jit(solution)/shard_map/conv_general_dilated | solution.py:11
  64.0 1.5 %multiply_reduce_fusion = f32[4,8,8]{0,2,1:T(8,128)S(1)} fusion(f32[4,8,8,768]{3,0,2,1:T(4,128)} %get-tuple-element.15, f32[4,8,8]{0,2,1:T(8,128)S(1)} %copy.62), kind=kLoop, calls=%fused_computation.23 | loop fusion | flops 589568 | bytes 788480 | tf_op jit(solution)/shard_map/reduce_sum | solution.py:84
  66.5 1.9 %collective-permute-start = (bf16[256,384]{1,0:T(8,128)(2,1)S(1)}, bf16[256,384]{1,0:T(8,128)(2,1)}, u32[]{:S(2)}, u32[]{:S(2)}) collective-permute-start(bf16[256,384]{1,0:T(8,128)(2,1)S(1)} %bitcast_select_fusion), channel_id=1, source_target_pairs={{0,1},{1,0},{2,3},{3,2},{4,5},{5,4},{6,7},{7,6},{8,9},{9,8},{10,11... | collective-permute-start | bytes 589832 | tf_op jit(solution)/shard_map/ppermute | solution.py:64
  68.4 2.3 %fusion.20 = (bf16[768,256]{0,1:T(8,128)(2,1)}, f32[256,768]{1,0:T(8,128)}) fusion(f32[768]{0:T(1024)S(1)} %copy-done.9, f32[256]{0:T(256)S(1)} %rsqrt.12, f32[256]{0:T(256)S(1)} %div.32, f32[4,8,8,768]{3,2,1,0:T(8,128)} %copy.65), kind=kLoop, calls=%fused_computation.44 | loop fusion | flops 786432 | bytes 1971200 | tf_op jit(solution)/shard_map/dot_general | solution.py:94
  70.8 1.9 %copy.69 = bf16[768,256]{1,0:T(8,128)(2,1)} copy(bf16[768,256]{0,1:T(8,128)(2,1)} %get-tuple-element.5) | data formatting | bytes 786432 | tf_op jit(solution)/shard_map/dot_general | solution.py:94
  72.7 1.7 %broadcast_select_fusion.1 = (bf16[256,384]{1,0:T(8,128)(2,1)S(1)}, bf16[256,384]{1,0:T(8,128)(2,1)}) fusion(bf16[256,384]{1,0:T(8,128)(2,1)} %collective-permute-done, pred[]{:T(512)S(6)} %eq.38, bf16[16,16,384]{2,1,0:T(8,128)(2,1)S(1)} %all-to-all-done, pred[256]{0:T(512)(128)(4,1)S(1)} %fusion.22), kind=kLoop, calls=%fused_computation.42 | loop fusion | flops 294912 | bytes 786689 | tf_op jit(solution)/shard_map/jit(_where)/select_n | solution.py:65
  74.4 5.0 %all-to-all-done.1 = bf16[8,4,24,1536]{3,2,0,1:T(8,128)(2,1)S(1)} async-done(((bf16[8,4,24,1536]{3,2,0,1:T(8,128)(2,1)}), bf16[8,4,24,1536]{3,2,0,1:T(8,128)(2,1)S(1)}, u32[]{:S(2)}, u32[]{:S(2)}) %all-to-all-start.1) | async-done | bytes 2359328 | tf_op jit(solution)/shard_map/all_to_all | solution.py:73
  79.7 0.9 copy-done.2
  83.5 1.6 %copy.70 = bf16[8,4,24,1536]{3,2,0,1:T(8,128)(2,1)} copy(bf16[8,4,24,1536]{3,2,1,0:T(8,128)(2,1)S(1)} %pad_maximum_fusion) | data formatting | bytes 4718592 | tf_op jit(solution)/shard_map/concatenate | solution.py:100
  85.1 3.6 %all-to-all-start.2 = ((bf16[8,4,24,1536]{3,2,0,1:T(8,128)(2,1)}), bf16[8,4,24,1536]{3,2,0,1:T(8,128)(2,1)S(1)}, u32[]{:S(2)}, u32[]{:S(2)}) async-start(bf16[8,4,24,1536]{3,2,0,1:T(8,128)(2,1)} %copy.70), calls=%async_computation.2 | async-start | bytes 4718592 | tf_op jit(solution)/shard_map/all_to_all | solution.py:102
  88.8 2.0 %fusion.2 = f32[256,768]{1,0:T(8,128)S(1)} fusion(bf16[256,768]{1,0:T(8,128)(2,1)} %copy-done.4, bf16[768,1536]{1,0:T(8,128)(2,1)} %bitcast.44), kind=kOutput, calls=%fused_computation.9 | convolution fusion | flops 301989888 | bytes 2359296 | tf_op jit(solution)/shard_map/dot_general | solution.py:109
  90.8 1.9 %collective-permute-start.1 = (bf16[256,384]{1,0:T(8,128)(2,1)S(1)}, bf16[256,384]{1,0:T(8,128)(2,1)S(1)}, u32[]{:S(2)}, u32[]{:S(2)}) collective-permute-start(bf16[256,384]{1,0:T(8,128)(2,1)S(1)} %select_convert_fusion), channel_id=1, source_target_pairs={{0,1},{1,0},{2,3},{3,2},{4,5},{5,4},{6,7},{7,6},{8,9},{9,8},{10,11... | collective-permute-start | bytes 589832 | tf_op jit(solution)/shard_map/ppermute | solution.py:116
  92.8 1.3 collective-permute-done.1
  94.1 0.8 fusion.27
  95.0 2.0 %collective-permute-start.2 = (f32[256,2]{0,1:T(2,128)S(1)}, f32[256,2]{0,1:T(2,128)S(1)}, u32[]{:S(2)}, u32[]{:S(2)}) collective-permute-start(f32[256,2]{0,1:T(2,128)S(1)} %pad_maximum_fusion.2), channel_id=1, source_target_pairs={{0,1},{1,0},{2,3},{3,2},{4,5},{5,4},{6,7},{7,6},{8,9},{9,8},{10,11... | collective-permute-start | bytes 6152 | tf_op jit(solution)/shard_map/ppermute | solution.py:124
  97.2 17.5 %all-to-all-done.2 = bf16[8,4,24,1536]{3,2,0,1:T(8,128)(2,1)S(1)} async-done(((bf16[8,4,24,1536]{3,2,0,1:T(8,128)(2,1)}), bf16[8,4,24,1536]{3,2,0,1:T(8,128)(2,1)S(1)}, u32[]{:S(2)}, u32[]{:S(2)}) %all-to-all-start.2) | async-done | bytes 2359328 | tf_op jit(solution)/shard_map/all_to_all | solution.py:102
  114.7 1.3 reduce_sum.71
  116.0 5.5 %all-to-all-start.3 = ((bf16[8,24,1536]{2,1,0:T(8,128)(2,1)}), bf16[8,24,1536]{2,1,0:T(8,128)(2,1)S(1)}, u32[]{:S(2)}, u32[]{:S(2)}) async-start(bf16[8,24,1536]{2,1,0:T(8,128)(2,1)} %reduce_sum.71), calls=%async_computation.3 | async-start | bytes 1179648 | tf_op jit(solution)/shard_map/all_to_all | solution.py:104
  121.5 1.3 subtract_multiply_fusion
  122.8 1.6 %fusion.13 = f32[4,8,8,384]{3,0,2,1:T(4,128)S(1)} fusion(f32[4,8,8,384]{3,2,1,0:T(8,128)S(1)} %bitcast.46, f32[7,7,1,384]{3,1,0,2:T(8,128)S(1)} %bitcast.49), kind=kOutput, calls=%fused_computation.28 | convolution fusion | flops 35684352 | bytes 861696 | tf_op jit(solution)/shard_map/conv_general_dilated | solution.py:11
  124.5 0.8 fusion.12
  125.3 10.3 %all-to-all-done.3 = bf16[8,24,1536]{2,1,0:T(8,128)(2,1)S(1)} async-done(((bf16[8,24,1536]{2,1,0:T(8,128)(2,1)}), bf16[8,24,1536]{2,1,0:T(8,128)(2,1)S(1)}, u32[]{:S(2)}, u32[]{:S(2)}) %all-to-all-start.3) | async-done | bytes 589856 | tf_op jit(solution)/shard_map/all_to_all | solution.py:104
  135.7 0.7 slice_multiply_fusion
  (50 shorter events, 4.3 us)
Async XLA Ops:
  0.6 1.8 %copy-start = (bf16[512,768]{1,0:T(8,128)(2,1)S(1)}, bf16[512,768]{1,0:T(8,128)(2,1)}, u32[]{:S(2)}) copy-start(bf16[512,768]{1,0:T(8,128)(2,1)} %param.11) | copy-start | bytes 2359300
  3.4 46.4 %all-to-all-start = ((bf16[16,16,384]{2,1,0:T(8,128)(2,1)}), bf16[16,16,384]{2,1,0:T(8,128)(2,1)S(1)}, u32[]{:S(2)}, u32[]{:S(2)}) async-start(bf16[16,16,384]{2,1,0:T(8,128)(2,1)} %bitcast.3), calls=%async_computation | async-start | bytes 393216 | tf_op jit(solution)/shard_map/all_to_all | solution.py:61
  51.5 4.4 %copy-start.7 = (f32[7,7,768]{2,1,0:T(8,128)S(1)}, f32[7,7,768]{2,1,0:T(8,128)}, u32[]{:S(2)}) copy-start(f32[7,7,768]{2,1,0:T(8,128)} %param.15) | copy-start | bytes 451588
  51.5 28.0 %all-to-all-start.1 = ((bf16[8,4,24,1536]{3,2,0,1:T(8,128)(2,1)}), bf16[8,4,24,1536]{3,2,0,1:T(8,128)(2,1)S(1)}, u32[]{:S(2)}, u32[]{:S(2)}) async-start(bf16[8,4,24,1536]{3,2,0,1:T(8,128)(2,1)} %broadcast_in_dim.53), calls=%async_computation.1 | async-start | bytes 4718592 | tf_op jit(solution)/shard_map/all_to_all | solution.py:73
  55.9 12.5 %copy-start.9 = (f32[768]{0:T(1024)S(1)}, f32[768]{0:T(1024)}, u32[]{:S(2)}) copy-start(f32[768]{0:T(1024)} %param.16) | copy-start | bytes 9220
  66.5 6.2 %collective-permute-start = (bf16[256,384]{1,0:T(8,128)(2,1)S(1)}, bf16[256,384]{1,0:T(8,128)(2,1)}, u32[]{:S(2)}, u32[]{:S(2)}) collective-permute-start(bf16[256,384]{1,0:T(8,128)(2,1)S(1)} %bitcast_select_fusion), channel_id=1, source_target_pairs={{0,1},{1,0},{2,3},{3,2},{4,5},{5,4},{6,7},{7,6},{8,9},{9,8},{10,11... | collective-permute-start | bytes 589832 | tf_op jit(solution)/shard_map/ppermute | solution.py:64
  79.4 1.1 copy-start.2
  79.7 2.0 %copy-start.1 = (bf16[8,4,24,1536]{3,2,1,0:T(8,128)(2,1)}, bf16[8,4,24,1536]{3,2,1,0:T(8,128)(2,1)S(1)}, u32[]{:S(2)}) copy-start(bf16[8,4,24,1536]{3,2,1,0:T(8,128)(2,1)S(1)} %copy.64) | copy-start | bytes 7077892
  79.7 1.4 %copy-start.6 = (bf16[256,384]{1,0:T(8,128)(2,1)S(1)}, bf16[256,384]{1,0:T(8,128)(2,1)}, u32[]{:S(2)}) copy-start(bf16[256,384]{1,0:T(8,128)(2,1)} %get-tuple-element.9) | copy-start | bytes 589828
  79.7 1.4 %copy-start.10 = (f32[768]{0:T(1024)S(1)}, f32[768]{0:T(1024)}, u32[]{:S(2)}) copy-start(f32[768]{0:T(1024)} %param.17) | copy-start | bytes 9220
  81.7 1.6 %copy-start.4 = (bf16[256,768]{1,0:T(8,128)(2,1)}, bf16[256,768]{1,0:T(8,128)(2,1)S(1)}, u32[]{:S(2)}) copy-start(bf16[256,768]{1,0:T(8,128)(2,1)S(1)} %fusion) | copy-start | bytes 1179652
  81.7 1.1 copy-start.5
  85.1 29.6 %all-to-all-start.2 = ((bf16[8,4,24,1536]{3,2,0,1:T(8,128)(2,1)}), bf16[8,4,24,1536]{3,2,0,1:T(8,128)(2,1)S(1)}, u32[]{:S(2)}, u32[]{:S(2)}) async-start(bf16[8,4,24,1536]{3,2,0,1:T(8,128)(2,1)} %copy.70), calls=%async_computation.2 | async-start | bytes 4718592 | tf_op jit(solution)/shard_map/all_to_all | solution.py:102
  88.7 5.4 %copy-start.3 = (f32[256,768]{1,0:T(8,128)S(1)}, f32[256,768]{1,0:T(8,128)}, u32[]{:S(2)}) copy-start(f32[256,768]{1,0:T(8,128)} %get-tuple-element.6) | copy-start | bytes 2359300
  88.8 8.3 %copy-start.8 = (f32[7,7,768]{2,1,0:T(8,128)S(1)}, f32[7,7,768]{2,1,0:T(8,128)}, u32[]{:S(2)}) copy-start(f32[7,7,768]{2,1,0:T(8,128)} %param.15) | copy-start | bytes 451588
  90.8 3.3 %collective-permute-start.1 = (bf16[256,384]{1,0:T(8,128)(2,1)S(1)}, bf16[256,384]{1,0:T(8,128)(2,1)S(1)}, u32[]{:S(2)}, u32[]{:S(2)}) collective-permute-start(bf16[256,384]{1,0:T(8,128)(2,1)S(1)} %select_convert_fusion), channel_id=1, source_target_pairs={{0,1},{1,0},{2,3},{3,2},{4,5},{5,4},{6,7},{7,6},{8,9},{9,8},{10,11... | collective-permute-start | bytes 589832 | tf_op jit(solution)/shard_map/ppermute | solution.py:116
  95.0 26.5 %collective-permute-start.2 = (f32[256,2]{0,1:T(2,128)S(1)}, f32[256,2]{0,1:T(2,128)S(1)}, u32[]{:S(2)}, u32[]{:S(2)}) collective-permute-start(f32[256,2]{0,1:T(2,128)S(1)} %pad_maximum_fusion.2), channel_id=1, source_target_pairs={{0,1},{1,0},{2,3},{3,2},{4,5},{5,4},{6,7},{7,6},{8,9},{9,8},{10,11... | collective-permute-start | bytes 6152 | tf_op jit(solution)/shard_map/ppermute | solution.py:124
  116.0 19.6 %all-to-all-start.3 = ((bf16[8,24,1536]{2,1,0:T(8,128)(2,1)}), bf16[8,24,1536]{2,1,0:T(8,128)(2,1)S(1)}, u32[]{:S(2)}, u32[]{:S(2)}) async-start(bf16[8,24,1536]{2,1,0:T(8,128)(2,1)} %reduce_sum.71), calls=%async_computation.3 | async-start | bytes 1179648 | tf_op jit(solution)/shard_map/all_to_all | solution.py:104

commit v11 on v10

--- a/solution.py
+++ b/solution.py
@@ -100,11 +100,10 @@
     terms = jnp.concatenate([term_in, term_out], axis=1).astype(jnp.bfloat16)
     terms = terms.reshape(height, width, channels // shards, 2 * hid)
     x_parts = lax.all_to_all(terms, "fx", split_axis=1, concat_axis=1, tiled=True)
-    x_sums = jnp.sum(x_parts.astype(jnp.float32), axis=1).astype(jnp.bfloat16)
+    x_sums = (jnp.sum(x_parts.astype(jnp.float32), axis=1) / ACCUM).astype(jnp.bfloat16)
     y_parts = lax.all_to_all(x_sums, "fy", split_axis=0, concat_axis=0, tiled=True)
-    totals = jnp.sum(y_parts.astype(jnp.float32), axis=0)
-    grad_in = totals[:, :hid] / ACCUM
-    grad_outw = totals[:, hid:] / ACCUM
+    grad_in = jnp.sum(y_parts[:, :, :hid].astype(jnp.float32), axis=0)
+    grad_outw = jnp.sum(y_parts[:, :, hid:].astype(jnp.float32), axis=0)
 
     grad_part = lax.dot_general(
         grad_pre, w_in_full, (((1,), (1,)), ((), ())), preferred_element_type=jnp.float32

time: 137 us -> 137 us (level)
  waiting for transfers between devices: 34.2 us -> 32.6 us
    all_to_all x1, waiting for transfers between devices: 17.5 us -> 14.6 us  [body(): lax.all_to_all(terms, 'fx', split_axis=1, concat_axis=1, tiled=True)]
  transfers between devices with their start and end apart: 7 -> 7, of which waited for: 4 -> 4; matrix products, arithmetic and copies ran while one was open for 18% -> 19% of each run, Pallas kernels for 0% -> 0%
where the time goes in v11:
time: 137 us; the launch traced here: 136 us
  starting transfers between devices  37.8 us (28%)
  waiting for transfers between devices  32.6 us (24%)
  blocking collectives  27.2 us (20%)
  other arithmetic  14.1 us (10%)
  matrix products  12.3 us (9%)
  local copies, waits for them, and re-layouts  10.8 us (8%)
  between operations  1.63 us (1%)
    all_gather x1, blocking collectives, body(): y_block = lax.all_gather(both, 'fy', axis=0)  27.2 us
    all_to_all x1, starting transfers between devices, body(): lax.all_to_all(out_half, 'dp', split_axis=0, concat_axis=0, tiled=True)  18.4 us
    all_to_all x1, waiting for transfers between devices, body(): lax.all_to_all(terms, 'fx', split_axis=1, concat_axis=1, tiled=True)  14.6 us
    all_to_all x1, waiting for transfers between devices, body(): lax.all_to_all(x_sums, 'fy', split_axis=0, concat_axis=0, tiled=True)  11.5 us
    conv_general_dilated x2, matrix products, depthwise(): lax.conv_general_dilated(images, kernel[:, :, None, :], (1, 1), 'SAME', d...  7.21 us
    all_to_all x1, starting transfers between devices, body(): lax.all_to_all(x_sums, 'fy', split_axis=0, concat_axis=0, tiled=True)  5.45 us
    all_to_all x1, waiting for transfers between devices, body(): lax.all_to_all(x_tiled, 'fx', split_axis=1, concat_axis=1, tiled=True)  4.99 us
    all_to_all x1, starting transfers between devices, body(): lax.all_to_all(x_tiled, 'fx', split_axis=1, concat_axis=1, tiled=True)  4.42 us
  transfers between devices with their start and end apart: 7, of which 4 were waited for; matrix products, arithmetic and copies ran while one was open for 19% of the time, Pallas kernels for 0%

profile of v11, /device:TPU:64, one launch (start us, length us, event | category | flops | bytes accessed | tf_op | source)
XLA Modules:
  0.0 136.4 jit_solution(10501709482926321710)
XLA Ops:
  0.7 0.7 multiply_bitcast_fusion
  1.5 0.9 select_reduce_fusion
  2.4 1.0 convolution_convert_fusion.2
  3.4 18.4 %all-to-all-start = ((bf16[16,16,384]{2,1,0:T(8,128)(2,1)}), bf16[16,16,384]{2,1,0:T(8,128)(2,1)S(1)}, u32[]{:S(2)}, u32[]{:S(2)}) async-start(bf16[16,16,384]{2,1,0:T(8,128)(2,1)} %bitcast.3), calls=%async_computation | async-start | bytes 393216 | tf_op jit(solution)/shard_map/all_to_all | solution.py:61
  21.9 0.8 pad_maximum_fusion.1
  22.7 27.2 %all-gather = bf16[192,1536]{1,0:T(8,128)(2,1)S(1)} all-gather(bf16[24,1536]{1,0:T(8,128)(2,1)S(1)} %pad_maximum_fusion.1), channel_id=2, replica_groups=mesh['dp'=16,'fy'=8,'fx'=4,'llm'=2] {'fy'}, dimensions={0}, use_global_device_ids=true | all-gather | bytes 663552 | tf_op jit(solution)/shard_map/all_gather | solution.py:71
  49.9 1.6 %broadcast_in_dim.53 = bf16[8,4,24,1536]{3,2,0,1:T(8,128)(2,1)} broadcast(bf16[8,24,1536]{2,1,0:T(8,128)(2,1)S(1)} %bitcast.45), dimensions={0,2,3} | broadcast | bytes 2949120 | tf_op jit(solution)/shard_map/broadcast_in_dim | solution.py:72
  51.5 4.4 %all-to-all-start.1 = ((bf16[8,4,24,1536]{3,2,0,1:T(8,128)(2,1)}), bf16[8,4,24,1536]{3,2,0,1:T(8,128)(2,1)S(1)}, u32[]{:S(2)}, u32[]{:S(2)}) async-start(bf16[8,4,24,1536]{3,2,0,1:T(8,128)(2,1)} %broadcast_in_dim.53), calls=%async_computation.1 | async-start | bytes 4718592 | tf_op jit(solution)/shard_map/all_to_all | solution.py:73
  55.9 5.6 %fusion.29 = (f32[4,8,8]{0,2,1:T(8,128)S(1)}, f32[4,8,8,768]{3,0,2,1:T(4,128)}) fusion(f32[7,7,1,768]{3,1,0,2:T(8,128)S(1)} %bitcast.50, bf16[4,8,8,768]{3,2,1,0:T(8,128)(2,1)} %bitcast.58), kind=kOutput, calls=%fused_computation.68 | convolution fusion | flops 71565056 | bytes 1331200 | tf_op jit(solution)/shard_map/conv_general_dilated | solution.py:11
  61.8 2.2 %copy.65 = f32[4,8,8,768]{3,2,1,0:T(8,128)} copy(f32[4,8,8,768]{3,0,2,1:T(4,128)} %get-tuple-element.15) | data formatting | bytes 1572864 | tf_op jit(solution)/shard_map/conv_general_dilated | solution.py:11
  64.0 1.5 %multiply_reduce_fusion = f32[4,8,8]{0,2,1:T(8,128)S(1)} fusion(f32[4,8,8,768]{3,0,2,1:T(4,128)} %get-tuple-element.15, f32[4,8,8]{0,2,1:T(8,128)S(1)} %copy.62), kind=kLoop, calls=%fused_computation.24 | loop fusion | flops 589568 | bytes 788480 | tf_op jit(solution)/shard_map/reduce_sum | solution.py:84
  66.5 1.9 %collective-permute-start = (bf16[256,384]{1,0:T(8,128)(2,1)S(1)}, bf16[256,384]{1,0:T(8,128)(2,1)}, u32[]{:S(2)}, u32[]{:S(2)}) collective-permute-start(bf16[256,384]{1,0:T(8,128)(2,1)S(1)} %bitcast_select_fusion), channel_id=1, source_target_pairs={{0,1},{1,0},{2,3},{3,2},{4,5},{5,4},{6,7},{7,6},{8,9},{9,8},{10,11... | collective-permute-start | bytes 589832 | tf_op jit(solution)/shard_map/ppermute | solution.py:64
  68.5 2.3 %fusion.20 = (bf16[768,256]{0,1:T(8,128)(2,1)}, f32[256,768]{1,0:T(8,128)}) fusion(f32[768]{0:T(1024)S(1)} %copy-done.11, f32[256]{0:T(256)S(1)} %rsqrt.12, f32[256]{0:T(256)S(1)} %div.32, f32[4,8,8,768]{3,2,1,0:T(8,128)} %copy.65), kind=kLoop, calls=%fused_computation.47 | loop fusion | flops 786432 | bytes 1971200 | tf_op jit(solution)/shard_map/dot_general | solution.py:94
  70.8 1.9 %copy.69 = bf16[768,256]{1,0:T(8,128)(2,1)} copy(bf16[768,256]{0,1:T(8,128)(2,1)} %get-tuple-element.7) | data formatting | bytes 786432 | tf_op jit(solution)/shard_map/dot_general | solution.py:94
  72.7 1.7 %broadcast_select_fusion.1 = (bf16[256,384]{1,0:T(8,128)(2,1)S(1)}, bf16[256,384]{1,0:T(8,128)(2,1)}) fusion(bf16[256,384]{1,0:T(8,128)(2,1)} %collective-permute-done, pred[]{:T(512)S(6)} %eq.38, bf16[16,16,384]{2,1,0:T(8,128)(2,1)S(1)} %all-to-all-done, pred[256]{0:T(512)(128)(4,1)S(1)} %fusion.22), kind=kLoop, calls=%fused_computation.45 | loop fusion | flops 294912 | bytes 786689 | tf_op jit(solution)/shard_map/jit(_where)/select_n | solution.py:65
  74.5 5.0 %all-to-all-done.1 = bf16[8,4,24,1536]{3,2,0,1:T(8,128)(2,1)S(1)} async-done(((bf16[8,4,24,1536]{3,2,0,1:T(8,128)(2,1)}), bf16[8,4,24,1536]{3,2,0,1:T(8,128)(2,1)S(1)}, u32[]{:S(2)}, u32[]{:S(2)}) %all-to-all-start.1) | async-done | bytes 2359328 | tf_op jit(solution)/shard_map/all_to_all | solution.py:73
  79.7 0.9 copy-done.2
  83.5 1.6 %copy.70 = bf16[8,4,24,1536]{3,2,0,1:T(8,128)(2,1)} copy(bf16[8,4,24,1536]{3,2,1,0:T(8,128)(2,1)S(1)} %pad_maximum_fusion) | data formatting | bytes 4718592 | tf_op jit(solution)/shard_map/concatenate | solution.py:100
  85.1 3.6 %all-to-all-start.2 = ((bf16[8,4,24,1536]{3,2,0,1:T(8,128)(2,1)}), bf16[8,4,24,1536]{3,2,0,1:T(8,128)(2,1)S(1)}, u32[]{:S(2)}, u32[]{:S(2)}) async-start(bf16[8,4,24,1536]{3,2,0,1:T(8,128)(2,1)} %copy.70), calls=%async_computation.2 | async-start | bytes 4718592 | tf_op jit(solution)/shard_map/all_to_all | solution.py:102
  88.8 1.9 %fusion.2 = f32[256,768]{1,0:T(8,128)S(1)} fusion(bf16[256,768]{1,0:T(8,128)(2,1)} %copy-done.6, bf16[768,1536]{1,0:T(8,128)(2,1)} %bitcast.44), kind=kOutput, calls=%fused_computation.10 | convolution fusion | flops 301989888 | bytes 2359296 | tf_op jit(solution)/shard_map/dot_general | solution.py:108
  90.7 0.9 copy-done.4
  92.3 1.9 %collective-permute-start.1 = (bf16[256,384]{1,0:T(8,128)(2,1)}, bf16[256,384]{1,0:T(8,128)(2,1)}, u32[]{:S(2)}, u32[]{:S(2)}) collective-permute-start(bf16[256,384]{1,0:T(8,128)(2,1)} %select_convert_fusion), channel_id=1, source_target_pairs={{0,1},{1,0},{2,3},{3,2},{4,5},{5,4},{6,7},{7,6},{8,9},{9,8},{10,11... | collective-permute-start | bytes 589832 | tf_op jit(solution)/shard_map/ppermute | solution.py:115
  94.5 1.5 %collective-permute-done.1 = bf16[256,384]{1,0:T(8,128)(2,1)} collective-permute-done((bf16[256,384]{1,0:T(8,128)(2,1)}, bf16[256,384]{1,0:T(8,128)(2,1)}, u32[]{:S(2)}, u32[]{:S(2)}) %collective-permute-start.1) | collective-permute-done | bytes 196640 | tf_op jit(solution)/shard_map/ppermute | solution.py:115
  96.0 2.1 %fusion.27 = (f32[256]{0:T(256)S(1)}, f32[256]{0:T(256)S(1)}, f32[256,384]{1,0:T(8,128)}) fusion(f32[256,768]{1,0:T(8,128)} %get-tuple-element.8, s32[]{:T(128)S(6)} %select_n.47, f32[384]{0:T(512)S(1)} %dynamic_slice.13, bf16[256,384]{1,0:T(8,128)(2,1)} %collective-permute-done.1, f32[256,768]{1,0:T(8,128)} %copy-done.4, pred[]{:T(512)S(6)} %eq.38), kind=kLoop, calls=%fused_computation.67 | loop fusion | flops 687616 | bytes 1773061 | tf_op jit(solution)/shard_map/reduce_sum | solution.py:121
  98.1 2.0 %collective-permute-start.2 = (f32[256,2]{0,1:T(2,128)S(1)}, f32[256,2]{0,1:T(2,128)S(1)}, u32[]{:S(2)}, u32[]{:S(2)}) collective-permute-start(f32[256,2]{0,1:T(2,128)S(1)} %pad_maximum_fusion.2), channel_id=1, source_target_pairs={{0,1},{1,0},{2,3},{3,2},{4,5},{5,4},{6,7},{7,6},{8,9},{9,8},{10,11... | collective-permute-start | bytes 6152 | tf_op jit(solution)/shard_map/ppermute | solution.py:123
  100.2 14.6 %all-to-all-done.2 = bf16[8,4,24,1536]{3,2,0,1:T(8,128)(2,1)S(1)} async-done(((bf16[8,4,24,1536]{3,2,0,1:T(8,128)(2,1)}), bf16[8,4,24,1536]{3,2,0,1:T(8,128)(2,1)S(1)}, u32[]{:S(2)}, u32[]{:S(2)}) %all-to-all-start.2) | async-done | bytes 2359328 | tf_op jit(solution)/shard_map/all_to_all | solution.py:102
  115.1 0.9 multiply_convert_fusion
  116.0 5.5 %all-to-all-start.3 = ((bf16[8,24,1536]{2,1,0:T(8,128)(2,1)}), bf16[8,24,1536]{2,1,0:T(8,128)(2,1)S(1)}, u32[]{:S(2)}, u32[]{:S(2)}) async-start(bf16[8,24,1536]{2,1,0:T(8,128)(2,1)} %multiply_convert_fusion), calls=%async_computation.3 | async-start | bytes 1179648 | tf_op jit(solution)/shard_map/all_to_all | solution.py:104
  121.7 1.6 %fusion.13 = f32[4,8,8,384]{3,0,2,1:T(4,128)S(1)} fusion(f32[4,8,8,384]{3,2,1,0:T(8,128)S(1)} %bitcast.46, f32[7,7,1,384]{3,1,0,2:T(8,128)S(1)} %bitcast.49), kind=kOutput, calls=%fused_computation.31 | convolution fusion | flops 35684352 | bytes 861696 | tf_op jit(solution)/shard_map/conv_general_dilated | solution.py:11
  123.4 0.8 fusion.12
  124.1 11.5 %all-to-all-done.3 = bf16[8,24,1536]{2,1,0:T(8,128)(2,1)S(1)} async-done(((bf16[8,24,1536]{2,1,0:T(8,128)(2,1)}), bf16[8,24,1536]{2,1,0:T(8,128)(2,1)S(1)}, u32[]{:S(2)}, u32[]{:S(2)}) %all-to-all-start.3) | async-done | bytes 589856 | tf_op jit(solution)/shard_map/all_to_all | solution.py:104
  135.6 0.7 convert_reduce_fusion.1
  (54 shorter events, 5.4 us)
Async XLA Ops:
  0.6 1.8 %copy-start = (bf16[512,768]{1,0:T(8,128)(2,1)S(1)}, bf16[512,768]{1,0:T(8,128)(2,1)}, u32[]{:S(2)}) copy-start(bf16[512,768]{1,0:T(8,128)(2,1)} %param.11) | copy-start | bytes 2359300
  3.4 46.4 %all-to-all-start = ((bf16[16,16,384]{2,1,0:T(8,128)(2,1)}), bf16[16,16,384]{2,1,0:T(8,128)(2,1)S(1)}, u32[]{:S(2)}, u32[]{:S(2)}) async-start(bf16[16,16,384]{2,1,0:T(8,128)(2,1)} %bitcast.3), calls=%async_computation | async-start | bytes 393216 | tf_op jit(solution)/shard_map/all_to_all | solution.py:61
  51.5 4.4 %copy-start.9 = (f32[7,7,768]{2,1,0:T(8,128)S(1)}, f32[7,7,768]{2,1,0:T(8,128)}, u32[]{:S(2)}) copy-start(f32[7,7,768]{2,1,0:T(8,128)} %param.15) | copy-start | bytes 451588
  51.5 28.0 %all-to-all-start.1 = ((bf16[8,4,24,1536]{3,2,0,1:T(8,128)(2,1)}), bf16[8,4,24,1536]{3,2,0,1:T(8,128)(2,1)S(1)}, u32[]{:S(2)}, u32[]{:S(2)}) async-start(bf16[8,4,24,1536]{3,2,0,1:T(8,128)(2,1)} %broadcast_in_dim.53), calls=%async_computation.1 | async-start | bytes 4718592 | tf_op jit(solution)/shard_map/all_to_all | solution.py:73
  55.9 12.5 %copy-start.11 = (f32[768]{0:T(1024)S(1)}, f32[768]{0:T(1024)}, u32[]{:S(2)}) copy-start(f32[768]{0:T(1024)} %param.16) | copy-start | bytes 9220
  66.5 6.2 %collective-permute-start = (bf16[256,384]{1,0:T(8,128)(2,1)S(1)}, bf16[256,384]{1,0:T(8,128)(2,1)}, u32[]{:S(2)}, u32[]{:S(2)}) collective-permute-start(bf16[256,384]{1,0:T(8,128)(2,1)S(1)} %bitcast_select_fusion), channel_id=1, source_target_pairs={{0,1},{1,0},{2,3},{3,2},{4,5},{5,4},{6,7},{7,6},{8,9},{9,8},{10,11... | collective-permute-start | bytes 589832 | tf_op jit(solution)/shard_map/ppermute | solution.py:64
  79.5 1.1 copy-start.2
  79.7 2.0 %copy-start.1 = (bf16[8,4,24,1536]{3,2,1,0:T(8,128)(2,1)}, bf16[8,4,24,1536]{3,2,1,0:T(8,128)(2,1)S(1)}, u32[]{:S(2)}) copy-start(bf16[8,4,24,1536]{3,2,1,0:T(8,128)(2,1)S(1)} %copy.64) | copy-start | bytes 7077892
  79.7 1.4 %copy-start.8 = (bf16[256,384]{1,0:T(8,128)(2,1)S(1)}, bf16[256,384]{1,0:T(8,128)(2,1)}, u32[]{:S(2)}) copy-start(bf16[256,384]{1,0:T(8,128)(2,1)} %get-tuple-element.11) | copy-start | bytes 589828
  79.7 1.4 %copy-start.12 = (f32[768]{0:T(1024)S(1)}, f32[768]{0:T(1024)}, u32[]{:S(2)}) copy-start(f32[768]{0:T(1024)} %param.17) | copy-start | bytes 9220
  81.7 1.6 %copy-start.6 = (bf16[256,768]{1,0:T(8,128)(2,1)}, bf16[256,768]{1,0:T(8,128)(2,1)S(1)}, u32[]{:S(2)}) copy-start(bf16[256,768]{1,0:T(8,128)(2,1)S(1)} %fusion) | copy-start | bytes 1179652
  81.7 1.1 copy-start.7
  85.1 29.6 %all-to-all-start.2 = ((bf16[8,4,24,1536]{3,2,0,1:T(8,128)(2,1)}), bf16[8,4,24,1536]{3,2,0,1:T(8,128)(2,1)S(1)}, u32[]{:S(2)}, u32[]{:S(2)}) async-start(bf16[8,4,24,1536]{3,2,0,1:T(8,128)(2,1)} %copy.70), calls=%async_computation.2 | async-start | bytes 4718592 | tf_op jit(solution)/shard_map/all_to_all | solution.py:102
  88.8 5.6 %copy-start.10 = (f32[7,7,768]{2,1,0:T(8,128)S(1)}, f32[7,7,768]{2,1,0:T(8,128)}, u32[]{:S(2)}) copy-start(f32[7,7,768]{2,1,0:T(8,128)} %param.15) | copy-start | bytes 451588
  90.7 0.9 copy-start.4
  92.3 3.7 %collective-permute-start.1 = (bf16[256,384]{1,0:T(8,128)(2,1)}, bf16[256,384]{1,0:T(8,128)(2,1)}, u32[]{:S(2)}, u32[]{:S(2)}) collective-permute-start(bf16[256,384]{1,0:T(8,128)(2,1)} %select_convert_fusion), channel_id=1, source_target_pairs={{0,1},{1,0},{2,3},{3,2},{4,5},{5,4},{6,7},{7,6},{8,9},{9,8},{10,11... | collective-permute-start | bytes 589832 | tf_op jit(solution)/shard_map/ppermute | solution.py:115
  98.1 23.3 %collective-permute-start.2 = (f32[256,2]{0,1:T(2,128)S(1)}, f32[256,2]{0,1:T(2,128)S(1)}, u32[]{:S(2)}, u32[]{:S(2)}) collective-permute-start(f32[256,2]{0,1:T(2,128)S(1)} %pad_maximum_fusion.2), channel_id=1, source_target_pairs={{0,1},{1,0},{2,3},{3,2},{4,5},{5,4},{6,7},{7,6},{8,9},{9,8},{10,11... | collective-permute-start | bytes 6152 | tf_op jit(solution)/shard_map/ppermute | solution.py:123
  115.1 6.4 %copy-start.3 = (f32[256,768]{1,0:T(8,128)S(1)}, f32[256,768]{1,0:T(8,128)}, u32[]{:S(2)}) copy-start(f32[256,768]{1,0:T(8,128)} %get-tuple-element.8) | copy-start | bytes 2359300
  115.1 6.4 %copy-start.5 = (f32[256,384]{1,0:T(8,128)S(1)}, f32[256,384]{1,0:T(8,128)}, u32[]{:S(2)}) copy-start(f32[256,384]{1,0:T(8,128)} %get-tuple-element.9) | copy-start | bytes 1179652
  116.0 19.6 %all-to-all-start.3 = ((bf16[8,24,1536]{2,1,0:T(8,128)(2,1)}), bf16[8,24,1536]{2,1,0:T(8,128)(2,1)S(1)}, u32[]{:S(2)}, u32[]{:S(2)}) async-start(bf16[8,24,1536]{2,1,0:T(8,128)(2,1)} %multiply_convert_fusion), calls=%async_computation.3 | async-start | bytes 1179648 | tf_op jit(solution)/shard_map/all_to_all | solution.py:104
